TPU v7x, 32 devices: a whole 2x2x4 slice. The times are simulated.
32 devices in a mesh: row: 8 (over y, x, core), col: 4 (over z).
Axes of the slice: x: 2, y: 2, z: 4, core: 2. Of those that a mesh axis runs over, the one named last changes fastest.
Arguments:
- adjacency: float32 [1024, 32768], P('row', 'col'), may hold values from 0 to 0.99, as said below
Outputs:
- tom: float32 [1024, 1024], P('row', 'col')
Inputs may be any that keep to these rules, and one draw needn't show every extreme that they name: `adjacency`: every entry is nonnegative and below 0.99.
All inputs are finite; a program needn't handle non-finite values.
Results may differ from a plain program's by a relative error of at most 0.000059.
Values sent between devices are 32-bit elements; how exact they have to be, the bound alone decides.
No kernel may reach another device: no remote copies, remote signals or barrier semaphores. Data moves between devices by JAX's collectives and lax.ppermute only.
A program may use at most 64 MiB of HBM per device.

v0:
```python
import jax
import jax.numpy as jnp
from jax import lax
from jax.sharding import PartitionSpec as P


def inner_rows(left, right):
    return lax.dot_general(
        left,
        right,
        (((1,), (1,)), ((), ())),
        precision=lax.Precision.HIGHEST,
        preferred_element_type=jnp.float32,
    )


def body(adjacency):
    strip_rows = adjacency.shape[0]
    window = strip_rows * lax.axis_size("row") // lax.axis_size("col")
    pieces = lax.all_to_all(adjacency, "row", split_axis=1, concat_axis=0, tiled=True)
    block_sums = lax.psum_scatter(
        inner_rows(pieces, pieces), "col", scatter_dimension=0, tiled=True
    )
    shared_sum = lax.psum_scatter(block_sums, "row", scatter_dimension=1, tiled=True).T
    own_degree = lax.psum(jnp.sum(adjacency, axis=1), "col")
    all_degree = lax.all_gather(own_degree, "row", axis=0, tiled=True)
    col_degree = lax.dynamic_slice_in_dim(all_degree, lax.axis_index("col") * window, window, 0)
    linked = adjacency[:, :window]
    smaller = jnp.minimum(own_degree[:, None], col_degree[None, :])
    return (shared_sum + linked) / (smaller + 1.0 - linked)


def solution(mesh):
    placed = (P("row", "col"),)
    return jax.shard_map(
        body, mesh=mesh, in_specs=placed, out_specs=P("row", "col"), check_vma=False
    )
```

profile of v0, /device:TPU:0, one launch (start us, length us, event | category | flops | bytes accessed | tf_op | source)
XLA Modules:
  0.0 215.7 jit_solution(15998971876274687652)
XLA Ops:
  6.5 0.0 reduce-scatter.3.cloned.1.call-start
  6.5 5.6 %copy.10 = f32[128,8192]{0,1:T(8,128)} copy(f32[128,8192]{1,0:T(8,128)} %param.1) | data formatting | bytes 8388608 | tf_op args[0]
  12.1 54.3 %all_to_all.19 = f32[128,8,1024]{0,2,1:T(8,128)} all-to-all(f32[128,8,1024]{0,2,1:T(8,128)} %bitcast.11), channel_id=1, replica_groups=mesh['row'=8,'col'=4] {'row'}, dimensions={1} | all-to-all | bytes 8388608 | tf_op jit(solution)/shard_map/all_to_all | solution.py:20
  66.4 5.3 %copy.11 = f32[8,128,1024]{2,1,0:T(8,128)} copy(f32[8,128,1024]{1,2,0:T(8,128)} %bitcast.12) | data formatting | bytes 8388608 | tf_op jit(solution)/shard_map/all_to_all | solution.py:20
  71.8 18.1 %fusion.1 = f32[1024,1024]{1,0:T(8,128)} fusion(f32[1024,1024]{1,0:T(8,128)} %bitcast.13), kind=kOutput, calls=%fused_computation.2 | convolution fusion | flops 12884901888 | bytes 8388608 | tf_op jit(solution)/shard_map/dot_general | solution.py:8
  89.9 0.0 reduce-scatter.3.cloned.1.call-update
  89.9 0.0 reduce-scatter.5.cloned.1.call-start
  90.0 76.9 %reduce-scatter.3.cloned.1.call-done = f32[256,1024]{1,0:T(8,128)} async-done(((f32[1024,1024]{1,0:T(8,128)}), f32[256,1024]{1,0:T(8,128)}) %reduce-scatter.3.cloned.1.call-update) | async-done | bytes 1048592 | tf_op jit(solution)/shard_map/reduce_scatter | solution.py:21
  166.9 0.0 reduce-scatter.5.cloned.1.call-update
  166.9 2.5 %reduce_sum.9 = f32[128]{0:T(128)S(1)} reduce(f32[128,8192]{1,0:T(8,128)} %param.1, f32[]{:T(128)} %constant.6.clone.1), dimensions={1}, to_apply=%region_2.0 | reduce | flops 1048448 | bytes 4194820 | tf_op jit(solution)/shard_map/reduce_sum | solution.py:25
  169.4 11.0 %psum.7 = f32[128]{0:T(128)S(1)} all-reduce(f32[128]{0:T(128)S(1)} %reduce_sum.9), channel_id=1, replica_groups=mesh['row'=8,'col'=4] {'col'}, use_global_device_ids=true, to_apply=%region_3.0 | all-reduce | flops 128 | bytes 1024 | tf_op jit(solution)/shard_map/psum | solution.py:25
  180.4 8.9 %all-gather = f32[8,1,128]{2,1,0:T(1,128)S(1)} all-gather(f32[1,1,128]{2,1,0:T(1,128)S(1)} %bitcast.15), channel_id=1, replica_groups=mesh['row'=8,'col'=4] {'row'}, dimensions={0}, use_global_device_ids=true | all-gather | bytes 4608 | tf_op jit(solution)/shard_map/all_gather | solution.py:26
  189.3 0.1 dynamic_slice.3
  189.4 17.6 %reduce-scatter.5.cloned.1.call-done = f32[256,128]{1,0:T(8,128)} async-done(((f32[256,1024]{1,0:T(8,128)}), f32[256,128]{1,0:T(8,128)}) %reduce-scatter.5.cloned.1.call-update) | async-done | bytes 131088 | tf_op jit(solution)/shard_map/reduce_scatter | solution.py:24
  207.0 1.1 fusion
  208.1 0.8 copy.13
Async XLA Ops:
  6.5 160.4 %reduce-scatter.3.cloned.1.call-start = ((), (), s32[]{:S(2)}) async-start(), calls=%async_computation.3 | async-start | bytes 5242880 | tf_op jit(solution)/shard_map/reduce_scatter | solution.py:21
  89.9 117.1 %reduce-scatter.5.cloned.1.call-start = ((), (), s32[]{:S(2)}) async-start(), calls=%async_computation.4 | async-start | bytes 1179648 | tf_op jit(solution)/shard_map/reduce_scatter | solution.py:24
Sparse Core Ops, SparseCore 0:
  90.1 76.8 reduce-scatter.2
  170.4 36.5 reduce-scatter.4
where the time goes:
time: 216 us
  waiting for transfers between devices  94.6 us (44%)
  blocking collectives  74.2 us (34%)
  matrix products  18.1 us (8%)
  between operations  13.4 us (6%)
  local copies, waits for them, and re-layouts  11.7 us (5%)
  other arithmetic  3.57 us (2%)
    reduce_scatter x1, waiting for transfers between devices, body(): lax.psum_scatter(inner_rows(pieces, pieces), 'col', scatter_dimension=0,...  76.9 us
    all_to_all x1, blocking collectives, body(): lax.all_to_all(adjacency, 'row', split_axis=1, concat_axis=0, tiled=True)  54.3 us
    dot_general x1, matrix products, inner_rows(): lax.dot_general(left, right, (((1,), (1,)), ((), ())), precision=lax.Prec...  18.1 us
    reduce_scatter x1, waiting for transfers between devices, body(): lax.psum_scatter(block_sums, 'row', scatter_dimension=1, tiled=True)  17.6 us
    psum x1, blocking collectives, body(): own_degree = lax.psum(jnp.sum(adjacency, axis=1), 'col')  11 us
    all_gather x1, blocking collectives, body(): all_degree = lax.all_gather(own_degree, 'row', axis=0, tiled=True)  8.92 us
    unnamed x1, local copies, waits for them, and re-layouts  5.57 us
    all_to_all x1, local copies, waits for them, and re-layouts, body(): lax.all_to_all(adjacency, 'row', split_axis=1, concat_axis=0, tiled=True)  5.34 us
  transfers between devices with their start and end apart: 2, of which 2 were waited for; matrix products, arithmetic and copies ran while one was open for 1% of the time, Pallas kernels for 0%

commit v1 on v0

v1 whole, which is shorter than its diff:
```python
import jax
import jax.numpy as jnp
from jax import lax
from jax.sharding import PartitionSpec as P


def inner_rows(left, right):
    return lax.dot_general(
        left,
        right,
        (((1,), (1,)), ((), ())),
        precision=lax.Precision.HIGHEST,
        preferred_element_type=jnp.float32,
    )


def finish(shared_sum, linked, own_degree, col_degree):
    smaller = jnp.minimum(own_degree[:, None], col_degree[None, :])
    return (shared_sum + linked) / (smaller + 1.0 - linked)


def degrees(adjacency, window):
    n_row = lax.axis_size("row")
    n_col = lax.axis_size("col")
    strip_rows = adjacency.shape[0]
    row_sum = jnp.sum(adjacency, axis=1)
    every = lax.all_gather(row_sum, ("row", "col"), axis=0, tiled=True)
    every = every.reshape(n_row, n_col, strip_rows).sum(axis=1).reshape(-1)
    own = lax.dynamic_slice_in_dim(every, lax.axis_index("row") * strip_rows, strip_rows, 0)
    col = lax.dynamic_slice_in_dim(every, lax.axis_index("col") * window, window, 0)
    return own, col


def solution(mesh):
    placed = (P("row", "col"),)
    return jax.shard_map(
        body, mesh=mesh, in_specs=placed, out_specs=P("row", "col"), check_vma=False
    )


def body(adjacency):
    strip_rows = adjacency.shape[0]
    window = strip_rows * lax.axis_size("row") // lax.axis_size("col")
    pieces = lax.all_to_all(adjacency, "row", split_axis=1, concat_axis=0, tiled=True)
    part = lax.psum_scatter(inner_rows(pieces, pieces), "row", scatter_dimension=0, tiled=True)
    shared_sum = lax.psum_scatter(part, "col", scatter_dimension=1, tiled=True)
    own_degree = lax.psum(jnp.sum(adjacency, axis=1), "col")
    all_degree = lax.all_gather(own_degree, "row", axis=0, tiled=True)
    col_degree = lax.dynamic_slice_in_dim(all_degree, lax.axis_index("col") * window, window, 0)
    linked = adjacency[:, :window]
    return finish(shared_sum, linked, own_degree, col_degree)
```

time: 216 us -> 174 us (0.81)
  waiting for transfers between devices: 94.6 us -> 52.4 us
    reduce_scatter x2, waiting for transfers between devices: 94.5 us -> 52.4 us  [the longest x1 51.4 us: body(): lax.psum_scatter(inner_rows(pieces, pieces), 'row', scatter_dimension=0,...]
where the time goes in v1:
time: 174 us
  blocking collectives  74.7 us (43%)
  waiting for transfers between devices  52.4 us (30%)
  matrix products  18.1 us (10%)
  between operations  13.4 us (8%)
  local copies, waits for them, and re-layouts  11 us (6%)
  other arithmetic  4.22 us (2%)
    all_to_all x1, blocking collectives, body(): lax.all_to_all(adjacency, 'row', split_axis=1, concat_axis=0, tiled=True)  54.3 us
    reduce_scatter x1, waiting for transfers between devices, body(): lax.psum_scatter(inner_rows(pieces, pieces), 'row', scatter_dimension=0,...  51.4 us
    dot_general x1, matrix products, inner_rows(): lax.dot_general(left, right, (((1,), (1,)), ((), ())), precision=lax.Prec...  18.1 us
    psum x1, blocking collectives, body(): own_degree = lax.psum(jnp.sum(adjacency, axis=1), 'col')  11.8 us
    all_gather x1, blocking collectives, body(): all_degree = lax.all_gather(own_degree, 'row', axis=0, tiled=True)  8.59 us
    unnamed x1, local copies, waits for them, and re-layouts  5.57 us
    all_to_all x1, local copies, waits for them, and re-layouts, body(): lax.all_to_all(adjacency, 'row', split_axis=1, concat_axis=0, tiled=True)  5.34 us
  transfers between devices with their start and end apart: 2, of which 2 were waited for; matrix products, arithmetic and copies ran while one was open for 1% of the time, Pallas kernels for 0%

profile of v1, /device:TPU:0, one launch (start us, length us, event | category | flops | bytes accessed | tf_op | source)
XLA Modules:
  0.0 173.9 jit_solution(5790078608132117459)
XLA Ops:
  6.5 0.0 reduce-scatter.3.cloned.1.call-start
  6.5 5.6 %copy.4 = f32[128,8192]{0,1:T(8,128)} copy(f32[128,8192]{1,0:T(8,128)} %param.1) | data formatting | bytes 8388608 | tf_op args[0]
  12.1 54.3 %all_to_all.19 = f32[128,8,1024]{0,2,1:T(8,128)} all-to-all(f32[128,8,1024]{0,2,1:T(8,128)} %bitcast.8), channel_id=1, replica_groups=mesh['row'=8,'col'=4] {'row'}, dimensions={1} | all-to-all | bytes 8388608 | tf_op jit(solution)/shard_map/all_to_all | solution.py:44
  66.4 5.3 %copy.5 = f32[8,128,1024]{2,1,0:T(8,128)} copy(f32[8,128,1024]{1,2,0:T(8,128)} %bitcast.7) | data formatting | bytes 8388608 | tf_op jit(solution)/shard_map/all_to_all | solution.py:44
  71.8 18.1 %fusion = f32[1024,1024]{1,0:T(8,128)} fusion(f32[1024,1024]{1,0:T(8,128)} %bitcast.9), kind=kOutput, calls=%fused_computation.1 | convolution fusion | flops 12884901888 | bytes 8388608 | tf_op jit(solution)/shard_map/dot_general | solution.py:8
  89.9 0.0 reduce-scatter.3.cloned.1.call-update
  90.0 0.0 reduce-scatter.5.cloned.1.call-start
  90.0 51.4 %reduce-scatter.3.cloned.1.call-done = f32[128,1024]{1,0:T(8,128)} async-done(((f32[1024,1024]{1,0:T(8,128)}), f32[128,1024]{1,0:T(8,128)}) %reduce-scatter.3.cloned.1.call-update) | async-done | bytes 524304 | tf_op jit(solution)/shard_map/reduce_scatter | solution.py:45
  141.4 0.0 reduce-scatter.5.cloned.1.call-update
  141.5 2.5 %reduce_sum.9 = f32[128]{0:T(128)S(1)} reduce(f32[128,8192]{1,0:T(8,128)} %param.1, f32[]{:T(128)} %constant.6.clone.1), dimensions={1}, to_apply=%region_2.0 | reduce | flops 1048448 | bytes 4194820 | tf_op jit(solution)/shard_map/reduce_sum | solution.py:47
  144.0 11.8 %psum.7 = f32[128]{0:T(128)S(1)} all-reduce(f32[128]{0:T(128)S(1)} %reduce_sum.9), channel_id=1, replica_groups=mesh['row'=8,'col'=4] {'col'}, use_global_device_ids=true, to_apply=%region_3.0 | all-reduce | flops 128 | bytes 1024 | tf_op jit(solution)/shard_map/psum | solution.py:47
  155.7 8.6 %all-gather = f32[8,1,128]{2,1,0:T(1,128)S(1)} all-gather(f32[1,1,128]{2,1,0:T(1,128)S(1)} %bitcast.11), channel_id=1, replica_groups=mesh['row'=8,'col'=4] {'row'}, dimensions={0}, use_global_device_ids=true | all-gather | bytes 4608 | tf_op jit(solution)/shard_map/all_gather | solution.py:48
  164.3 0.1 dynamic_slice.3
  164.4 1.0 reduce-scatter.5.cloned.1.call-done
  165.3 1.7 subtract_divide_fusion
Async XLA Ops:
  6.5 134.9 %reduce-scatter.3.cloned.1.call-start = ((), (), s32[]{:S(2)}) async-start(), calls=%async_computation.3 | async-start | bytes 4718592 | tf_op jit(solution)/shard_map/reduce_scatter | solution.py:45
  90.0 75.4 %reduce-scatter.5.cloned.1.call-start = ((), (), s32[]{:S(2)}) async-start(), calls=%async_computation.4 | async-start | bytes 655360 | tf_op jit(solution)/shard_map/reduce_scatter | solution.py:46
Sparse Core Ops, SparseCore 0:
  90.1 51.3 reduce-scatter.2
  143.8 21.4 reduce-scatter.4

commit v2 on v1

--- a/solution.py
+++ b/solution.py
@@ -9,7 +9,7 @@
         left,
         right,
         (((1,), (1,)), ((), ())),
-        precision=lax.Precision.HIGHEST,
+        precision=lax.Precision.HIGH,
         preferred_element_type=jnp.float32,
     )
 
@@ -38,14 +38,29 @@
     )
 
 
+def col_reduce_scatter(part):
+    n_col = lax.axis_size("col")
+    me = lax.axis_index("col")
+    rows, cols = part.shape
+    width = cols // n_col
+    blocks = part.reshape(rows, n_col, width)
+    total = lax.dynamic_index_in_dim(blocks, me, 1, keepdims=False)
+    for s in range(1, n_col):
+        send = lax.dynamic_index_in_dim(blocks, (me + s) % n_col, 1, keepdims=False)
+        perm = [(i, (i + s) % n_col) for i in range(n_col)]
+        total = total + lax.ppermute(send, "col", perm)
+    return total
+
+
 def body(adjacency):
     strip_rows = adjacency.shape[0]
     window = strip_rows * lax.axis_size("row") // lax.axis_size("col")
     pieces = lax.all_to_all(adjacency, "row", split_axis=1, concat_axis=0, tiled=True)
     part = lax.psum_scatter(inner_rows(pieces, pieces), "row", scatter_dimension=0, tiled=True)
-    shared_sum = lax.psum_scatter(part, "col", scatter_dimension=1, tiled=True)
     own_degree = lax.psum(jnp.sum(adjacency, axis=1), "col")
     all_degree = lax.all_gather(own_degree, "row", axis=0, tiled=True)
     col_degree = lax.dynamic_slice_in_dim(all_degree, lax.axis_index("col") * window, window, 0)
+    part, own_degree, col_degree = lax.optimization_barrier((part, own_degree, col_degree))
+    shared_sum = col_reduce_scatter(part)
     linked = adjacency[:, :window]
     return finish(shared_sum, linked, own_degree, col_degree)

time: 174 us -> 160 us (0.920)
  waiting for transfers between devices: 52.4 us -> 38.5 us
  matrix products: 18.1 us -> 11.7 us
  starting transfers between devices: 0.04 us -> 4.6 us
  local copies, waits for them, and re-layouts: 11 us -> 12.8 us
    reduce_scatter x1, waiting for transfers between devices: 51.4 us -> 28.5 us  [body(): lax.psum_scatter(inner_rows(pieces, pieces), 'row', scatter_dimension=0,...]
    ppermute x0 -> x3, waiting for transfers between devices: none -> 10 us  [col_reduce_scatter(): total = total + lax.ppermute(send, 'col', perm)]
    dot_general x1, matrix products: 18.1 us -> 11.7 us  [inner_rows(): lax.dot_general(left, right, (((1,), (1,)), ((), ())), precision=lax.Prec...]
    ppermute x0 -> x3, starting transfers between devices: none -> 4.59 us  [col_reduce_scatter(): total = total + lax.ppermute(send, 'col', perm)]
    unnamed x1 -> x4, local copies, waits for them, and re-layouts: 5.57 us -> 5.6 us
  transfers between devices with their start and end apart: 2 -> 4, of which waited for: 2 -> 3; matrix products, arithmetic and copies ran while one was open for 1% -> 2% of each run, Pallas kernels for 0% -> 0%
where the time goes in v2:
time: 160 us
  blocking collectives  74.7 us (47%)
  waiting for transfers between devices  38.5 us (24%)
  between operations  13.5 us (8%)
  local copies, waits for them, and re-layouts  12.8 us (8%)
  matrix products  11.7 us (7%)
  starting transfers between devices  4.6 us (3%)
  other arithmetic  4.17 us (3%)
    all_to_all x1, blocking collectives, body(): lax.all_to_all(adjacency, 'row', split_axis=1, concat_axis=0, tiled=True)  54.3 us
    reduce_scatter x1, waiting for transfers between devices, body(): lax.psum_scatter(inner_rows(pieces, pieces), 'row', scatter_dimension=0,...  28.5 us
    psum x1, blocking collectives, body(): own_degree = lax.psum(jnp.sum(adjacency, axis=1), 'col')  12.6 us
    dot_general x1, matrix products, inner_rows(): lax.dot_general(left, right, (((1,), (1,)), ((), ())), precision=lax.Prec...  11.7 us
    ppermute x3, waiting for transfers between devices, col_reduce_scatter(): total = total + lax.ppermute(send, 'col', perm)  10 us
    all_gather x1, blocking collectives, body(): all_degree = lax.all_gather(own_degree, 'row', axis=0, tiled=True)  7.79 us
    unnamed x4, local copies, waits for them, and re-layouts  5.6 us
    all_to_all x1, local copies, waits for them, and re-layouts, body(): lax.all_to_all(adjacency, 'row', split_axis=1, concat_axis=0, tiled=True)  5.34 us
  transfers between devices with their start and end apart: 4, of which 3 were waited for; matrix products, arithmetic and copies ran while one was open for 2% of the time, Pallas kernels for 0%

profile of v2, /device:TPU:0, one launch (start us, length us, event | category | flops | bytes accessed | tf_op | source)
XLA Modules:
  0.0 159.9 jit_solution(11532271974828495544)
XLA Ops:
  6.5 0.0 reduce-scatter.2.cloned.1.call-start
  6.5 5.6 %copy.4 = f32[128,8192]{0,1:T(8,128)} copy(f32[128,8192]{1,0:T(8,128)} %param.1) | data formatting | bytes 8388608 | tf_op args[0]
  12.1 54.3 %all_to_all.19 = f32[128,8,1024]{0,2,1:T(8,128)} all-to-all(f32[128,8,1024]{0,2,1:T(8,128)} %bitcast.27), channel_id=1, replica_groups=mesh['row'=8,'col'=4] {'row'}, dimensions={1} | all-to-all | bytes 8388608 | tf_op jit(solution)/shard_map/all_to_all | solution.py:58
  66.4 5.3 %copy.5 = f32[8,128,1024]{2,1,0:T(8,128)} copy(f32[8,128,1024]{1,2,0:T(8,128)} %bitcast.26) | data formatting | bytes 8388608 | tf_op jit(solution)/shard_map/all_to_all | solution.py:58
  71.8 11.7 %fusion.4 = f32[1024,1024]{1,0:T(8,128)} fusion(f32[1024,1024]{1,0:T(8,128)} %bitcast.28), kind=kOutput, calls=%fused_computation.12 | convolution fusion | flops 6442450944 | bytes 8388608 | tf_op jit(solution)/shard_map/dot_general | solution.py:8
  83.5 0.0 reduce-scatter.2.cloned.1.call-update
  83.5 2.5 %reduce_sum.9 = f32[128]{0:T(128)S(1)} reduce(f32[128,8192]{1,0:T(8,128)} %param.1, f32[]{:T(128)} %constant.39.clone.1), dimensions={1}, to_apply=%region_1.0 | reduce | flops 1048448 | bytes 4194820 | tf_op jit(solution)/shard_map/reduce_sum | solution.py:60
  86.0 12.6 %psum.7 = f32[128]{0:T(128)S(1)} all-reduce(f32[128]{0:T(128)S(1)} %reduce_sum.9), channel_id=1, replica_groups=mesh['row'=8,'col'=4] {'col'}, use_global_device_ids=true, to_apply=%region_2.0 | all-reduce | flops 128 | bytes 1024 | tf_op jit(solution)/shard_map/psum | solution.py:60
  98.6 7.8 %all-gather = f32[8,1,128]{2,1,0:T(1,128)S(1)} all-gather(f32[1,1,128]{2,1,0:T(1,128)S(1)} %bitcast.33), channel_id=1, replica_groups=mesh['row'=8,'col'=4] {'row'}, dimensions={0}, use_global_device_ids=true | all-gather | bytes 4608 | tf_op jit(solution)/shard_map/all_gather | solution.py:61
  106.4 0.1 dynamic_slice.16
  106.5 28.5 %reduce-scatter.2.cloned.1.call-done = f32[128,1024]{1,0:T(8,128)} async-done(((f32[1024,1024]{1,0:T(8,128)}), f32[128,1024]{1,0:T(8,128)}) %reduce-scatter.2.cloned.1.call-update) | async-done | bytes 524304 | tf_op jit(solution)/shard_map/reduce_scatter | solution.py:59
  135.0 1.3 reshape.8
  136.3 0.5 constant_dynamic-slice_fusion.3
  136.7 3.4 %collective-permute-start.2 = (f32[128,256]{1,0:T(8,128)S(1)}, f32[128,256]{1,0:T(8,128)S(1)}, u32[]{:S(2)}, u32[]{:S(2)}) collective-permute-start(f32[128,256]{1,0:T(8,128)S(1)} %bitcast.29), channel_id=1, source_target_pairs={{0,3},{1,0},{2,1},{3,2},{4,7},{5,4},{6,5},{7,6},{8,11},{9,8},{10,9... | collective-permute-start | bytes 393224 | tf_op jit(solution)/shard_map/ppermute | solution.py:51
  140.1 0.1 collective-permute-start.1
  140.2 1.1 collective-permute-start
  141.4 2.7 %collective-permute-done.2 = f32[128,256]{1,0:T(8,128)S(1)} collective-permute-done((f32[128,256]{1,0:T(8,128)S(1)}, f32[128,256]{1,0:T(8,128)S(1)}, u32[]{:S(2)}, u32[]{:S(2)}) %collective-permute-start.2) | collective-permute-done | bytes 131104 | tf_op jit(solution)/shard_map/ppermute | solution.py:51
  144.0 7.4 %collective-permute-done.1 = f32[128,256]{1,0:T(8,128)S(1)} collective-permute-done((f32[128,256]{1,0:T(8,128)S(1)}, f32[128,256]{1,0:T(8,128)S(1)}, u32[]{:S(2)}, u32[]{:S(2)}) %collective-permute-start.1) | collective-permute-done | bytes 131104 | tf_op jit(solution)/shard_map/ppermute | solution.py:51
  151.4 0.0 collective-permute-done
  151.4 1.7 %fusion.3 = f32[128,256]{1,0:T(8,128)} fusion(f32[128,256]{1,0:T(8,128)S(1)} %collective-permute-done.2, f32[128,256]{1,0:T(8,128)S(1)} %collective-permute-done.1, f32[128,256]{1,0:T(8,128)S(1)} %collective-permute-done, f32[128,1,256]{2,1,0:T(1,128)S(1)} %get-tuple-element.11, f32[128,8192]{1,0:T(8,128)} %param.1, f32[256]{0:T(256)S(1)} %dynamic_slice.16, ...), kind=kLoop, calls=%fused_computation.7 | loop fusion | flops 262144 | bytes 787968 | tf_op jit(solution)/shard_map/div | solution.py:19
  (3 shorter events, 0.0 us)
Async XLA Ops:
  6.5 128.4 %reduce-scatter.2.cloned.1.call-start = ((), (), s32[]{:S(2)}) async-start(), calls=%async_computation.2 | async-start | bytes 4718592 | tf_op jit(solution)/shard_map/reduce_scatter | solution.py:59
  136.7 7.3 %collective-permute-start.2 = (f32[128,256]{1,0:T(8,128)S(1)}, f32[128,256]{1,0:T(8,128)S(1)}, u32[]{:S(2)}, u32[]{:S(2)}) collective-permute-start(f32[128,256]{1,0:T(8,128)S(1)} %bitcast.29), channel_id=1, source_target_pairs={{0,3},{1,0},{2,1},{3,2},{4,7},{5,4},{6,5},{7,6},{8,11},{9,8},{10,9... | collective-permute-start | bytes 393224 | tf_op jit(solution)/shard_map/ppermute | solution.py:51
  140.1 11.3 %collective-permute-start.1 = (f32[128,256]{1,0:T(8,128)S(1)}, f32[128,256]{1,0:T(8,128)S(1)}, u32[]{:S(2)}, u32[]{:S(2)}) collective-permute-start(f32[128,256]{1,0:T(8,128)S(1)} %bitcast.30), channel_id=1, source_target_pairs={{0,2},{1,3},{2,0},{3,1},{4,6},{5,7},{6,4},{7,5},{8,10},{9,11},{10,... | collective-permute-start | bytes 393224 | tf_op jit(solution)/shard_map/ppermute | solution.py:51
  140.2 11.2 %collective-permute-start = (f32[128,256]{1,0:T(8,128)S(1)}, f32[128,256]{1,0:T(8,128)S(1)}, u32[]{:S(2)}, u32[]{:S(2)}) collective-permute-start(f32[128,256]{1,0:T(8,128)S(1)} %bitcast.31), channel_id=1, source_target_pairs={{0,1},{1,2},{2,3},{3,0},{4,5},{5,6},{6,7},{7,4},{8,9},{9,10},{10,1... | collective-permute-start | bytes 393224 | tf_op jit(solution)/shard_map/ppermute | solution.py:51
Sparse Core Ops, SparseCore 0:
  83.6 51.3 reduce-scatter.1

commit v3 on v2

--- a/solution.py
+++ b/solution.py
@@ -50,12 +50,19 @@
         perm = [(i, (i + s) % n_col) for i in range(n_col)]
         total = total + lax.ppermute(send, "col", perm)
     return total
+from jax.experimental.layout import Layout, with_layout_constraint
 
 
 def body(adjacency):
-    strip_rows = adjacency.shape[0]
-    window = strip_rows * lax.axis_size("row") // lax.axis_size("col")
-    pieces = lax.all_to_all(adjacency, "row", split_axis=1, concat_axis=0, tiled=True)
+    strip_rows, cols = adjacency.shape
+    n_row = lax.axis_size("row")
+    window = strip_rows * n_row // lax.axis_size("col")
+    piece = cols // n_row
+    chunks = jnp.stack([adjacency[:, d * piece : (d + 1) * piece] for d in range(n_row)])
+    chunks = with_layout_constraint(chunks, Layout((0, 1, 2)))
+    pieces = lax.all_to_all(chunks, "row", split_axis=0, concat_axis=0, tiled=True)
+    pieces = with_layout_constraint(pieces, Layout((0, 1, 2)))
+    pieces = pieces.reshape(n_row * strip_rows, cols // n_row)
     part = lax.psum_scatter(inner_rows(pieces, pieces), "row", scatter_dimension=0, tiled=True)
     own_degree = lax.psum(jnp.sum(adjacency, axis=1), "col")
     all_degree = lax.all_gather(own_degree, "row", axis=0, tiled=True)

time: 160 us -> 154 us (0.963)
  matrix products: 11.7 us -> 8.3 us
  local copies, waits for them, and re-layouts: 12.8 us -> 10.5 us
    all_to_all x1 -> x0, local copies, waits for them, and re-layouts: 5.34 us -> none  [body(): lax.all_to_all(adjacency, 'row', split_axis=1, concat_axis=0, tiled=True)]
    dot_general x1, matrix products: 11.7 us -> 8.3 us  [inner_rows(): lax.dot_general(left, right, (((1,), (1,)), ((), ())), precision=lax.Prec...]
    unnamed x4 -> x10, local copies, waits for them, and re-layouts: 5.6 us -> 7.59 us
where the time goes in v3:
time: 154 us; the launch traced here: 153 us
  blocking collectives  73.8 us (48%)
  waiting for transfers between devices  38.5 us (25%)
  between operations  13.5 us (9%)
  local copies, waits for them, and re-layouts  10.5 us (7%)
  matrix products  8.3 us (5%)
  starting transfers between devices  4.61 us (3%)
  other arithmetic  4.17 us (3%)
    all_to_all x1, blocking collectives, body(): lax.all_to_all(chunks, 'row', split_axis=0, concat_axis=0, tiled=True)  54 us
    reduce_scatter x1, waiting for transfers between devices, body(): lax.psum_scatter(inner_rows(pieces, pieces), 'row', scatter_dimension=0,...  28.5 us
    psum x1, blocking collectives, body(): own_degree = lax.psum(jnp.sum(adjacency, axis=1), 'col')  12 us
    ppermute x3, waiting for transfers between devices, col_reduce_scatter(): total = total + lax.ppermute(send, 'col', perm)  10 us
    dot_general x1, matrix products, inner_rows(): lax.dot_general(left, right, (((1,), (1,)), ((), ())), precision=lax.Prec...  8.3 us
    all_gather x1, blocking collectives, body(): all_degree = lax.all_gather(own_degree, 'row', axis=0, tiled=True)  7.78 us
    unnamed x10, local copies, waits for them, and re-layouts  7.59 us
    ppermute x3, starting transfers between devices, col_reduce_scatter(): total = total + lax.ppermute(send, 'col', perm)  4.61 us
  transfers between devices with their start and end apart: 4, of which 3 were waited for; matrix products, arithmetic and copies ran while one was open for 2% of the time, Pallas kernels for 0%

profile of v3, /device:TPU:0, one launch (start us, length us, event | category | flops | bytes accessed | tf_op | source)
XLA Modules:
  0.0 153.3 jit_solution(5997456584988540996)
XLA Ops:
  6.5 0.0 reduce-scatter.2.cloned.1.call-start
  6.5 1.1 bitcast_dynamic-update-slice_fusion.7
  7.6 1.1 bitcast_dynamic-update-slice_fusion.6
  8.7 1.1 bitcast_dynamic-update-slice_fusion.5
  9.8 1.1 bitcast_dynamic-update-slice_fusion.4
  10.9 1.1 bitcast_dynamic-update-slice_fusion.3
  12.0 1.1 bitcast_dynamic-update-slice_fusion.2
  13.0 1.1 bitcast_dynamic-update-slice_fusion.1
  14.1 1.1 bitcast_dynamic-update-slice_fusion
  15.2 54.0 %all_to_all.5 = f32[8,128,1024]{2,1,0:T(8,128)S(1)} all-to-all(f32[8,128,1024]{2,1,0:T(8,128)S(1)} %bitcast_dynamic-update-slice_fusion), channel_id=1, replica_groups=mesh['row'=8,'col'=4] {'row'}, dimensions={0} | all-to-all | bytes 8388608 | tf_op jit(solution)/shard_map/all_to_all | solution.py:63
  69.2 8.3 %fusion.4 = f32[1024,1024]{1,0:T(8,128)} fusion(f32[1024,1024]{1,0:T(8,128)S(1)} %bitcast.40), kind=kOutput, calls=%fused_computation.20 | convolution fusion | flops 6442450944 | bytes 8388608 | tf_op jit(solution)/shard_map/dot_general | solution.py:8
  77.5 0.0 reduce-scatter.2.cloned.1.call-update
  77.6 2.5 %reduce_sum.9 = f32[128]{0:T(128)S(1)} reduce(f32[128,8192]{1,0:T(8,128)} %param.1, f32[]{:T(128)} %constant.39.clone.1), dimensions={1}, to_apply=%region_1.0 | reduce | flops 1048448 | bytes 4194820 | tf_op jit(solution)/shard_map/reduce_sum | solution.py:67
  80.1 12.0 %psum.7 = f32[128]{0:T(128)S(1)} all-reduce(f32[128]{0:T(128)S(1)} %reduce_sum.9), channel_id=1, replica_groups=mesh['row'=8,'col'=4] {'col'}, use_global_device_ids=true, to_apply=%region_2.0 | all-reduce | flops 128 | bytes 1024 | tf_op jit(solution)/shard_map/psum | solution.py:67
  92.1 7.8 %all-gather = f32[8,1,128]{2,1,0:T(1,128)S(1)} all-gather(f32[1,1,128]{2,1,0:T(1,128)S(1)} %bitcast.45), channel_id=1, replica_groups=mesh['row'=8,'col'=4] {'row'}, dimensions={0}, use_global_device_ids=true | all-gather | bytes 4608 | tf_op jit(solution)/shard_map/all_gather | solution.py:68
  99.8 0.1 dynamic_slice.16
  99.9 28.5 %reduce-scatter.2.cloned.1.call-done = f32[128,1024]{1,0:T(8,128)} async-done(((f32[1024,1024]{1,0:T(8,128)}), f32[128,1024]{1,0:T(8,128)}) %reduce-scatter.2.cloned.1.call-update) | async-done | bytes 524304 | tf_op jit(solution)/shard_map/reduce_scatter | solution.py:66
  128.4 1.3 reshape.9
  129.7 0.5 constant_dynamic-slice_fusion.3
  130.2 3.4 %collective-permute-start.2 = (f32[128,256]{1,0:T(8,128)S(1)}, f32[128,256]{1,0:T(8,128)S(1)}, u32[]{:S(2)}, u32[]{:S(2)}) collective-permute-start(f32[128,256]{1,0:T(8,128)S(1)} %bitcast.41), channel_id=1, source_target_pairs={{0,3},{1,0},{2,1},{3,2},{4,7},{5,4},{6,5},{7,6},{8,11},{9,8},{10,9... | collective-permute-start | bytes 393224 | tf_op jit(solution)/shard_map/ppermute | solution.py:51
  133.6 0.1 collective-permute-start.1
  133.7 1.1 collective-permute-start
  134.8 2.7 %collective-permute-done.2 = f32[128,256]{1,0:T(8,128)S(1)} collective-permute-done((f32[128,256]{1,0:T(8,128)S(1)}, f32[128,256]{1,0:T(8,128)S(1)}, u32[]{:S(2)}, u32[]{:S(2)}) %collective-permute-start.2) | collective-permute-done | bytes 131104 | tf_op jit(solution)/shard_map/ppermute | solution.py:51
  137.5 7.4 %collective-permute-done.1 = f32[128,256]{1,0:T(8,128)S(1)} collective-permute-done((f32[128,256]{1,0:T(8,128)S(1)}, f32[128,256]{1,0:T(8,128)S(1)}, u32[]{:S(2)}, u32[]{:S(2)}) %collective-permute-start.1) | collective-permute-done | bytes 131104 | tf_op jit(solution)/shard_map/ppermute | solution.py:51
  144.8 0.0 collective-permute-done
  144.8 1.7 %fusion.3 = f32[128,256]{1,0:T(8,128)} fusion(f32[128,256]{1,0:T(8,128)S(1)} %collective-permute-done.2, f32[128,256]{1,0:T(8,128)S(1)} %collective-permute-done.1, f32[128,256]{1,0:T(8,128)S(1)} %collective-permute-done, f32[128,1,256]{2,1,0:T(1,128)S(1)} %get-tuple-element.11, f32[128,8192]{1,0:T(8,128)} %param.1, f32[256]{0:T(256)S(1)} %dynamic_slice.16, ...), kind=kLoop, calls=%fused_computation.15 | loop fusion | flops 262144 | bytes 787968 | tf_op jit(solution)/shard_map/div | solution.py:19
  (3 shorter events, 0.0 us)
Async XLA Ops:
  6.5 121.9 %reduce-scatter.2.cloned.1.call-start = ((), (), s32[]{:S(2)}) async-start(), calls=%async_computation.2 | async-start | bytes 4718592 | tf_op jit(solution)/shard_map/reduce_scatter | solution.py:66
  130.2 7.3 %collective-permute-start.2 = (f32[128,256]{1,0:T(8,128)S(1)}, f32[128,256]{1,0:T(8,128)S(1)}, u32[]{:S(2)}, u32[]{:S(2)}) collective-permute-start(f32[128,256]{1,0:T(8,128)S(1)} %bitcast.41), channel_id=1, source_target_pairs={{0,3},{1,0},{2,1},{3,2},{4,7},{5,4},{6,5},{7,6},{8,11},{9,8},{10,9... | collective-permute-start | bytes 393224 | tf_op jit(solution)/shard_map/ppermute | solution.py:51
  133.6 11.3 %collective-permute-start.1 = (f32[128,256]{1,0:T(8,128)S(1)}, f32[128,256]{1,0:T(8,128)S(1)}, u32[]{:S(2)}, u32[]{:S(2)}) collective-permute-start(f32[128,256]{1,0:T(8,128)S(1)} %bitcast.42), channel_id=1, source_target_pairs={{0,2},{1,3},{2,0},{3,1},{4,6},{5,7},{6,4},{7,5},{8,10},{9,11},{10,... | collective-permute-start | bytes 393224 | tf_op jit(solution)/shard_map/ppermute | solution.py:51
  133.7 11.2 %collective-permute-start = (f32[128,256]{1,0:T(8,128)S(1)}, f32[128,256]{1,0:T(8,128)S(1)}, u32[]{:S(2)}, u32[]{:S(2)}) collective-permute-start(f32[128,256]{1,0:T(8,128)S(1)} %bitcast.43), channel_id=1, source_target_pairs={{0,1},{1,2},{2,3},{3,0},{4,5},{5,6},{6,7},{7,4},{8,9},{9,10},{10,1... | collective-permute-start | bytes 393224 | tf_op jit(solution)/shard_map/ppermute | solution.py:51
Sparse Core Ops, SparseCore 0:
  77.7 50.6 reduce-scatter.1

commit v4 on v3

v4 whole, which is shorter than its diff:
```python
import jax
import jax.numpy as jnp
from jax import lax
from jax.sharding import Mesh
from jax.sharding import PartitionSpec as P
from jax.experimental.layout import Layout, with_layout_constraint

ROW = ("chip", "core")


def inner_rows(left, right):
    return lax.dot_general(
        left,
        right,
        (((1,), (1,)), ((), ())),
        precision=lax.Precision.HIGH,
        preferred_element_type=jnp.float32,
    )


def col_reduce_scatter(part):
    n_col = lax.axis_size("col")
    me = lax.axis_index("col")
    rows, cols = part.shape
    width = cols // n_col
    blocks = part.reshape(rows, n_col, width)
    total = lax.dynamic_index_in_dim(blocks, me, 1, keepdims=False)
    for s in range(1, n_col):
        send = lax.dynamic_index_in_dim(blocks, (me + s) % n_col, 1, keepdims=False)
        perm = [(i, (i + s) % n_col) for i in range(n_col)]
        total = total + lax.ppermute(send, "col", perm)
    return total


def row_reduce_scatter(pieces):
    n_chip = lax.axis_size("chip")
    n_core = lax.axis_size("core")
    me = lax.axis_index("core")
    rows, depth = pieces.shape
    strip = rows // (n_chip * n_core)
    paired = inner_rows(pieces, pieces).reshape(n_chip, n_core, strip, rows)
    on_chip = lax.dynamic_index_in_dim(paired, me, 1, keepdims=False)
    for s in range(1, n_core):
        send = lax.dynamic_index_in_dim(paired, (me + s) % n_core, 1, keepdims=False)
        perm = [(i, (i + s) % n_core) for i in range(n_core)]
        on_chip = on_chip + lax.ppermute(send, "core", perm)
    blocks = on_chip.reshape(n_chip, strip, rows)
    mine = lax.axis_index("chip")
    total = lax.dynamic_index_in_dim(blocks, mine, 0, keepdims=False)
    for s in range(1, n_chip):
        send = lax.dynamic_index_in_dim(blocks, (mine + s) % n_chip, 0, keepdims=False)
        perm = [(i, (i + s) % n_chip) for i in range(n_chip)]
        total = total + lax.ppermute(send, "chip", perm)
    return total


def body(adjacency):
    strip_rows, cols = adjacency.shape
    n_row = lax.axis_size(ROW)
    window = strip_rows * n_row // lax.axis_size("col")
    piece = cols // n_row
    chunks = jnp.stack([adjacency[:, d * piece : (d + 1) * piece] for d in range(n_row)])
    chunks = with_layout_constraint(chunks, Layout((0, 1, 2)))
    pieces = lax.all_to_all(chunks, ROW, split_axis=0, concat_axis=0, tiled=True)
    pieces = with_layout_constraint(pieces, Layout((0, 1, 2)))
    own_degree = lax.psum(jnp.sum(adjacency, axis=1), "col")
    all_degree = lax.all_gather(own_degree, ROW, axis=0, tiled=True)
    col_degree = lax.dynamic_slice_in_dim(all_degree, lax.axis_index("col") * window, window, 0)
    pieces, own_degree, col_degree = lax.optimization_barrier((pieces, own_degree, col_degree))
    pieces = pieces.reshape(n_row * strip_rows, piece)
    shared_sum = col_reduce_scatter(row_reduce_scatter(pieces))
    linked = adjacency[:, :window]
    smaller = jnp.minimum(own_degree[:, None], col_degree[None, :])
    return (shared_sum + linked) / (smaller + 1.0 - linked)


def solution(mesh):
    n_row, n_col = mesh.devices.shape
    split = Mesh(mesh.devices.reshape(n_row // 2, 2, n_col), ("chip", "core", "col"))
    placed = (P(ROW, "col"),)
    return jax.shard_map(body, mesh=split, in_specs=placed, out_specs=P(ROW, "col"), check_vma=False)
```

time: 154 us -> 138 us (0.90)
  blocking collectives: 73.8 us -> 49.6 us
  between operations: 13.5 us -> 0.11 us
  local copies, waits for them, and re-layouts: 10.5 us -> 21.7 us
  starting transfers between devices: 4.61 us -> 13.7 us
  waiting for transfers between devices: 38.5 us -> 35.2 us
  matrix products: 8.3 us -> 11 us
  other arithmetic: 4.17 us -> 6.23 us
    all_to_all x1 -> x0, blocking collectives: 54 us -> none  [body(): lax.all_to_all(chunks, 'row', split_axis=0, concat_axis=0, tiled=True)]
    all_gather x1, blocking collectives: 7.78 us -> 36.8 us  [body(): all_degree = lax.all_gather(own_degree, ROW, axis=0, tiled=True)]
    reduce_scatter x1 -> x0, waiting for transfers between devices: 28.5 us -> none  [body(): lax.psum_scatter(inner_rows(pieces, pieces), 'row', scatter_dimension=0,...]
    ppermute x0 -> x4, waiting for transfers between devices: none -> 25.8 us  [the longest x3 21.8 us: row_reduce_scatter(): total = total + lax.ppermute(send, 'chip', perm)]
    unnamed x10 -> x9, local copies, waits for them, and re-layouts: 7.59 us -> 15.2 us
    all_to_all x0 -> x1, starting transfers between devices: none -> 5.17 us  [body(): lax.all_to_all(chunks, ROW, split_axis=0, concat_axis=0, tiled=True)]
    ppermute x0 -> x4, starting transfers between devices: none -> 3.04 us  [the longest x3 2.72 us: row_reduce_scatter(): total = total + lax.ppermute(send, 'chip', perm)]
    dynamic_slice x0 -> x8, local copies, waits for them, and re-layouts: none -> 2.8 us  [the longest x3 2.18 us: row_reduce_scatter(): lax.dynamic_index_in_dim(blocks, (mine + s) % n_chip, 0, keepdims=False)]
  transfers between devices with their start and end apart: 4 -> 8, of which waited for: 3 -> 5; matrix products, arithmetic and copies ran while one was open for 2% -> 4% of each run, Pallas kernels for 0% -> 0%
where the time goes in v4:
time: 138 us; the launch traced here: 137 us
  blocking collectives  49.6 us (36%)
  waiting for transfers between devices  35.2 us (26%)
  local copies, waits for them, and re-layouts  21.7 us (16%)
  starting transfers between devices  13.7 us (10%)
  matrix products  11 us (8%)
  other arithmetic  6.23 us (5%)
    all_gather x1, blocking collectives, body(): all_degree = lax.all_gather(own_degree, ROW, axis=0, tiled=True)  36.8 us
    ppermute x3, waiting for transfers between devices, row_reduce_scatter(): total = total + lax.ppermute(send, 'chip', perm)  21.8 us
    unnamed x9, local copies, waits for them, and re-layouts  15.2 us
    psum x1, blocking collectives, body(): own_degree = lax.psum(jnp.sum(adjacency, axis=1), 'col')  12.8 us
    dot_general x1, matrix products, inner_rows(): lax.dot_general(left, right, (((1,), (1,)), ((), ())), precision=lax.Prec...  11 us
    ppermute x3, waiting for transfers between devices, col_reduce_scatter(): total = total + lax.ppermute(send, 'col', perm)  9.37 us
    ppermute x3, starting transfers between devices, col_reduce_scatter(): total = total + lax.ppermute(send, 'col', perm)  5.5 us
    all_to_all x1, starting transfers between devices, body(): lax.all_to_all(chunks, ROW, split_axis=0, concat_axis=0, tiled=True)  5.17 us
  transfers between devices with their start and end apart: 8, of which 5 were waited for; matrix products, arithmetic and copies ran while one was open for 4% of the time, Pallas kernels for 0%

profile of v4, /device:TPU:0, one launch (start us, length us, event | category | flops | bytes accessed | tf_op | source)
XLA Modules:
  0.0 137.5 jit_solution(6909396505464349731)
XLA Ops:
  0.0 1.9 %bitcast_dynamic-update-slice_fusion.7 = f32[8,128,1024]{2,1,0:T(8,128)} fusion(f32[128,8192]{1,0:T(8,128)} %param.1), kind=kLoop, calls=%fused_computation.12 | loop fusion | bytes 1048576
  1.9 1.9 %bitcast_dynamic-update-slice_fusion.6 = f32[8,128,1024]{2,1,0:T(8,128)} fusion(f32[8,128,1024]{2,1,0:T(8,128)} %bitcast_dynamic-update-slice_fusion.7, f32[128,8192]{1,0:T(8,128)} %param.1), kind=kLoop, calls=%fused_computation.11 | loop fusion | bytes 1048576
  3.8 1.9 %bitcast_dynamic-update-slice_fusion.5 = f32[8,128,1024]{2,1,0:T(8,128)} fusion(f32[8,128,1024]{2,1,0:T(8,128)} %bitcast_dynamic-update-slice_fusion.6, f32[128,8192]{1,0:T(8,128)} %param.1), kind=kLoop, calls=%fused_computation.10 | loop fusion | bytes 1048576
  5.7 1.9 %bitcast_dynamic-update-slice_fusion.4 = f32[8,128,1024]{2,1,0:T(8,128)} fusion(f32[8,128,1024]{2,1,0:T(8,128)} %bitcast_dynamic-update-slice_fusion.5, f32[128,8192]{1,0:T(8,128)} %param.1), kind=kLoop, calls=%fused_computation.9 | loop fusion | bytes 1048576
  7.6 1.9 %bitcast_dynamic-update-slice_fusion.3 = f32[8,128,1024]{2,1,0:T(8,128)} fusion(f32[8,128,1024]{2,1,0:T(8,128)} %bitcast_dynamic-update-slice_fusion.4, f32[128,8192]{1,0:T(8,128)} %param.1), kind=kLoop, calls=%fused_computation.8 | loop fusion | bytes 1048576
  9.5 1.9 %bitcast_dynamic-update-slice_fusion.2 = f32[8,128,1024]{2,1,0:T(8,128)} fusion(f32[8,128,1024]{2,1,0:T(8,128)} %bitcast_dynamic-update-slice_fusion.3, f32[128,8192]{1,0:T(8,128)} %param.1), kind=kLoop, calls=%fused_computation.7 | loop fusion | bytes 1048576
  11.4 1.9 %bitcast_dynamic-update-slice_fusion.1 = f32[8,128,1024]{2,1,0:T(8,128)} fusion(f32[8,128,1024]{2,1,0:T(8,128)} %bitcast_dynamic-update-slice_fusion.2, f32[128,8192]{1,0:T(8,128)} %param.1), kind=kLoop, calls=%fused_computation.6 | loop fusion | bytes 1048576
  13.3 1.9 %bitcast_dynamic-update-slice_fusion = f32[8,128,1024]{2,1,0:T(8,128)} fusion(f32[8,128,1024]{2,1,0:T(8,128)} %bitcast_dynamic-update-slice_fusion.1, f32[128,8192]{1,0:T(8,128)} %param.1), kind=kLoop, calls=%fused_computation.5 | loop fusion | bytes 1048576 | tf_op jit(solution)/shard_map/stack | solution.py:62
  15.2 5.2 %all-to-all-start = ((f32[8,128,1024]{2,1,0:T(8,128)}), f32[8,128,1024]{2,1,0:T(8,128)}, u32[]{:S(2)}, u32[]{:S(2)}) async-start(f32[8,128,1024]{2,1,0:T(8,128)} %bitcast_dynamic-update-slice_fusion), calls=%async_computation | async-start | bytes 8388608 | tf_op jit(solution)/shard_map/all_to_all | solution.py:64
  20.4 2.5 %reduce_sum.9 = f32[128]{0:T(128)S(1)} reduce(f32[128,8192]{1,0:T(8,128)} %param.1, f32[]{:T(128)} %constant.80.clone.1), dimensions={1}, to_apply=%region_0.0 | reduce | flops 1048448 | bytes 4194820 | tf_op jit(solution)/shard_map/reduce_sum | solution.py:66
  22.9 12.8 %psum.7 = f32[128]{0:T(128)S(1)} all-reduce(f32[128]{0:T(128)S(1)} %reduce_sum.9), channel_id=1, replica_groups=mesh['chip'=4,'core'=2,'col'=4] {'col'}, use_global_device_ids=true, to_apply=%region_1.0 | all-reduce | flops 128 | bytes 1024 | tf_op jit(solution)/shard_map/psum | solution.py:66
  35.7 36.8 %all-gather = f32[8,1,128]{2,1,0:T(1,128)S(1)} all-gather(f32[1,1,128]{2,1,0:T(1,128)S(1)} %bitcast.59), channel_id=1, replica_groups=mesh['chip'=4,'core'=2,'col'=4] {'chip','core'}, dimensions={0}, use_global_device_ids=true | all-gather | bytes 4608 | tf_op jit(solution)/shard_map/all_gather | solution.py:67
  72.5 0.1 dynamic_slice.36
  72.5 0.0 all-to-all-done
  72.5 11.0 %fusion.6 = f32[4,2,128,1024]{3,2,1,0:T(8,128)S(1)} fusion(f32[4,2,128,1024]{3,2,1,0:T(8,128)} %bitcast.10, f32[1024,1024,1,1]{1,0,3,2:T(8,128)} %bitcast.13), kind=kOutput, calls=%fused_computation.26 | convolution fusion | flops 6442450944 | bytes 12582912 | tf_op jit(solution)/shard_map/dot_general | solution.py:12
  83.5 0.0 copy-start
  83.5 1.9 %copy-done = f32[4,2,128,1024]{3,2,1,0:T(8,128)} copy-done((f32[4,2,128,1024]{3,2,1,0:T(8,128)}, f32[4,2,128,1024]{3,2,1,0:T(8,128)S(1)}, u32[]{:S(2)}) %copy-start) | copy-done | bytes 4194328
  85.5 1.6 %dynamic-slice_bitcast_fusion = f32[4,128,1024]{2,1,0:T(8,128)} fusion(f32[4,2,128,1024]{3,2,1,0:T(8,128)S(1)} %fusion.6, s32[]{:T(128)S(6)} %select_n.70), kind=kLoop, calls=%fused_computation.1 | loop fusion | bytes 4194308 | tf_op jit(solution)/shard_map/jit(dynamic_index_in_dim)/squeeze | solution.py:44
  87.0 0.3 collective-permute-start
  87.4 4.0 %collective-permute-done = f32[4,128,1024]{2,1,0:T(8,128)S(1)} collective-permute-done((f32[4,128,1024]{2,1,0:T(8,128)}, f32[4,128,1024]{2,1,0:T(8,128)S(1)}, u32[]{:S(2)}, u32[]{:S(2)}) %collective-permute-start) | collective-permute-done | bytes 2097184 | tf_op jit(solution)/shard_map/ppermute | solution.py:46
  91.4 2.0 %bitcast_add_fusion = f32[4,128,1024]{2,1,0:T(8,128)S(1)} fusion(f32[4,128,1024]{2,1,0:T(8,128)S(1)} %collective-permute-done, f32[4,2,128,1024]{3,2,1,0:T(8,128)} %copy-done, s32[]{:T(128)S(6)} %select_n.68), kind=kLoop, calls=%fused_computation | loop fusion | flops 524288 | bytes 6291460 | tf_op jit(solution)/shard_map/add | solution.py:46
  93.4 0.1 constant_dynamic-slice_fusion.7
  93.5 0.2 copy.17
  93.7 0.3 collective-permute-start.3
  94.0 1.0 copy.16
  95.0 0.7 collective-permute-start.2
  95.6 1.0 copy.15
  96.6 1.8 %collective-permute-start.1 = (f32[128,1024]{0,1:T(8,128)}, f32[128,1024]{0,1:T(8,128)S(1)}, u32[]{:S(2)}, u32[]{:S(2)}) collective-permute-start(f32[128,1024]{0,1:T(8,128)} %bitcast.17), channel_id=1, source_target_pairs={{0,8},{8,16},{16,24},{24,0},{1,9},{9,17},{17,25},{25,1},{2,10},{10... | collective-permute-start | bytes 1572872 | tf_op jit(solution)/shard_map/ppermute | solution.py:53
  98.5 0.2 copy.14
  98.6 9.9 %collective-permute-done.3 = f32[128,1024]{0,1:T(8,128)S(1)} collective-permute-done((f32[128,1024]{0,1:T(8,128)S(1)}, f32[128,1024]{0,1:T(8,128)S(1)}, u32[]{:S(2)}, u32[]{:S(2)}) %collective-permute-start.3) | collective-permute-done | bytes 524320 | tf_op jit(solution)/shard_map/ppermute | solution.py:53
  108.5 11.9 %collective-permute-done.2 = f32[128,1024]{0,1:T(8,128)S(1)} collective-permute-done((f32[128,1024]{0,1:T(8,128)}, f32[128,1024]{0,1:T(8,128)S(1)}, u32[]{:S(2)}, u32[]{:S(2)}) %collective-permute-start.2) | collective-permute-done | bytes 524320 | tf_op jit(solution)/shard_map/ppermute | solution.py:53
  120.4 0.0 collective-permute-done.1
  120.4 0.1 fusion.1
  120.6 0.1 copy.21
  120.7 4.4 %collective-permute-start.6 = (f32[128,256]{1,0:T(8,128)S(1)}, f32[128,256]{1,0:T(8,128)S(1)}, u32[]{:S(2)}, u32[]{:S(2)}) collective-permute-start(f32[128,256]{1,0:T(8,128)S(1)} %bitcast.55), channel_id=1, source_target_pairs={{0,3},{1,0},{2,1},{3,2},{4,7},{5,4},{6,5},{7,6},{8,11},{9,8},{10,9... | collective-permute-start | bytes 393224 | tf_op jit(solution)/shard_map/ppermute | solution.py:31
  125.0 0.1 copy.20
  125.1 0.1 collective-permute-start.5
  125.2 0.1 copy.19
  125.3 1.1 collective-permute-start.4
  126.4 0.1 copy.18
  126.5 2.5 %collective-permute-done.6 = f32[128,256]{1,0:T(8,128)S(1)} collective-permute-done((f32[128,256]{1,0:T(8,128)S(1)}, f32[128,256]{1,0:T(8,128)S(1)}, u32[]{:S(2)}, u32[]{:S(2)}) %collective-permute-start.6) | collective-permute-done | bytes 131104 | tf_op jit(solution)/shard_map/ppermute | solution.py:31
  129.0 6.8 %collective-permute-done.5 = f32[128,256]{1,0:T(8,128)S(1)} collective-permute-done((f32[128,256]{1,0:T(8,128)S(1)}, f32[128,256]{1,0:T(8,128)S(1)}, u32[]{:S(2)}, u32[]{:S(2)}) %collective-permute-start.5) | collective-permute-done | bytes 131104 | tf_op jit(solution)/shard_map/ppermute | solution.py:31
  135.8 0.0 collective-permute-done.4
  135.8 1.7 %fusion.5 = f32[128,256]{1,0:T(8,128)} fusion(f32[128,256]{1,0:T(8,128)S(1)} %collective-permute-done.6, f32[128,256]{1,0:T(8,128)S(1)} %collective-permute-done.5, f32[128,256]{1,0:T(8,128)S(1)} %collective-permute-done.4, f32[128,1,256]{2,0,1:T(8,128)S(1)} %copy.18, f32[128,8192]{1,0:T(8,128)} %param.1, f32[256]{0:T(256)S(1)} %dynamic_slice.36, f32[128]{0:T(128)S(1)} %psum.7), kind=kLoop, calls=%fused_computation.17 | loop fusion | flops 262144 | bytes 787968 | tf_op jit(solution)/shard_map/div | solution.py:74
  (1 shorter events, 0.0 us)
Async XLA Ops:
  15.2 57.4 %all-to-all-start = ((f32[8,128,1024]{2,1,0:T(8,128)}), f32[8,128,1024]{2,1,0:T(8,128)}, u32[]{:S(2)}, u32[]{:S(2)}) async-start(f32[8,128,1024]{2,1,0:T(8,128)} %bitcast_dynamic-update-slice_fusion), calls=%async_computation | async-start | bytes 8388608 | tf_op jit(solution)/shard_map/all_to_all | solution.py:64
  83.5 1.9 %copy-start = (f32[4,2,128,1024]{3,2,1,0:T(8,128)}, f32[4,2,128,1024]{3,2,1,0:T(8,128)S(1)}, u32[]{:S(2)}) copy-start(f32[4,2,128,1024]{3,2,1,0:T(8,128)S(1)} %fusion.6) | copy-start | bytes 12582916
  87.0 4.4 %collective-permute-start = (f32[4,128,1024]{2,1,0:T(8,128)}, f32[4,128,1024]{2,1,0:T(8,128)S(1)}, u32[]{:S(2)}, u32[]{:S(2)}) collective-permute-start(f32[4,128,1024]{2,1,0:T(8,128)} %dynamic-slice_bitcast_fusion), channel_id=1, source_target_pairs={{0,4},{4,0},{1,5},{5,1},{2,6},{6,2},{3,7},{7,3},{8,12},{12,8},{9,1... | collective-permute-start | bytes 6291464 | tf_op jit(solution)/shard_map/ppermute | solution.py:46
  93.7 14.8 %collective-permute-start.3 = (f32[128,1024]{0,1:T(8,128)S(1)}, f32[128,1024]{0,1:T(8,128)S(1)}, u32[]{:S(2)}, u32[]{:S(2)}) collective-permute-start(f32[128,1024]{0,1:T(8,128)S(1)} %bitcast.54), channel_id=1, source_target_pairs={{0,24},{8,0},{16,8},{24,16},{1,25},{9,1},{17,9},{25,17},{2,26},{10... | collective-permute-start | bytes 1572872 | tf_op jit(solution)/shard_map/ppermute | solution.py:53
  95.0 25.4 %collective-permute-start.2 = (f32[128,1024]{0,1:T(8,128)}, f32[128,1024]{0,1:T(8,128)S(1)}, u32[]{:S(2)}, u32[]{:S(2)}) collective-permute-start(f32[128,1024]{0,1:T(8,128)} %bitcast.18), channel_id=1, source_target_pairs={{0,16},{8,24},{16,0},{24,8},{1,17},{9,25},{17,1},{25,9},{2,18},{10... | collective-permute-start | bytes 1572872 | tf_op jit(solution)/shard_map/ppermute | solution.py:53
  96.6 23.8 %collective-permute-start.1 = (f32[128,1024]{0,1:T(8,128)}, f32[128,1024]{0,1:T(8,128)S(1)}, u32[]{:S(2)}, u32[]{:S(2)}) collective-permute-start(f32[128,1024]{0,1:T(8,128)} %bitcast.17), channel_id=1, source_target_pairs={{0,8},{8,16},{16,24},{24,0},{1,9},{9,17},{17,25},{25,1},{2,10},{10... | collective-permute-start | bytes 1572872 | tf_op jit(solution)/shard_map/ppermute | solution.py:53
  120.7 8.3 %collective-permute-start.6 = (f32[128,256]{1,0:T(8,128)S(1)}, f32[128,256]{1,0:T(8,128)S(1)}, u32[]{:S(2)}, u32[]{:S(2)}) collective-permute-start(f32[128,256]{1,0:T(8,128)S(1)} %bitcast.55), channel_id=1, source_target_pairs={{0,3},{1,0},{2,1},{3,2},{4,7},{5,4},{6,5},{7,6},{8,11},{9,8},{10,9... | collective-permute-start | bytes 393224 | tf_op jit(solution)/shard_map/ppermute | solution.py:31
  125.1 10.7 %collective-permute-start.5 = (f32[128,256]{1,0:T(8,128)S(1)}, f32[128,256]{1,0:T(8,128)S(1)}, u32[]{:S(2)}, u32[]{:S(2)}) collective-permute-start(f32[128,256]{1,0:T(8,128)S(1)} %bitcast.56), channel_id=1, source_target_pairs={{0,2},{1,3},{2,0},{3,1},{4,6},{5,7},{6,4},{7,5},{8,10},{9,11},{10,... | collective-permute-start | bytes 393224 | tf_op jit(solution)/shard_map/ppermute | solution.py:31
  125.3 10.5 %collective-permute-start.4 = (f32[128,256]{1,0:T(8,128)S(1)}, f32[128,256]{1,0:T(8,128)S(1)}, u32[]{:S(2)}, u32[]{:S(2)}) collective-permute-start(f32[128,256]{1,0:T(8,128)S(1)} %bitcast.57), channel_id=1, source_target_pairs={{0,1},{1,2},{2,3},{3,0},{4,5},{5,6},{6,7},{7,4},{8,9},{9,10},{10,1... | collective-permute-start | bytes 393224 | tf_op jit(solution)/shard_map/ppermute | solution.py:31

commit v5 on v4

--- a/solution.py
+++ b/solution.py
@@ -3,6 +3,7 @@
 from jax import lax
 from jax.sharding import Mesh
 from jax.sharding import PartitionSpec as P
+from jax.experimental import pallas as pl
 from jax.experimental.layout import Layout, with_layout_constraint
 
 ROW = ("chip", "core")
@@ -16,6 +17,22 @@
         precision=lax.Precision.HIGH,
         preferred_element_type=jnp.float32,
     )
+
+
+def _copy_block(block_ref, out_ref):
+    out_ref[0] = block_ref[...]
+
+
+def column_chunks(adjacency, n_chunks):
+    rows, cols = adjacency.shape
+    piece = cols // n_chunks
+    return pl.pallas_call(
+        _copy_block,
+        grid=(n_chunks,),
+        in_specs=[pl.BlockSpec((rows, piece), lambda d: (0, d))],
+        out_specs=pl.BlockSpec((1, rows, piece), lambda d: (d, 0, 0)),
+        out_shape=jax.ShapeDtypeStruct((n_chunks, rows, piece), adjacency.dtype),
+    )(adjacency)
 
 
 def col_reduce_scatter(part):
@@ -59,8 +76,7 @@
     n_row = lax.axis_size(ROW)
     window = strip_rows * n_row // lax.axis_size("col")
     piece = cols // n_row
-    chunks = jnp.stack([adjacency[:, d * piece : (d + 1) * piece] for d in range(n_row)])
-    chunks = with_layout_constraint(chunks, Layout((0, 1, 2)))
+    chunks = column_chunks(adjacency, n_row)
     pieces = lax.all_to_all(chunks, ROW, split_axis=0, concat_axis=0, tiled=True)
     pieces = with_layout_constraint(pieces, Layout((0, 1, 2)))
     own_degree = lax.psum(jnp.sum(adjacency, axis=1), "col")

time: 138 us -> 129 us (0.935)
  local copies, waits for them, and re-layouts: 21.7 us -> 6.51 us
  Pallas kernels: 0 us -> 6.65 us
    unnamed x9 -> x2, local copies, waits for them, and re-layouts: 15.2 us -> 1.94 us
    pallas_call x0 -> x1, Pallas kernels: none -> 6.65 us  [column_chunks(): pl.pallas_call(_copy_block, grid=(n_chunks,), in_specs=[pl.BlockSpec((row...]
    another operation x1 -> x0, local copies, waits for them, and re-layouts: 1.93 us -> none  [body(): jnp.stack([adjacency[:, d * piece:(d + 1) * piece] for d in range(n_row)])]
where the time goes in v5:
time: 129 us
  blocking collectives  49.6 us (38%)
  waiting for transfers between devices  35.2 us (27%)
  starting transfers between devices  13.7 us (11%)
  matrix products  11 us (9%)
  Pallas kernels  6.65 us (5%)
  local copies, waits for them, and re-layouts  6.51 us (5%)
  other arithmetic  6.23 us (5%)
    all_gather x1, blocking collectives, body(): all_degree = lax.all_gather(own_degree, ROW, axis=0, tiled=True)  36.8 us
    ppermute x3, waiting for transfers between devices, row_reduce_scatter(): total = total + lax.ppermute(send, 'chip', perm)  21.8 us
    psum x1, blocking collectives, body(): own_degree = lax.psum(jnp.sum(adjacency, axis=1), 'col')  12.8 us
    dot_general x1, matrix products, inner_rows(): lax.dot_general(left, right, (((1,), (1,)), ((), ())), precision=lax.Prec...  11 us
    ppermute x3, waiting for transfers between devices, col_reduce_scatter(): total = total + lax.ppermute(send, 'col', perm)  9.37 us
    pallas_call x1, Pallas kernels, column_chunks(): pl.pallas_call(_copy_block, grid=(n_chunks,), in_specs=[pl.BlockSpec((row...  6.65 us
    ppermute x3, starting transfers between devices, col_reduce_scatter(): total = total + lax.ppermute(send, 'col', perm)  5.5 us
    all_to_all x1, starting transfers between devices, body(): lax.all_to_all(chunks, ROW, split_axis=0, concat_axis=0, tiled=True)  5.17 us
  transfers between devices with their start and end apart: 8, of which 5 were waited for; matrix products, arithmetic and copies ran while one was open for 4% of the time, Pallas kernels for 0%

profile of v5, /device:TPU:0, one launch (start us, length us, event | category | flops | bytes accessed | tf_op | source)
XLA Modules:
  0.0 129.0 jit_solution(13029815919550303420)
XLA Ops:
  0.0 6.7 %shard_map.17 = f32[8,128,1024]{2,1,0:T(8,128)} custom-call(f32[128,8192]{1,0:T(8,128)} %block_ref.1), custom_call_target="tpu_custom_call" | custom-call | tf_op jit(solution)/shard_map/pallas_call | solution.py:29
  6.7 5.2 %all-to-all-start = ((f32[8,128,1024]{2,1,0:T(8,128)}), f32[8,128,1024]{2,1,0:T(8,128)}, u32[]{:S(2)}, u32[]{:S(2)}) async-start(f32[8,128,1024]{2,1,0:T(8,128)} %shard_map.17), calls=%async_computation | async-start | bytes 8388608 | tf_op jit(solution)/shard_map/all_to_all | solution.py:80
  11.8 2.5 %reduce_sum.9 = f32[128]{0:T(128)S(1)} reduce(f32[128,8192]{1,0:T(8,128)} %block_ref.1, f32[]{:T(128)} %constant.80.clone.1), dimensions={1}, to_apply=%region_0.0 | reduce | flops 1048448 | bytes 4194820 | tf_op jit(solution)/shard_map/reduce_sum | solution.py:82
  14.3 12.8 %psum.7 = f32[128]{0:T(128)S(1)} all-reduce(f32[128]{0:T(128)S(1)} %reduce_sum.9), channel_id=1, replica_groups=mesh['chip'=4,'core'=2,'col'=4] {'col'}, use_global_device_ids=true, to_apply=%region_1.0 | all-reduce | flops 128 | bytes 1024 | tf_op jit(solution)/shard_map/psum | solution.py:82
  27.1 36.8 %all-gather = f32[8,1,128]{2,1,0:T(1,128)S(1)} all-gather(f32[1,1,128]{2,1,0:T(1,128)S(1)} %bitcast.43), channel_id=1, replica_groups=mesh['chip'=4,'core'=2,'col'=4] {'chip','core'}, dimensions={0}, use_global_device_ids=true | all-gather | bytes 4608 | tf_op jit(solution)/shard_map/all_gather | solution.py:83
  63.9 0.1 dynamic_slice.36
  64.0 0.0 all-to-all-done
  64.0 11.0 %fusion.6 = f32[4,2,128,1024]{3,2,1,0:T(8,128)S(1)} fusion(f32[4,2,128,1024]{3,2,1,0:T(8,128)} %bitcast.2, f32[1024,1024,1,1]{1,0,3,2:T(8,128)} %bitcast.5), kind=kOutput, calls=%fused_computation.18 | convolution fusion | flops 6442450944 | bytes 12582912 | tf_op jit(solution)/shard_map/dot_general | solution.py:13
  75.0 0.0 copy-start
  75.0 1.9 %copy-done = f32[4,2,128,1024]{3,2,1,0:T(8,128)} copy-done((f32[4,2,128,1024]{3,2,1,0:T(8,128)}, f32[4,2,128,1024]{3,2,1,0:T(8,128)S(1)}, u32[]{:S(2)}) %copy-start) | copy-done | bytes 4194328
  76.9 1.6 %dynamic-slice_bitcast_fusion = f32[4,128,1024]{2,1,0:T(8,128)} fusion(f32[4,2,128,1024]{3,2,1,0:T(8,128)S(1)} %fusion.6, s32[]{:T(128)S(6)} %select_n.70), kind=kLoop, calls=%fused_computation.1 | loop fusion | bytes 4194308 | tf_op jit(solution)/shard_map/jit(dynamic_index_in_dim)/squeeze | solution.py:61
  78.5 0.3 collective-permute-start
  78.8 4.1 %collective-permute-done = f32[4,128,1024]{2,1,0:T(8,128)S(1)} collective-permute-done((f32[4,128,1024]{2,1,0:T(8,128)}, f32[4,128,1024]{2,1,0:T(8,128)S(1)}, u32[]{:S(2)}, u32[]{:S(2)}) %collective-permute-start) | collective-permute-done | bytes 2097184 | tf_op jit(solution)/shard_map/ppermute | solution.py:63
  82.9 2.0 %bitcast_add_fusion = f32[4,128,1024]{2,1,0:T(8,128)S(1)} fusion(f32[4,128,1024]{2,1,0:T(8,128)S(1)} %collective-permute-done, f32[4,2,128,1024]{3,2,1,0:T(8,128)} %copy-done, s32[]{:T(128)S(6)} %select_n.68), kind=kLoop, calls=%fused_computation | loop fusion | flops 524288 | bytes 6291460 | tf_op jit(solution)/shard_map/add | solution.py:63
  84.9 0.1 constant_dynamic-slice_fusion.7
  85.0 0.2 copy.17
  85.2 0.3 collective-permute-start.3
  85.5 1.0 copy.16
  86.5 0.7 collective-permute-start.2
  87.1 1.0 copy.15
  88.1 1.8 %collective-permute-start.1 = (f32[128,1024]{0,1:T(8,128)}, f32[128,1024]{0,1:T(8,128)S(1)}, u32[]{:S(2)}, u32[]{:S(2)}) collective-permute-start(f32[128,1024]{0,1:T(8,128)} %bitcast.9), channel_id=1, source_target_pairs={{0,8},{8,16},{16,24},{24,0},{1,9},{9,17},{17,25},{25,1},{2,10},{10... | collective-permute-start | bytes 1572872 | tf_op jit(solution)/shard_map/ppermute | solution.py:70
  89.9 0.2 copy.14
  90.1 9.9 %collective-permute-done.3 = f32[128,1024]{0,1:T(8,128)S(1)} collective-permute-done((f32[128,1024]{0,1:T(8,128)S(1)}, f32[128,1024]{0,1:T(8,128)S(1)}, u32[]{:S(2)}, u32[]{:S(2)}) %collective-permute-start.3) | collective-permute-done | bytes 524320 | tf_op jit(solution)/shard_map/ppermute | solution.py:70
  100.0 11.9 %collective-permute-done.2 = f32[128,1024]{0,1:T(8,128)S(1)} collective-permute-done((f32[128,1024]{0,1:T(8,128)}, f32[128,1024]{0,1:T(8,128)S(1)}, u32[]{:S(2)}, u32[]{:S(2)}) %collective-permute-start.2) | collective-permute-done | bytes 524320 | tf_op jit(solution)/shard_map/ppermute | solution.py:70
  111.9 0.0 collective-permute-done.1
  111.9 0.1 fusion.1
  112.0 0.1 copy.21
  112.1 4.4 %collective-permute-start.6 = (f32[128,256]{1,0:T(8,128)S(1)}, f32[128,256]{1,0:T(8,128)S(1)}, u32[]{:S(2)}, u32[]{:S(2)}) collective-permute-start(f32[128,256]{1,0:T(8,128)S(1)} %bitcast.39), channel_id=1, source_target_pairs={{0,3},{1,0},{2,1},{3,2},{4,7},{5,4},{6,5},{7,6},{8,11},{9,8},{10,9... | collective-permute-start | bytes 393224 | tf_op jit(solution)/shard_map/ppermute | solution.py:48
  116.5 0.1 copy.20
  116.6 0.1 collective-permute-start.5
  116.7 0.1 copy.19
  116.8 1.1 collective-permute-start.4
  117.8 0.1 copy.18
  117.9 2.5 %collective-permute-done.6 = f32[128,256]{1,0:T(8,128)S(1)} collective-permute-done((f32[128,256]{1,0:T(8,128)S(1)}, f32[128,256]{1,0:T(8,128)S(1)}, u32[]{:S(2)}, u32[]{:S(2)}) %collective-permute-start.6) | collective-permute-done | bytes 131104 | tf_op jit(solution)/shard_map/ppermute | solution.py:48
  120.5 6.9 %collective-permute-done.5 = f32[128,256]{1,0:T(8,128)S(1)} collective-permute-done((f32[128,256]{1,0:T(8,128)S(1)}, f32[128,256]{1,0:T(8,128)S(1)}, u32[]{:S(2)}, u32[]{:S(2)}) %collective-permute-start.5) | collective-permute-done | bytes 131104 | tf_op jit(solution)/shard_map/ppermute | solution.py:48
  127.3 0.0 collective-permute-done.4
  127.3 1.7 %fusion.5 = f32[128,256]{1,0:T(8,128)} fusion(f32[128,256]{1,0:T(8,128)S(1)} %collective-permute-done.6, f32[128,256]{1,0:T(8,128)S(1)} %collective-permute-done.5, f32[128,256]{1,0:T(8,128)S(1)} %collective-permute-done.4, f32[128,1,256]{2,0,1:T(8,128)S(1)} %copy.18, f32[128,8192]{1,0:T(8,128)} %block_ref.1, f32[256]{0:T(256)S(1)} %dynamic_slice.36, ...), kind=kLoop, calls=%fused_computation.9 | loop fusion | flops 262144 | bytes 787968 | tf_op jit(solution)/shard_map/div | solution.py:90
  (1 shorter events, 0.0 us)
Async XLA Ops:
  6.7 57.4 %all-to-all-start = ((f32[8,128,1024]{2,1,0:T(8,128)}), f32[8,128,1024]{2,1,0:T(8,128)}, u32[]{:S(2)}, u32[]{:S(2)}) async-start(f32[8,128,1024]{2,1,0:T(8,128)} %shard_map.17), calls=%async_computation | async-start | bytes 8388608 | tf_op jit(solution)/shard_map/all_to_all | solution.py:80
  75.0 1.9 %copy-start = (f32[4,2,128,1024]{3,2,1,0:T(8,128)}, f32[4,2,128,1024]{3,2,1,0:T(8,128)S(1)}, u32[]{:S(2)}) copy-start(f32[4,2,128,1024]{3,2,1,0:T(8,128)S(1)} %fusion.6) | copy-start | bytes 12582916
  78.5 4.4 %collective-permute-start = (f32[4,128,1024]{2,1,0:T(8,128)}, f32[4,128,1024]{2,1,0:T(8,128)S(1)}, u32[]{:S(2)}, u32[]{:S(2)}) collective-permute-start(f32[4,128,1024]{2,1,0:T(8,128)} %dynamic-slice_bitcast_fusion), channel_id=1, source_target_pairs={{0,4},{4,0},{1,5},{5,1},{2,6},{6,2},{3,7},{7,3},{8,12},{12,8},{9,1... | collective-permute-start | bytes 6291464 | tf_op jit(solution)/shard_map/ppermute | solution.py:63
  85.2 14.8 %collective-permute-start.3 = (f32[128,1024]{0,1:T(8,128)S(1)}, f32[128,1024]{0,1:T(8,128)S(1)}, u32[]{:S(2)}, u32[]{:S(2)}) collective-permute-start(f32[128,1024]{0,1:T(8,128)S(1)} %bitcast.38), channel_id=1, source_target_pairs={{0,24},{8,0},{16,8},{24,16},{1,25},{9,1},{17,9},{25,17},{2,26},{10... | collective-permute-start | bytes 1572872 | tf_op jit(solution)/shard_map/ppermute | solution.py:70
  86.5 25.4 %collective-permute-start.2 = (f32[128,1024]{0,1:T(8,128)}, f32[128,1024]{0,1:T(8,128)S(1)}, u32[]{:S(2)}, u32[]{:S(2)}) collective-permute-start(f32[128,1024]{0,1:T(8,128)} %bitcast.10), channel_id=1, source_target_pairs={{0,16},{8,24},{16,0},{24,8},{1,17},{9,25},{17,1},{25,9},{2,18},{10... | collective-permute-start | bytes 1572872 | tf_op jit(solution)/shard_map/ppermute | solution.py:70
  88.1 23.7 %collective-permute-start.1 = (f32[128,1024]{0,1:T(8,128)}, f32[128,1024]{0,1:T(8,128)S(1)}, u32[]{:S(2)}, u32[]{:S(2)}) collective-permute-start(f32[128,1024]{0,1:T(8,128)} %bitcast.9), channel_id=1, source_target_pairs={{0,8},{8,16},{16,24},{24,0},{1,9},{9,17},{17,25},{25,1},{2,10},{10... | collective-permute-start | bytes 1572872 | tf_op jit(solution)/shard_map/ppermute | solution.py:70
  112.1 8.3 %collective-permute-start.6 = (f32[128,256]{1,0:T(8,128)S(1)}, f32[128,256]{1,0:T(8,128)S(1)}, u32[]{:S(2)}, u32[]{:S(2)}) collective-permute-start(f32[128,256]{1,0:T(8,128)S(1)} %bitcast.39), channel_id=1, source_target_pairs={{0,3},{1,0},{2,1},{3,2},{4,7},{5,4},{6,5},{7,6},{8,11},{9,8},{10,9... | collective-permute-start | bytes 393224 | tf_op jit(solution)/shard_map/ppermute | solution.py:48
  116.6 10.7 %collective-permute-start.5 = (f32[128,256]{1,0:T(8,128)S(1)}, f32[128,256]{1,0:T(8,128)S(1)}, u32[]{:S(2)}, u32[]{:S(2)}) collective-permute-start(f32[128,256]{1,0:T(8,128)S(1)} %bitcast.40), channel_id=1, source_target_pairs={{0,2},{1,3},{2,0},{3,1},{4,6},{5,7},{6,4},{7,5},{8,10},{9,11},{10,... | collective-permute-start | bytes 393224 | tf_op jit(solution)/shard_map/ppermute | solution.py:48
  116.8 10.5 %collective-permute-start.4 = (f32[128,256]{1,0:T(8,128)S(1)}, f32[128,256]{1,0:T(8,128)S(1)}, u32[]{:S(2)}, u32[]{:S(2)}) collective-permute-start(f32[128,256]{1,0:T(8,128)S(1)} %bitcast.41), channel_id=1, source_target_pairs={{0,1},{1,2},{2,3},{3,0},{4,5},{5,6},{6,7},{7,4},{8,9},{9,10},{10,1... | collective-permute-start | bytes 393224 | tf_op jit(solution)/shard_map/ppermute | solution.py:48

commit v6 on v5

--- a/solution.py
+++ b/solution.py
@@ -49,19 +49,20 @@
     return total
 
 
-def row_reduce_scatter(pieces):
+def row_reduce_scatter(pieces, right):
     n_chip = lax.axis_size("chip")
     n_core = lax.axis_size("core")
     me = lax.axis_index("core")
-    rows, depth = pieces.shape
+    rows = pieces.shape[0]
+    width = right.shape[0]
     strip = rows // (n_chip * n_core)
-    paired = inner_rows(pieces, pieces).reshape(n_chip, n_core, strip, rows)
+    paired = inner_rows(pieces, right).reshape(n_chip, n_core, strip, width)
     on_chip = lax.dynamic_index_in_dim(paired, me, 1, keepdims=False)
     for s in range(1, n_core):
         send = lax.dynamic_index_in_dim(paired, (me + s) % n_core, 1, keepdims=False)
         perm = [(i, (i + s) % n_core) for i in range(n_core)]
         on_chip = on_chip + lax.ppermute(send, "core", perm)
-    blocks = on_chip.reshape(n_chip, strip, rows)
+    blocks = on_chip
     mine = lax.axis_index("chip")
     total = lax.dynamic_index_in_dim(blocks, mine, 0, keepdims=False)
     for s in range(1, n_chip):
@@ -74,7 +75,8 @@
 def body(adjacency):
     strip_rows, cols = adjacency.shape
     n_row = lax.axis_size(ROW)
-    window = strip_rows * n_row // lax.axis_size("col")
+    n_col = lax.axis_size("col")
+    window = strip_rows * n_row // n_col
     piece = cols // n_row
     chunks = column_chunks(adjacency, n_row)
     pieces = lax.all_to_all(chunks, ROW, split_axis=0, concat_axis=0, tiled=True)
@@ -84,7 +86,14 @@
     col_degree = lax.dynamic_slice_in_dim(all_degree, lax.axis_index("col") * window, window, 0)
     pieces, own_degree, col_degree = lax.optimization_barrier((pieces, own_degree, col_degree))
     pieces = pieces.reshape(n_row * strip_rows, piece)
-    shared_sum = col_reduce_scatter(row_reduce_scatter(pieces))
+    groups = 2 if window % 256 == 0 else 1
+    sub = window // groups
+    by_group = pieces.reshape(n_col, groups, sub, piece)
+    outs = []
+    for g in range(groups):
+        right = by_group[:, g].reshape(n_col * sub, piece)
+        outs.append(col_reduce_scatter(row_reduce_scatter(pieces, right)))
+    shared_sum = jnp.stack(outs, axis=1).reshape(strip_rows, window)
     linked = adjacency[:, :window]
     smaller = jnp.minimum(own_degree[:, None], col_degree[None, :])
     return (shared_sum + linked) / (smaller + 1.0 - linked)

time: 129 us -> 123 us (0.953)
  waiting for transfers between devices: 35.2 us -> 10.4 us
  starting transfers between devices: 13.7 us -> 28.1 us
  local copies, waits for them, and re-layouts: 6.51 us -> 11 us
    ppermute x3 -> x6, waiting for transfers between devices: 21.8 us -> 5.97 us  [row_reduce_scatter(): total = total + lax.ppermute(send, 'chip', perm)]
    ppermute x3 -> x6, starting transfers between devices: 5.5 us -> 15.8 us  [col_reduce_scatter(): total = total + lax.ppermute(send, 'col', perm)]
    ppermute x3 -> x6, waiting for transfers between devices: 9.37 us -> 3.2 us  [col_reduce_scatter(): total = total + lax.ppermute(send, 'col', perm)]
    ppermute x3 -> x6, starting transfers between devices: 2.71 us -> 6.58 us  [row_reduce_scatter(): total = total + lax.ppermute(send, 'chip', perm)]
    ppermute x1 -> x2, waiting for transfers between devices: 4.05 us -> 1.23 us  [row_reduce_scatter(): on_chip = on_chip + lax.ppermute(send, 'core', perm)]
    slice x0 -> x3, local copies, waits for them, and re-layouts: none -> 2.75 us  [the longest x1 2.75 us: body(): right = by_group[:, g].reshape(n_col * sub, piece)]
    div x1, other arithmetic: 1.66 us -> 0.11 us  [body(): return (shared_sum + linked) / (smaller + 1.0 - linked)]
    dynamic_slice x3 -> x6, local copies, waits for them, and re-layouts: 2.18 us -> 3.59 us  [row_reduce_scatter(): lax.dynamic_index_in_dim(blocks, (mine + s) % n_chip, 0, keepdims=False)]
  transfers between devices with their start and end apart: 8 -> 15, of which waited for: 5 -> 7; matrix products, arithmetic and copies ran while one was open for 4% -> 13% of each run, Pallas kernels for 0% -> 0%
where the time goes in v6:
time: 123 us
  blocking collectives  49.6 us (40%)
  starting transfers between devices  28.1 us (23%)
  local copies, waits for them, and re-layouts  11 us (9%)
  matrix products  11 us (9%)
  waiting for transfers between devices  10.4 us (8%)
  Pallas kernels  6.66 us (5%)
  other arithmetic  5.76 us (5%)
    all_gather x1, blocking collectives, body(): all_degree = lax.all_gather(own_degree, ROW, axis=0, tiled=True)  36.8 us
    ppermute x6, starting transfers between devices, col_reduce_scatter(): total = total + lax.ppermute(send, 'col', perm)  15.8 us
    psum x1, blocking collectives, body(): own_degree = lax.psum(jnp.sum(adjacency, axis=1), 'col')  12.8 us
    dot_general x2, matrix products, inner_rows(): lax.dot_general(left, right, (((1,), (1,)), ((), ())), precision=lax.Prec...  11 us
    pallas_call x1, Pallas kernels, column_chunks(): pl.pallas_call(_copy_block, grid=(n_chunks,), in_specs=[pl.BlockSpec((row...  6.66 us
    ppermute x6, starting transfers between devices, row_reduce_scatter(): total = total + lax.ppermute(send, 'chip', perm)  6.58 us
    ppermute x6, waiting for transfers between devices, row_reduce_scatter(): total = total + lax.ppermute(send, 'chip', perm)  5.97 us
    all_to_all x1, starting transfers between devices, body(): lax.all_to_all(chunks, ROW, split_axis=0, concat_axis=0, tiled=True)  5.17 us
  transfers between devices with their start and end apart: 15, of which 7 were waited for; matrix products, arithmetic and copies ran while one was open for 13% of the time, Pallas kernels for 0%

profile of v6, /device:TPU:0, one launch (start us, length us, event | category | flops | bytes accessed | tf_op | source)
XLA Modules:
  0.0 122.8 jit_solution(13756894448065611046)
XLA Ops:
  0.0 6.7 %shard_map.17 = f32[8,128,1024]{2,1,0:T(8,128)} custom-call(f32[128,8192]{1,0:T(8,128)} %block_ref.1), custom_call_target="tpu_custom_call" | custom-call | tf_op jit(solution)/shard_map/pallas_call | solution.py:29
  6.7 5.2 %all-to-all-start = ((f32[8,128,1024]{2,1,0:T(8,128)}), f32[8,128,1024]{2,1,0:T(8,128)}, u32[]{:S(2)}, u32[]{:S(2)}) async-start(f32[8,128,1024]{2,1,0:T(8,128)} %shard_map.17), calls=%async_computation | async-start | bytes 8388608 | tf_op jit(solution)/shard_map/all_to_all | solution.py:82
  11.8 2.5 %reduce_sum.9 = f32[128]{0:T(128)S(1)} reduce(f32[128,8192]{1,0:T(8,128)} %block_ref.1, f32[]{:T(128)} %constant.114.clone.1), dimensions={1}, to_apply=%region_0.0 | reduce | flops 1048448 | bytes 4194820 | tf_op jit(solution)/shard_map/reduce_sum | solution.py:84
  14.3 12.8 %psum.7 = f32[128]{0:T(128)S(1)} all-reduce(f32[128]{0:T(128)S(1)} %reduce_sum.9), channel_id=1, replica_groups=mesh['chip'=4,'core'=2,'col'=4] {'col'}, use_global_device_ids=true, to_apply=%region_1.0 | all-reduce | flops 128 | bytes 1024 | tf_op jit(solution)/shard_map/psum | solution.py:84
  27.2 36.8 %all-gather = f32[8,1,128]{2,1,0:T(1,128)S(1)} all-gather(f32[1,1,128]{2,1,0:T(1,128)S(1)} %bitcast.89), channel_id=1, replica_groups=mesh['chip'=4,'core'=2,'col'=4] {'chip','core'}, dimensions={0}, use_global_device_ids=true | all-gather | bytes 4608 | tf_op jit(solution)/shard_map/all_gather | solution.py:85
  63.9 0.1 dynamic_slice.66
  64.0 0.0 all-to-all-done
  64.0 2.7 %fusion.11 = (f32[4,1,128,1024]{3,2,1,0:T(8,128)S(1)}, f32[4,1,128,1024]{3,2,1,0:T(8,128)S(1)}) fusion(f32[4,2,128,1024]{3,2,1,0:T(8,128)} %bitcast.2), kind=kLoop, calls=%fused_computation.37 | loop fusion | bytes 8388608 | tf_op jit(solution)/shard_map/slice | solution.py:94
  66.8 5.5 %fusion.12 = f32[4,2,128,512]{3,2,1,0:T(8,128)S(1)} fusion(f32[4,2,128,1024]{3,2,1,0:T(8,128)} %bitcast.2, f32[512,1024,1,1]{1,0,3,2:T(8,128)S(1)} %bitcast.76), kind=kOutput, calls=%fused_computation.38 | convolution fusion | flops 3221225472 | bytes 8388608 | tf_op jit(solution)/shard_map/dot_general | solution.py:13
  72.3 0.1 dynamic-slice_bitcast_fusion.1
  72.4 0.4 collective-permute-start
  72.8 5.5 %fusion.13 = f32[4,2,128,512]{3,2,1,0:T(8,128)S(1)} fusion(f32[4,2,128,1024]{3,2,1,0:T(8,128)} %bitcast.2, f32[512,1024,1,1]{1,0,3,2:T(8,128)S(1)} %bitcast.75), kind=kOutput, calls=%fused_computation.39 | convolution fusion | flops 3221225472 | bytes 8388608 | tf_op jit(solution)/shard_map/dot_general | solution.py:13
  78.3 1.3 %copy-done = f32[4,2,128,512]{3,2,1,0:T(8,128)} copy-done((f32[4,2,128,512]{3,2,1,0:T(8,128)}, f32[4,2,128,512]{3,2,1,0:T(8,128)S(1)}, u32[]{:S(2)}) %copy-start) | copy-done | bytes 2097176
  79.6 1.1 dynamic-slice_bitcast_fusion
  80.7 0.2 collective-permute-start.7
  80.8 0.0 collective-permute-done
  80.9 1.6 %bitcast_add_fusion.1 = f32[4,128,512]{2,1,0:T(8,128)S(1)} fusion(f32[4,128,512]{2,1,0:T(8,128)} %collective-permute-done, f32[4,2,128,512]{3,2,1,0:T(8,128)S(1)} %fusion.12, s32[]{:T(128)S(6)} %select_n.92), kind=kLoop, calls=%fused_computation.1 | loop fusion | flops 262144 | bytes 3145732 | tf_op jit(solution)/shard_map/add | solution.py:64
  82.4 1.2 %collective-permute-done.7 = f32[4,128,512]{2,1,0:T(8,128)} collective-permute-done((f32[4,128,512]{2,1,0:T(8,128)}, f32[4,128,512]{2,1,0:T(8,128)}, u32[]{:S(2)}, u32[]{:S(2)}) %collective-permute-start.7) | collective-permute-done | bytes 1048608 | tf_op jit(solution)/shard_map/ppermute | solution.py:64
  83.7 1.4 %bitcast_add_fusion = f32[4,128,512]{2,1,0:T(8,128)S(1)} fusion(f32[4,128,512]{2,1,0:T(8,128)} %collective-permute-done.7, f32[4,2,128,512]{3,2,1,0:T(8,128)S(1)} %copy-done.1, s32[]{:T(128)S(6)} %select_n.92), kind=kLoop, calls=%fused_computation | loop fusion | flops 262144 | bytes 3145732 | tf_op jit(solution)/shard_map/add | solution.py:64
  85.1 0.0 slice-start
  85.1 0.2 constant_dynamic-slice_fusion.7
  85.3 0.1 copy.43
  85.4 0.1 collective-permute-start.1
  85.5 0.1 copy.44
  85.6 0.8 collective-permute-start.2
  86.5 0.8 copy.45
  87.3 2.8 %collective-permute-start.3 = (f32[128,512]{0,1:T(8,128)}, f32[128,512]{0,1:T(8,128)S(1)}, u32[]{:S(2)}, u32[]{:S(2)}) collective-permute-start(f32[128,512]{0,1:T(8,128)} %bitcast.11), channel_id=1, source_target_pairs={{0,24},{8,0},{16,8},{24,16},{1,25},{9,1},{17,9},{25,17},{2,26},{10... | collective-permute-start | bytes 786440 | tf_op jit(solution)/shard_map/ppermute | solution.py:71
  90.1 0.1 copy.63
  90.2 0.1 copy.42
  90.3 0.8 copy.53
  91.2 0.0 collective-permute-start.10
  91.2 0.8 copy.51
  92.0 2.0 %collective-permute-start.8 = (f32[128,512]{0,1:T(8,128)}, f32[128,512]{0,1:T(8,128)S(1)}, u32[]{:S(2)}, u32[]{:S(2)}) collective-permute-start(f32[128,512]{0,1:T(8,128)} %bitcast.24), channel_id=1, source_target_pairs={{0,8},{8,16},{16,24},{24,0},{1,9},{9,17},{17,25},{25,1},{2,10},{10... | collective-permute-start | bytes 786440 | tf_op jit(solution)/shard_map/ppermute | solution.py:71
  94.0 0.8 copy.52
  94.9 0.1 copy.50
  95.0 0.6 collective-permute-done.1
  95.6 0.9 collective-permute-start.9
  96.5 4.0 %collective-permute-done.2 = f32[128,512]{0,1:T(8,128)S(1)} collective-permute-done((f32[128,512]{0,1:T(8,128)S(1)}, f32[128,512]{0,1:T(8,128)S(1)}, u32[]{:S(2)}, u32[]{:S(2)}) %collective-permute-start.2) | collective-permute-done | bytes 262176 | tf_op jit(solution)/shard_map/ppermute | solution.py:71
  100.5 0.1 copy.47
  100.6 2.4 %collective-permute-start.4 = (f32[128,128]{1,0:T(8,128)S(1)}, f32[128,128]{1,0:T(8,128)S(1)}, u32[]{:S(2)}, u32[]{:S(2)}) collective-permute-start(f32[128,128]{1,0:T(8,128)S(1)} %bitcast.83), channel_id=1, source_target_pairs={{0,1},{1,2},{2,3},{3,0},{4,5},{5,6},{6,7},{7,4},{8,9},{9,10},{10,1... | collective-permute-start | bytes 196616 | tf_op jit(solution)/shard_map/ppermute | solution.py:48
  103.0 0.1 copy.48
  103.1 2.7 %collective-permute-start.5 = (f32[128,128]{1,0:T(8,128)S(1)}, f32[128,128]{1,0:T(8,128)S(1)}, u32[]{:S(2)}, u32[]{:S(2)}) collective-permute-start(f32[128,128]{1,0:T(8,128)S(1)} %bitcast.82), channel_id=1, source_target_pairs={{0,2},{1,3},{2,0},{3,1},{4,6},{5,7},{6,4},{7,5},{8,10},{9,11},{10,... | collective-permute-start | bytes 196616 | tf_op jit(solution)/shard_map/ppermute | solution.py:48
  105.8 0.1 copy.49
  105.8 0.1 copy.46
  106.0 0.0 collective-permute-done.10
  106.0 4.3 %collective-permute-start.6 = (f32[128,128]{1,0:T(8,128)S(1)}, f32[128,128]{1,0:T(8,128)S(1)}, u32[]{:S(2)}, u32[]{:S(2)}) collective-permute-start(f32[128,128]{1,0:T(8,128)S(1)} %bitcast.84), channel_id=1, source_target_pairs={{0,3},{1,0},{2,1},{3,2},{4,7},{5,4},{6,5},{7,6},{8,11},{9,8},{10,9... | collective-permute-start | bytes 196616 | tf_op jit(solution)/shard_map/ppermute | solution.py:48
  110.3 1.3 %collective-permute-done.8 = f32[128,512]{0,1:T(8,128)S(1)} collective-permute-done((f32[128,512]{0,1:T(8,128)}, f32[128,512]{0,1:T(8,128)S(1)}, u32[]{:S(2)}, u32[]{:S(2)}) %collective-permute-start.8) | collective-permute-done | bytes 262176 | tf_op jit(solution)/shard_map/ppermute | solution.py:71
  111.7 0.0 collective-permute-done.9
  111.8 0.1 copy.55
  111.9 2.4 %collective-permute-start.11 = (f32[128,128]{1,0:T(8,128)S(1)}, f32[128,128]{1,0:T(8,128)S(1)}, u32[]{:S(2)}, u32[]{:S(2)}) collective-permute-start(f32[128,128]{1,0:T(8,128)S(1)} %bitcast.85), channel_id=1, source_target_pairs={{0,1},{1,2},{2,3},{3,0},{4,5},{5,6},{6,7},{7,4},{8,9},{9,10},{10,1... | collective-permute-start | bytes 196616 | tf_op jit(solution)/shard_map/ppermute | solution.py:48
  114.2 0.1 copy.56
  114.3 2.7 %collective-permute-start.12 = (f32[128,128]{1,0:T(8,128)S(1)}, f32[128,128]{1,0:T(8,128)S(1)}, u32[]{:S(2)}, u32[]{:S(2)}) collective-permute-start(f32[128,128]{1,0:T(8,128)S(1)} %bitcast.86), channel_id=1, source_target_pairs={{0,2},{1,3},{2,0},{3,1},{4,6},{5,7},{6,4},{7,5},{8,10},{9,11},{10,... | collective-permute-start | bytes 196616 | tf_op jit(solution)/shard_map/ppermute | solution.py:48
  117.0 0.1 copy.57
  117.1 0.1 copy.54
  117.2 0.0 collective-permute-done.4
  117.2 1.4 %collective-permute-start.13 = (f32[128,128]{1,0:T(8,128)S(1)}, f32[128,128]{1,0:T(8,128)S(1)}, u32[]{:S(2)}, u32[]{:S(2)}) collective-permute-start(f32[128,128]{1,0:T(8,128)S(1)} %bitcast.87), channel_id=1, source_target_pairs={{0,3},{1,0},{2,1},{3,2},{4,7},{5,4},{6,5},{7,6},{8,11},{9,8},{10,9... | collective-permute-start | bytes 196616 | tf_op jit(solution)/shard_map/ppermute | solution.py:48
  118.6 0.0 collective-permute-done.5
  118.6 0.0 collective-permute-done.6
  118.6 0.5 collective-permute-done.11
  119.1 2.4 %collective-permute-done.12 = f32[128,128]{1,0:T(8,128)S(1)} collective-permute-done((f32[128,128]{1,0:T(8,128)S(1)}, f32[128,128]{1,0:T(8,128)S(1)}, u32[]{:S(2)}, u32[]{:S(2)}) %collective-permute-start.12) | collective-permute-done | bytes 65568 | tf_op jit(solution)/shard_map/ppermute | solution.py:48
  121.5 0.3 collective-permute-done.13
  121.8 0.1 copy.58
  122.0 0.1 fusion.4
  122.1 0.8 copy.60
  (12 shorter events, 0.2 us)
Async XLA Ops:
  6.7 57.4 %all-to-all-start = ((f32[8,128,1024]{2,1,0:T(8,128)}), f32[8,128,1024]{2,1,0:T(8,128)}, u32[]{:S(2)}, u32[]{:S(2)}) async-start(f32[8,128,1024]{2,1,0:T(8,128)} %shard_map.17), calls=%async_computation | async-start | bytes 8388608 | tf_op jit(solution)/shard_map/all_to_all | solution.py:82
  72.4 8.5 %collective-permute-start = (f32[4,128,512]{2,1,0:T(8,128)S(1)}, f32[4,128,512]{2,1,0:T(8,128)}, u32[]{:S(2)}, u32[]{:S(2)}) collective-permute-start(f32[4,128,512]{2,1,0:T(8,128)S(1)} %dynamic-slice_bitcast_fusion.1), channel_id=1, source_target_pairs={{0,4},{4,0},{1,5},{5,1},{2,6},{6,2},{3,7},{7,3},{8,12},{12,8},{9,1... | collective-permute-start | bytes 3145736 | tf_op jit(solution)/shard_map/ppermute | solution.py:64
  78.3 1.3 %copy-start = (f32[4,2,128,512]{3,2,1,0:T(8,128)}, f32[4,2,128,512]{3,2,1,0:T(8,128)S(1)}, u32[]{:S(2)}) copy-start(f32[4,2,128,512]{3,2,1,0:T(8,128)S(1)} %fusion.13) | copy-start | bytes 6291460
  80.7 3.0 %collective-permute-start.7 = (f32[4,128,512]{2,1,0:T(8,128)}, f32[4,128,512]{2,1,0:T(8,128)}, u32[]{:S(2)}, u32[]{:S(2)}) collective-permute-start(f32[4,128,512]{2,1,0:T(8,128)} %dynamic-slice_bitcast_fusion), channel_id=1, source_target_pairs={{0,4},{4,0},{1,5},{5,1},{2,6},{6,2},{3,7},{7,3},{8,12},{12,8},{9,1... | collective-permute-start | bytes 3145736 | tf_op jit(solution)/shard_map/ppermute | solution.py:64
  80.8 2.8 %copy-start.1 = (f32[4,2,128,512]{3,2,1,0:T(8,128)S(1)}, f32[4,2,128,512]{3,2,1,0:T(8,128)}, u32[]{:S(2)}) copy-start(f32[4,2,128,512]{3,2,1,0:T(8,128)} %copy-done) | copy-start | bytes 6291460
  85.1 5.0 %slice-start = ((f32[128,8192]{1,0:T(8,128)}), f32[128,256]{1,0:T(8,128)S(1)}, s32[]{:S(2)}) async-start(f32[128,8192]{1,0:T(8,128)} %block_ref.1), calls=%async_computation.1 | async-start | bytes 262144 | tf_op jit(solution)/shard_map/slice | solution.py:97
  85.4 10.1 %collective-permute-start.1 = (f32[128,512]{0,1:T(8,128)S(1)}, f32[128,512]{0,1:T(8,128)S(1)}, u32[]{:S(2)}, u32[]{:S(2)}) collective-permute-start(f32[128,512]{0,1:T(8,128)S(1)} %bitcast.80), channel_id=1, source_target_pairs={{0,8},{8,16},{16,24},{24,0},{1,9},{9,17},{17,25},{25,1},{2,10},{10... | collective-permute-start | bytes 786440 | tf_op jit(solution)/shard_map/ppermute | solution.py:71
  85.6 14.8 %collective-permute-start.2 = (f32[128,512]{0,1:T(8,128)S(1)}, f32[128,512]{0,1:T(8,128)S(1)}, u32[]{:S(2)}, u32[]{:S(2)}) collective-permute-start(f32[128,512]{0,1:T(8,128)S(1)} %bitcast.79), channel_id=1, source_target_pairs={{0,16},{8,24},{16,0},{24,8},{1,17},{9,25},{17,1},{25,9},{2,18},{10... | collective-permute-start | bytes 786440 | tf_op jit(solution)/shard_map/ppermute | solution.py:71
  87.3 13.2 %collective-permute-start.3 = (f32[128,512]{0,1:T(8,128)}, f32[128,512]{0,1:T(8,128)S(1)}, u32[]{:S(2)}, u32[]{:S(2)}) collective-permute-start(f32[128,512]{0,1:T(8,128)} %bitcast.11), channel_id=1, source_target_pairs={{0,24},{8,0},{16,8},{24,16},{1,25},{9,1},{17,9},{25,17},{2,26},{10... | collective-permute-start | bytes 786440 | tf_op jit(solution)/shard_map/ppermute | solution.py:71
  91.2 14.8 %collective-permute-start.10 = (f32[128,512]{0,1:T(8,128)}, f32[128,512]{0,1:T(8,128)S(1)}, u32[]{:S(2)}, u32[]{:S(2)}) collective-permute-start(f32[128,512]{0,1:T(8,128)} %bitcast.26), channel_id=1, source_target_pairs={{0,24},{8,0},{16,8},{24,16},{1,25},{9,1},{17,9},{25,17},{2,26},{10... | collective-permute-start | bytes 786440 | tf_op jit(solution)/shard_map/ppermute | solution.py:71
  92.0 19.7 %collective-permute-start.8 = (f32[128,512]{0,1:T(8,128)}, f32[128,512]{0,1:T(8,128)S(1)}, u32[]{:S(2)}, u32[]{:S(2)}) collective-permute-start(f32[128,512]{0,1:T(8,128)} %bitcast.24), channel_id=1, source_target_pairs={{0,8},{8,16},{16,24},{24,0},{1,9},{9,17},{17,25},{25,1},{2,10},{10... | collective-permute-start | bytes 786440 | tf_op jit(solution)/shard_map/ppermute | solution.py:71
  95.6 16.1 %collective-permute-start.9 = (f32[128,512]{0,1:T(8,128)}, f32[128,512]{0,1:T(8,128)S(1)}, u32[]{:S(2)}, u32[]{:S(2)}) collective-permute-start(f32[128,512]{0,1:T(8,128)} %bitcast.81), channel_id=1, source_target_pairs={{0,16},{8,24},{16,0},{24,8},{1,17},{9,25},{17,1},{25,9},{2,18},{10... | collective-permute-start | bytes 786440 | tf_op jit(solution)/shard_map/ppermute | solution.py:71
  100.6 16.5 %collective-permute-start.4 = (f32[128,128]{1,0:T(8,128)S(1)}, f32[128,128]{1,0:T(8,128)S(1)}, u32[]{:S(2)}, u32[]{:S(2)}) collective-permute-start(f32[128,128]{1,0:T(8,128)S(1)} %bitcast.83), channel_id=1, source_target_pairs={{0,1},{1,2},{2,3},{3,0},{4,5},{5,6},{6,7},{7,4},{8,9},{9,10},{10,1... | collective-permute-start | bytes 196616 | tf_op jit(solution)/shard_map/ppermute | solution.py:48
  103.1 15.5 %collective-permute-start.5 = (f32[128,128]{1,0:T(8,128)S(1)}, f32[128,128]{1,0:T(8,128)S(1)}, u32[]{:S(2)}, u32[]{:S(2)}) collective-permute-start(f32[128,128]{1,0:T(8,128)S(1)} %bitcast.82), channel_id=1, source_target_pairs={{0,2},{1,3},{2,0},{3,1},{4,6},{5,7},{6,4},{7,5},{8,10},{9,11},{10,... | collective-permute-start | bytes 196616 | tf_op jit(solution)/shard_map/ppermute | solution.py:48
  106.0 12.6 %collective-permute-start.6 = (f32[128,128]{1,0:T(8,128)S(1)}, f32[128,128]{1,0:T(8,128)S(1)}, u32[]{:S(2)}, u32[]{:S(2)}) collective-permute-start(f32[128,128]{1,0:T(8,128)S(1)} %bitcast.84), channel_id=1, source_target_pairs={{0,3},{1,0},{2,1},{3,2},{4,7},{5,4},{6,5},{7,6},{8,11},{9,8},{10,9... | collective-permute-start | bytes 196616 | tf_op jit(solution)/shard_map/ppermute | solution.py:48
  111.9 7.3 %collective-permute-start.11 = (f32[128,128]{1,0:T(8,128)S(1)}, f32[128,128]{1,0:T(8,128)S(1)}, u32[]{:S(2)}, u32[]{:S(2)}) collective-permute-start(f32[128,128]{1,0:T(8,128)S(1)} %bitcast.85), channel_id=1, source_target_pairs={{0,1},{1,2},{2,3},{3,0},{4,5},{5,6},{6,7},{7,4},{8,9},{9,10},{10,1... | collective-permute-start | bytes 196616 | tf_op jit(solution)/shard_map/ppermute | solution.py:48
  114.3 7.2 %collective-permute-start.12 = (f32[128,128]{1,0:T(8,128)S(1)}, f32[128,128]{1,0:T(8,128)S(1)}, u32[]{:S(2)}, u32[]{:S(2)}) collective-permute-start(f32[128,128]{1,0:T(8,128)S(1)} %bitcast.86), channel_id=1, source_target_pairs={{0,2},{1,3},{2,0},{3,1},{4,6},{5,7},{6,4},{7,5},{8,10},{9,11},{10,... | collective-permute-start | bytes 196616 | tf_op jit(solution)/shard_map/ppermute | solution.py:48
  117.2 4.6 %collective-permute-start.13 = (f32[128,128]{1,0:T(8,128)S(1)}, f32[128,128]{1,0:T(8,128)S(1)}, u32[]{:S(2)}, u32[]{:S(2)}) collective-permute-start(f32[128,128]{1,0:T(8,128)S(1)} %bitcast.87), channel_id=1, source_target_pairs={{0,3},{1,0},{2,1},{3,2},{4,7},{5,4},{6,5},{7,6},{8,11},{9,8},{10,9... | collective-permute-start | bytes 196616 | tf_op jit(solution)/shard_map/ppermute | solution.py:48

commit v7 on v6

--- a/solution.py
+++ b/solution.py
@@ -19,18 +19,21 @@
     )
 
 
-def _copy_block(block_ref, out_ref):
-    out_ref[0] = block_ref[...]
+def _copy_blocks(block_ref, out_ref):
+    per_step, _, width = out_ref.shape
+    for t in range(per_step):
+        out_ref[t] = block_ref[:, t * width : (t + 1) * width]
 
 
 def column_chunks(adjacency, n_chunks):
     rows, cols = adjacency.shape
     piece = cols // n_chunks
+    per_step = 4 if n_chunks % 4 == 0 else 1
     return pl.pallas_call(
-        _copy_block,
-        grid=(n_chunks,),
-        in_specs=[pl.BlockSpec((rows, piece), lambda d: (0, d))],
-        out_specs=pl.BlockSpec((1, rows, piece), lambda d: (d, 0, 0)),
+        _copy_blocks,
+        grid=(n_chunks // per_step,),
+        in_specs=[pl.BlockSpec((rows, piece * per_step), lambda d: (0, d))],
+        out_specs=pl.BlockSpec((per_step, rows, piece), lambda d: (d, 0, 0)),
         out_shape=jax.ShapeDtypeStruct((n_chunks, rows, piece), adjacency.dtype),
     )(adjacency)
 

time: 123 us -> 120 us (0.976)
  Pallas kernels: 6.66 us -> 3.72 us
    pallas_call x1, Pallas kernels: 6.66 us -> 3.72 us  [column_chunks(): pl.pallas_call(_copy_blocks, grid=(n_chunks // per_step,), in_specs=[pl.B...]
where the time goes in v7:
time: 120 us
  blocking collectives  49.6 us (41%)
  starting transfers between devices  28.1 us (23%)
  local copies, waits for them, and re-layouts  11 us (9%)
  matrix products  11 us (9%)
  waiting for transfers between devices  10.4 us (9%)
  other arithmetic  5.76 us (5%)
  Pallas kernels  3.72 us (3%)
    all_gather x1, blocking collectives, body(): all_degree = lax.all_gather(own_degree, ROW, axis=0, tiled=True)  36.8 us
    ppermute x6, starting transfers between devices, col_reduce_scatter(): total = total + lax.ppermute(send, 'col', perm)  15.8 us
    psum x1, blocking collectives, body(): own_degree = lax.psum(jnp.sum(adjacency, axis=1), 'col')  12.8 us
    dot_general x2, matrix products, inner_rows(): lax.dot_general(left, right, (((1,), (1,)), ((), ())), precision=lax.Prec...  11 us
    ppermute x6, starting transfers between devices, row_reduce_scatter(): total = total + lax.ppermute(send, 'chip', perm)  6.57 us
    ppermute x6, waiting for transfers between devices, row_reduce_scatter(): total = total + lax.ppermute(send, 'chip', perm)  5.98 us
    all_to_all x1, starting transfers between devices, body(): lax.all_to_all(chunks, ROW, split_axis=0, concat_axis=0, tiled=True)  5.17 us
    pallas_call x1, Pallas kernels, column_chunks(): pl.pallas_call(_copy_blocks, grid=(n_chunks // per_step,), in_specs=[pl.B...  3.72 us
  transfers between devices with their start and end apart: 15, of which 7 were waited for; matrix products, arithmetic and copies ran while one was open for 13% of the time, Pallas kernels for 0%

profile of v7, /device:TPU:0, one launch (start us, length us, event | category | flops | bytes accessed | tf_op | source)
XLA Modules:
  0.0 119.9 jit_solution(11932201740484370687)
XLA Ops:
  0.0 3.7 %shard_map.17 = f32[8,128,1024]{2,1,0:T(8,128)} custom-call(f32[128,8192]{1,0:T(8,128)} %block_ref.1), custom_call_target="tpu_custom_call" | custom-call | tf_op jit(solution)/shard_map/pallas_call | solution.py:32
  3.7 5.2 %all-to-all-start = ((f32[8,128,1024]{2,1,0:T(8,128)}), f32[8,128,1024]{2,1,0:T(8,128)}, u32[]{:S(2)}, u32[]{:S(2)}) async-start(f32[8,128,1024]{2,1,0:T(8,128)} %shard_map.17), calls=%async_computation | async-start | bytes 8388608 | tf_op jit(solution)/shard_map/all_to_all | solution.py:85
  8.9 2.5 %reduce_sum.9 = f32[128]{0:T(128)S(1)} reduce(f32[128,8192]{1,0:T(8,128)} %block_ref.1, f32[]{:T(128)} %constant.114.clone.1), dimensions={1}, to_apply=%region_0.0 | reduce | flops 1048448 | bytes 4194820 | tf_op jit(solution)/shard_map/reduce_sum | solution.py:87
  11.4 12.8 %psum.7 = f32[128]{0:T(128)S(1)} all-reduce(f32[128]{0:T(128)S(1)} %reduce_sum.9), channel_id=1, replica_groups=mesh['chip'=4,'core'=2,'col'=4] {'col'}, use_global_device_ids=true, to_apply=%region_1.0 | all-reduce | flops 128 | bytes 1024 | tf_op jit(solution)/shard_map/psum | solution.py:87
  24.2 36.8 %all-gather = f32[8,1,128]{2,1,0:T(1,128)S(1)} all-gather(f32[1,1,128]{2,1,0:T(1,128)S(1)} %bitcast.89), channel_id=1, replica_groups=mesh['chip'=4,'core'=2,'col'=4] {'chip','core'}, dimensions={0}, use_global_device_ids=true | all-gather | bytes 4608 | tf_op jit(solution)/shard_map/all_gather | solution.py:88
  61.0 0.1 dynamic_slice.66
  61.1 0.0 all-to-all-done
  61.1 2.7 %fusion.11 = (f32[4,1,128,1024]{3,2,1,0:T(8,128)S(1)}, f32[4,1,128,1024]{3,2,1,0:T(8,128)S(1)}) fusion(f32[4,2,128,1024]{3,2,1,0:T(8,128)} %bitcast.2), kind=kLoop, calls=%fused_computation.37 | loop fusion | bytes 8388608 | tf_op jit(solution)/shard_map/slice | solution.py:97
  63.8 5.5 %fusion.12 = f32[4,2,128,512]{3,2,1,0:T(8,128)S(1)} fusion(f32[4,2,128,1024]{3,2,1,0:T(8,128)} %bitcast.2, f32[512,1024,1,1]{1,0,3,2:T(8,128)S(1)} %bitcast.76), kind=kOutput, calls=%fused_computation.38 | convolution fusion | flops 3221225472 | bytes 8388608 | tf_op jit(solution)/shard_map/dot_general | solution.py:13
  69.3 0.1 dynamic-slice_bitcast_fusion.1
  69.4 0.4 collective-permute-start
  69.8 5.5 %fusion.13 = f32[4,2,128,512]{3,2,1,0:T(8,128)S(1)} fusion(f32[4,2,128,1024]{3,2,1,0:T(8,128)} %bitcast.2, f32[512,1024,1,1]{1,0,3,2:T(8,128)S(1)} %bitcast.75), kind=kOutput, calls=%fused_computation.39 | convolution fusion | flops 3221225472 | bytes 8388608 | tf_op jit(solution)/shard_map/dot_general | solution.py:13
  75.3 1.3 %copy-done = f32[4,2,128,512]{3,2,1,0:T(8,128)} copy-done((f32[4,2,128,512]{3,2,1,0:T(8,128)}, f32[4,2,128,512]{3,2,1,0:T(8,128)S(1)}, u32[]{:S(2)}) %copy-start) | copy-done | bytes 2097176
  76.6 1.1 dynamic-slice_bitcast_fusion
  77.7 0.2 collective-permute-start.7
  77.9 0.0 collective-permute-done
  77.9 1.6 %bitcast_add_fusion.1 = f32[4,128,512]{2,1,0:T(8,128)S(1)} fusion(f32[4,128,512]{2,1,0:T(8,128)} %collective-permute-done, f32[4,2,128,512]{3,2,1,0:T(8,128)S(1)} %fusion.12, s32[]{:T(128)S(6)} %select_n.92), kind=kLoop, calls=%fused_computation.1 | loop fusion | flops 262144 | bytes 3145732 | tf_op jit(solution)/shard_map/add | solution.py:67
  79.5 1.2 %collective-permute-done.7 = f32[4,128,512]{2,1,0:T(8,128)} collective-permute-done((f32[4,128,512]{2,1,0:T(8,128)}, f32[4,128,512]{2,1,0:T(8,128)}, u32[]{:S(2)}, u32[]{:S(2)}) %collective-permute-start.7) | collective-permute-done | bytes 1048608 | tf_op jit(solution)/shard_map/ppermute | solution.py:67
  80.7 1.4 %bitcast_add_fusion = f32[4,128,512]{2,1,0:T(8,128)S(1)} fusion(f32[4,128,512]{2,1,0:T(8,128)} %collective-permute-done.7, f32[4,2,128,512]{3,2,1,0:T(8,128)S(1)} %copy-done.1, s32[]{:T(128)S(6)} %select_n.92), kind=kLoop, calls=%fused_computation | loop fusion | flops 262144 | bytes 3145732 | tf_op jit(solution)/shard_map/add | solution.py:67
  82.2 0.0 slice-start
  82.2 0.2 constant_dynamic-slice_fusion.7
  82.4 0.1 copy.43
  82.5 0.1 collective-permute-start.1
  82.6 0.1 copy.44
  82.7 0.8 collective-permute-start.2
  83.5 0.8 copy.45
  84.3 2.8 %collective-permute-start.3 = (f32[128,512]{0,1:T(8,128)}, f32[128,512]{0,1:T(8,128)S(1)}, u32[]{:S(2)}, u32[]{:S(2)}) collective-permute-start(f32[128,512]{0,1:T(8,128)} %bitcast.11), channel_id=1, source_target_pairs={{0,24},{8,0},{16,8},{24,16},{1,25},{9,1},{17,9},{25,17},{2,26},{10... | collective-permute-start | bytes 786440 | tf_op jit(solution)/shard_map/ppermute | solution.py:74
  87.1 0.1 copy.63
  87.3 0.1 copy.42
  87.4 0.8 copy.53
  88.2 0.0 collective-permute-start.10
  88.2 0.8 copy.51
  89.1 2.0 %collective-permute-start.8 = (f32[128,512]{0,1:T(8,128)}, f32[128,512]{0,1:T(8,128)S(1)}, u32[]{:S(2)}, u32[]{:S(2)}) collective-permute-start(f32[128,512]{0,1:T(8,128)} %bitcast.24), channel_id=1, source_target_pairs={{0,8},{8,16},{16,24},{24,0},{1,9},{9,17},{17,25},{25,1},{2,10},{10... | collective-permute-start | bytes 786440 | tf_op jit(solution)/shard_map/ppermute | solution.py:74
  91.1 0.8 copy.52
  91.9 0.1 copy.50
  92.0 0.6 collective-permute-done.1
  92.6 0.9 collective-permute-start.9
  93.5 4.0 %collective-permute-done.2 = f32[128,512]{0,1:T(8,128)S(1)} collective-permute-done((f32[128,512]{0,1:T(8,128)S(1)}, f32[128,512]{0,1:T(8,128)S(1)}, u32[]{:S(2)}, u32[]{:S(2)}) %collective-permute-start.2) | collective-permute-done | bytes 262176 | tf_op jit(solution)/shard_map/ppermute | solution.py:74
  97.5 0.0 collective-permute-done.3
  97.6 0.1 copy.47
  97.7 2.4 %collective-permute-start.4 = (f32[128,128]{1,0:T(8,128)S(1)}, f32[128,128]{1,0:T(8,128)S(1)}, u32[]{:S(2)}, u32[]{:S(2)}) collective-permute-start(f32[128,128]{1,0:T(8,128)S(1)} %bitcast.83), channel_id=1, source_target_pairs={{0,1},{1,2},{2,3},{3,0},{4,5},{5,6},{6,7},{7,4},{8,9},{9,10},{10,1... | collective-permute-start | bytes 196616 | tf_op jit(solution)/shard_map/ppermute | solution.py:51
  100.1 0.1 copy.48
  100.2 2.7 %collective-permute-start.5 = (f32[128,128]{1,0:T(8,128)S(1)}, f32[128,128]{1,0:T(8,128)S(1)}, u32[]{:S(2)}, u32[]{:S(2)}) collective-permute-start(f32[128,128]{1,0:T(8,128)S(1)} %bitcast.82), channel_id=1, source_target_pairs={{0,2},{1,3},{2,0},{3,1},{4,6},{5,7},{6,4},{7,5},{8,10},{9,11},{10,... | collective-permute-start | bytes 196616 | tf_op jit(solution)/shard_map/ppermute | solution.py:51
  102.8 0.1 copy.49
  102.9 0.1 copy.46
  103.0 0.0 collective-permute-done.10
  103.0 4.3 %collective-permute-start.6 = (f32[128,128]{1,0:T(8,128)S(1)}, f32[128,128]{1,0:T(8,128)S(1)}, u32[]{:S(2)}, u32[]{:S(2)}) collective-permute-start(f32[128,128]{1,0:T(8,128)S(1)} %bitcast.84), channel_id=1, source_target_pairs={{0,3},{1,0},{2,1},{3,2},{4,7},{5,4},{6,5},{7,6},{8,11},{9,8},{10,9... | collective-permute-start | bytes 196616 | tf_op jit(solution)/shard_map/ppermute | solution.py:51
  107.4 1.4 %collective-permute-done.8 = f32[128,512]{0,1:T(8,128)S(1)} collective-permute-done((f32[128,512]{0,1:T(8,128)}, f32[128,512]{0,1:T(8,128)S(1)}, u32[]{:S(2)}, u32[]{:S(2)}) %collective-permute-start.8) | collective-permute-done | bytes 262176 | tf_op jit(solution)/shard_map/ppermute | solution.py:74
  108.7 0.0 collective-permute-done.9
  108.8 0.1 copy.55
  108.9 2.4 %collective-permute-start.11 = (f32[128,128]{1,0:T(8,128)S(1)}, f32[128,128]{1,0:T(8,128)S(1)}, u32[]{:S(2)}, u32[]{:S(2)}) collective-permute-start(f32[128,128]{1,0:T(8,128)S(1)} %bitcast.85), channel_id=1, source_target_pairs={{0,1},{1,2},{2,3},{3,0},{4,5},{5,6},{6,7},{7,4},{8,9},{9,10},{10,1... | collective-permute-start | bytes 196616 | tf_op jit(solution)/shard_map/ppermute | solution.py:51
  111.3 0.1 copy.56
  111.4 2.7 %collective-permute-start.12 = (f32[128,128]{1,0:T(8,128)S(1)}, f32[128,128]{1,0:T(8,128)S(1)}, u32[]{:S(2)}, u32[]{:S(2)}) collective-permute-start(f32[128,128]{1,0:T(8,128)S(1)} %bitcast.86), channel_id=1, source_target_pairs={{0,2},{1,3},{2,0},{3,1},{4,6},{5,7},{6,4},{7,5},{8,10},{9,11},{10,... | collective-permute-start | bytes 196616 | tf_op jit(solution)/shard_map/ppermute | solution.py:51
  114.0 0.1 copy.57
  114.1 0.1 copy.54
  114.2 0.0 collective-permute-done.4
  114.3 1.4 %collective-permute-start.13 = (f32[128,128]{1,0:T(8,128)S(1)}, f32[128,128]{1,0:T(8,128)S(1)}, u32[]{:S(2)}, u32[]{:S(2)}) collective-permute-start(f32[128,128]{1,0:T(8,128)S(1)} %bitcast.87), channel_id=1, source_target_pairs={{0,3},{1,0},{2,1},{3,2},{4,7},{5,4},{6,5},{7,6},{8,11},{9,8},{10,9... | collective-permute-start | bytes 196616 | tf_op jit(solution)/shard_map/ppermute | solution.py:51
  115.7 0.0 collective-permute-done.6
  115.7 0.5 collective-permute-done.11
  116.2 2.4 %collective-permute-done.12 = f32[128,128]{1,0:T(8,128)S(1)} collective-permute-done((f32[128,128]{1,0:T(8,128)S(1)}, f32[128,128]{1,0:T(8,128)S(1)}, u32[]{:S(2)}, u32[]{:S(2)}) %collective-permute-start.12) | collective-permute-done | bytes 65568 | tf_op jit(solution)/shard_map/ppermute | solution.py:51
  118.6 0.3 collective-permute-done.13
  118.9 0.1 copy.58
  119.0 0.1 fusion.4
  119.1 0.8 copy.60
  (12 shorter events, 0.2 us)
Async XLA Ops:
  3.7 57.4 %all-to-all-start = ((f32[8,128,1024]{2,1,0:T(8,128)}), f32[8,128,1024]{2,1,0:T(8,128)}, u32[]{:S(2)}, u32[]{:S(2)}) async-start(f32[8,128,1024]{2,1,0:T(8,128)} %shard_map.17), calls=%async_computation | async-start | bytes 8388608 | tf_op jit(solution)/shard_map/all_to_all | solution.py:85
  69.4 8.5 %collective-permute-start = (f32[4,128,512]{2,1,0:T(8,128)S(1)}, f32[4,128,512]{2,1,0:T(8,128)}, u32[]{:S(2)}, u32[]{:S(2)}) collective-permute-start(f32[4,128,512]{2,1,0:T(8,128)S(1)} %dynamic-slice_bitcast_fusion.1), channel_id=1, source_target_pairs={{0,4},{4,0},{1,5},{5,1},{2,6},{6,2},{3,7},{7,3},{8,12},{12,8},{9,1... | collective-permute-start | bytes 3145736 | tf_op jit(solution)/shard_map/ppermute | solution.py:67
  75.3 1.3 %copy-start = (f32[4,2,128,512]{3,2,1,0:T(8,128)}, f32[4,2,128,512]{3,2,1,0:T(8,128)S(1)}, u32[]{:S(2)}) copy-start(f32[4,2,128,512]{3,2,1,0:T(8,128)S(1)} %fusion.13) | copy-start | bytes 6291460
  77.7 3.0 %collective-permute-start.7 = (f32[4,128,512]{2,1,0:T(8,128)}, f32[4,128,512]{2,1,0:T(8,128)}, u32[]{:S(2)}, u32[]{:S(2)}) collective-permute-start(f32[4,128,512]{2,1,0:T(8,128)} %dynamic-slice_bitcast_fusion), channel_id=1, source_target_pairs={{0,4},{4,0},{1,5},{5,1},{2,6},{6,2},{3,7},{7,3},{8,12},{12,8},{9,1... | collective-permute-start | bytes 3145736 | tf_op jit(solution)/shard_map/ppermute | solution.py:67
  77.9 2.8 %copy-start.1 = (f32[4,2,128,512]{3,2,1,0:T(8,128)S(1)}, f32[4,2,128,512]{3,2,1,0:T(8,128)}, u32[]{:S(2)}) copy-start(f32[4,2,128,512]{3,2,1,0:T(8,128)} %copy-done) | copy-start | bytes 6291460
  82.2 5.0 %slice-start = ((f32[128,8192]{1,0:T(8,128)}), f32[128,256]{1,0:T(8,128)S(1)}, s32[]{:S(2)}) async-start(f32[128,8192]{1,0:T(8,128)} %block_ref.1), calls=%async_computation.1 | async-start | bytes 262144 | tf_op jit(solution)/shard_map/slice | solution.py:100
  82.5 10.1 %collective-permute-start.1 = (f32[128,512]{0,1:T(8,128)S(1)}, f32[128,512]{0,1:T(8,128)S(1)}, u32[]{:S(2)}, u32[]{:S(2)}) collective-permute-start(f32[128,512]{0,1:T(8,128)S(1)} %bitcast.80), channel_id=1, source_target_pairs={{0,8},{8,16},{16,24},{24,0},{1,9},{9,17},{17,25},{25,1},{2,10},{10... | collective-permute-start | bytes 786440 | tf_op jit(solution)/shard_map/ppermute | solution.py:74
  82.7 14.8 %collective-permute-start.2 = (f32[128,512]{0,1:T(8,128)S(1)}, f32[128,512]{0,1:T(8,128)S(1)}, u32[]{:S(2)}, u32[]{:S(2)}) collective-permute-start(f32[128,512]{0,1:T(8,128)S(1)} %bitcast.79), channel_id=1, source_target_pairs={{0,16},{8,24},{16,0},{24,8},{1,17},{9,25},{17,1},{25,9},{2,18},{10... | collective-permute-start | bytes 786440 | tf_op jit(solution)/shard_map/ppermute | solution.py:74
  84.3 13.2 %collective-permute-start.3 = (f32[128,512]{0,1:T(8,128)}, f32[128,512]{0,1:T(8,128)S(1)}, u32[]{:S(2)}, u32[]{:S(2)}) collective-permute-start(f32[128,512]{0,1:T(8,128)} %bitcast.11), channel_id=1, source_target_pairs={{0,24},{8,0},{16,8},{24,16},{1,25},{9,1},{17,9},{25,17},{2,26},{10... | collective-permute-start | bytes 786440 | tf_op jit(solution)/shard_map/ppermute | solution.py:74
  88.2 14.8 %collective-permute-start.10 = (f32[128,512]{0,1:T(8,128)}, f32[128,512]{0,1:T(8,128)S(1)}, u32[]{:S(2)}, u32[]{:S(2)}) collective-permute-start(f32[128,512]{0,1:T(8,128)} %bitcast.26), channel_id=1, source_target_pairs={{0,24},{8,0},{16,8},{24,16},{1,25},{9,1},{17,9},{25,17},{2,26},{10... | collective-permute-start | bytes 786440 | tf_op jit(solution)/shard_map/ppermute | solution.py:74
  89.1 19.7 %collective-permute-start.8 = (f32[128,512]{0,1:T(8,128)}, f32[128,512]{0,1:T(8,128)S(1)}, u32[]{:S(2)}, u32[]{:S(2)}) collective-permute-start(f32[128,512]{0,1:T(8,128)} %bitcast.24), channel_id=1, source_target_pairs={{0,8},{8,16},{16,24},{24,0},{1,9},{9,17},{17,25},{25,1},{2,10},{10... | collective-permute-start | bytes 786440 | tf_op jit(solution)/shard_map/ppermute | solution.py:74
  92.6 16.1 %collective-permute-start.9 = (f32[128,512]{0,1:T(8,128)}, f32[128,512]{0,1:T(8,128)S(1)}, u32[]{:S(2)}, u32[]{:S(2)}) collective-permute-start(f32[128,512]{0,1:T(8,128)} %bitcast.81), channel_id=1, source_target_pairs={{0,16},{8,24},{16,0},{24,8},{1,17},{9,25},{17,1},{25,9},{2,18},{10... | collective-permute-start | bytes 786440 | tf_op jit(solution)/shard_map/ppermute | solution.py:74
  97.7 16.5 %collective-permute-start.4 = (f32[128,128]{1,0:T(8,128)S(1)}, f32[128,128]{1,0:T(8,128)S(1)}, u32[]{:S(2)}, u32[]{:S(2)}) collective-permute-start(f32[128,128]{1,0:T(8,128)S(1)} %bitcast.83), channel_id=1, source_target_pairs={{0,1},{1,2},{2,3},{3,0},{4,5},{5,6},{6,7},{7,4},{8,9},{9,10},{10,1... | collective-permute-start | bytes 196616 | tf_op jit(solution)/shard_map/ppermute | solution.py:51
  100.2 15.5 %collective-permute-start.5 = (f32[128,128]{1,0:T(8,128)S(1)}, f32[128,128]{1,0:T(8,128)S(1)}, u32[]{:S(2)}, u32[]{:S(2)}) collective-permute-start(f32[128,128]{1,0:T(8,128)S(1)} %bitcast.82), channel_id=1, source_target_pairs={{0,2},{1,3},{2,0},{3,1},{4,6},{5,7},{6,4},{7,5},{8,10},{9,11},{10,... | collective-permute-start | bytes 196616 | tf_op jit(solution)/shard_map/ppermute | solution.py:51
  103.0 12.6 %collective-permute-start.6 = (f32[128,128]{1,0:T(8,128)S(1)}, f32[128,128]{1,0:T(8,128)S(1)}, u32[]{:S(2)}, u32[]{:S(2)}) collective-permute-start(f32[128,128]{1,0:T(8,128)S(1)} %bitcast.84), channel_id=1, source_target_pairs={{0,3},{1,0},{2,1},{3,2},{4,7},{5,4},{6,5},{7,6},{8,11},{9,8},{10,9... | collective-permute-start | bytes 196616 | tf_op jit(solution)/shard_map/ppermute | solution.py:51
  108.9 7.3 %collective-permute-start.11 = (f32[128,128]{1,0:T(8,128)S(1)}, f32[128,128]{1,0:T(8,128)S(1)}, u32[]{:S(2)}, u32[]{:S(2)}) collective-permute-start(f32[128,128]{1,0:T(8,128)S(1)} %bitcast.85), channel_id=1, source_target_pairs={{0,1},{1,2},{2,3},{3,0},{4,5},{5,6},{6,7},{7,4},{8,9},{9,10},{10,1... | collective-permute-start | bytes 196616 | tf_op jit(solution)/shard_map/ppermute | solution.py:51
  111.4 7.2 %collective-permute-start.12 = (f32[128,128]{1,0:T(8,128)S(1)}, f32[128,128]{1,0:T(8,128)S(1)}, u32[]{:S(2)}, u32[]{:S(2)}) collective-permute-start(f32[128,128]{1,0:T(8,128)S(1)} %bitcast.86), channel_id=1, source_target_pairs={{0,2},{1,3},{2,0},{3,1},{4,6},{5,7},{6,4},{7,5},{8,10},{9,11},{10,... | collective-permute-start | bytes 196616 | tf_op jit(solution)/shard_map/ppermute | solution.py:51
  114.3 4.6 %collective-permute-start.13 = (f32[128,128]{1,0:T(8,128)S(1)}, f32[128,128]{1,0:T(8,128)S(1)}, u32[]{:S(2)}, u32[]{:S(2)}) collective-permute-start(f32[128,128]{1,0:T(8,128)S(1)} %bitcast.87), channel_id=1, source_target_pairs={{0,3},{1,0},{2,1},{3,2},{4,7},{5,4},{6,5},{7,6},{8,11},{9,8},{10,9... | collective-permute-start | bytes 196616 | tf_op jit(solution)/shard_map/ppermute | solution.py:51

commit v8 on v7

--- a/solution.py
+++ b/solution.py
@@ -52,25 +52,46 @@
     return total
 
 
-def row_reduce_scatter(pieces, right):
+def row_reduce_scatter(gram, core_major):
     n_chip = lax.axis_size("chip")
     n_core = lax.axis_size("core")
     me = lax.axis_index("core")
-    rows = pieces.shape[0]
-    width = right.shape[0]
+    rows, width = gram.shape
     strip = rows // (n_chip * n_core)
-    paired = inner_rows(pieces, right).reshape(n_chip, n_core, strip, width)
-    on_chip = lax.dynamic_index_in_dim(paired, me, 1, keepdims=False)
+    if core_major:
+        paired, axis = gram.reshape(n_core, n_chip, strip, width), 0
+    else:
+        paired, axis = gram.reshape(n_chip, n_core, strip, width), 1
+    on_chip = lax.dynamic_index_in_dim(paired, me, axis, keepdims=False)
     for s in range(1, n_core):
-        send = lax.dynamic_index_in_dim(paired, (me + s) % n_core, 1, keepdims=False)
+        send = lax.dynamic_index_in_dim(paired, (me + s) % n_core, axis, keepdims=False)
         perm = [(i, (i + s) % n_core) for i in range(n_core)]
         on_chip = on_chip + lax.ppermute(send, "core", perm)
     blocks = on_chip
     mine = lax.axis_index("chip")
     total = lax.dynamic_index_in_dim(blocks, mine, 0, keepdims=False)
     for s in range(1, n_chip):
-        send = lax.dynamic_index_in_dim(blocks, (mine + s) % n_chip, 0, keepdims=False)
-        perm = [(i, (i + s) % n_chip) for i in range(n_chip)]
+        if n_chip & (n_chip - 1) == 0:
+            peer, perm = mine ^ s, [(i, i ^ s) for i in range(n_chip)]
+        else:
+            peer, perm = (mine + s) % n_chip, [(i, (i + s) % n_chip) for i in range(n_chip)]
+        send = lax.dynamic_index_in_dim(blocks, peer, 0, keepdims=False)
+        total = total + lax.ppermute(send, "chip", perm)
+    return total
+
+
+def chip_reduce_scatter(on_chip):
+    n_chip = lax.axis_size("chip")
+    rows, width = on_chip.shape
+    blocks = on_chip.reshape(n_chip, rows // n_chip, width)
+    mine = lax.axis_index("chip")
+    total = lax.dynamic_index_in_dim(blocks, mine, 0, keepdims=False)
+    for s in range(1, n_chip):
+        if n_chip & (n_chip - 1) == 0:
+            peer, perm = mine ^ s, [(i, i ^ s) for i in range(n_chip)]
+        else:
+            peer, perm = (mine + s) % n_chip, [(i, (i + s) % n_chip) for i in range(n_chip)]
+        send = lax.dynamic_index_in_dim(blocks, peer, 0, keepdims=False)
         total = total + lax.ppermute(send, "chip", perm)
     return total
 
@@ -79,23 +100,43 @@
     strip_rows, cols = adjacency.shape
     n_row = lax.axis_size(ROW)
     n_col = lax.axis_size("col")
+    n_core = lax.axis_size("core")
     window = strip_rows * n_row // n_col
     piece = cols // n_row
+    core_major = n_col == lax.axis_size("chip") and window == n_core * strip_rows
     chunks = column_chunks(adjacency, n_row)
-    pieces = lax.all_to_all(chunks, ROW, split_axis=0, concat_axis=0, tiled=True)
+    order = ("core", "chip") if core_major else ROW
+    pieces = lax.all_to_all(chunks, order, split_axis=0, concat_axis=0, tiled=True)
     pieces = with_layout_constraint(pieces, Layout((0, 1, 2)))
     own_degree = lax.psum(jnp.sum(adjacency, axis=1), "col")
     all_degree = lax.all_gather(own_degree, ROW, axis=0, tiled=True)
     col_degree = lax.dynamic_slice_in_dim(all_degree, lax.axis_index("col") * window, window, 0)
     pieces, own_degree, col_degree = lax.optimization_barrier((pieces, own_degree, col_degree))
-    pieces = pieces.reshape(n_row * strip_rows, piece)
-    groups = 2 if window % 256 == 0 else 1
-    sub = window // groups
-    by_group = pieces.reshape(n_col, groups, sub, piece)
     outs = []
-    for g in range(groups):
-        right = by_group[:, g].reshape(n_col * sub, piece)
-        outs.append(col_reduce_scatter(row_reduce_scatter(pieces, right)))
+    if core_major:
+        groups = n_core
+        flat = pieces.reshape(n_row * strip_rows, piece)
+        by_core = pieces.reshape(n_core, n_col * strip_rows, piece)
+        me = lax.axis_index("core")
+        for g in range(groups):
+            right = by_core[g]
+            on_chip = None
+            for s in range(1, n_core):
+                left = lax.dynamic_index_in_dim(by_core, (me + s) % n_core, 0, keepdims=False)
+                perm = [(i, (i + s) % n_core) for i in range(n_core)]
+                got = lax.ppermute(inner_rows(left, right), "core", perm)
+                on_chip = got if on_chip is None else on_chip + got
+            left = lax.dynamic_index_in_dim(by_core, me, 0, keepdims=False)
+            on_chip = inner_rows(left, right) + on_chip
+            outs.append(col_reduce_scatter(chip_reduce_scatter(on_chip)))
+    else:
+        groups = 2 if window % 256 == 0 else 1
+        sub = window // groups
+        flat = pieces.reshape(n_row * strip_rows, piece)
+        by_group = flat.reshape(n_col, groups, sub, piece)
+        for g in range(groups):
+            right = by_group[:, g].reshape(n_col * sub, piece)
+            outs.append(col_reduce_scatter(row_reduce_scatter(inner_rows(flat, right), False)))
     shared_sum = jnp.stack(outs, axis=1).reshape(strip_rows, window)
     linked = adjacency[:, :window]
     smaller = jnp.minimum(own_degree[:, None], col_degree[None, :])

time: 120 us -> 119 us (level)
  matrix products: 11 us -> 17.5 us
  other arithmetic: 5.76 us -> 2.75 us
  local copies, waits for them, and re-layouts: 11 us -> 8.33 us
  waiting for transfers between devices: 10.4 us -> 8.25 us
    dot_general x2 -> x4, matrix products: 11 us -> 17.5 us  [inner_rows(): lax.dot_general(left, right, (((1,), (1,)), ((), ())), precision=lax.Prec...]
    add x4 -> x2, other arithmetic: 3.11 us -> 0.1 us  [chip_reduce_scatter(): total = total + lax.ppermute(send, 'chip', perm)]
    ppermute x8, waiting for transfers between devices: 7.21 us -> 4.84 us  [the longest x6 4.84 us: chip_reduce_scatter(): total = total + lax.ppermute(send, 'chip', perm)]
    unnamed x5 -> x3, local copies, waits for them, and re-layouts: 1.42 us -> 0.09 us
where the time goes in v8:
time: 119 us
  blocking collectives  49.5 us (42%)
  starting transfers between devices  28.6 us (24%)
  matrix products  17.5 us (15%)
  local copies, waits for them, and re-layouts  8.33 us (7%)
  waiting for transfers between devices  8.25 us (7%)
  Pallas kernels  3.71 us (3%)
  other arithmetic  2.75 us (2%)
    all_gather x1, blocking collectives, body(): all_degree = lax.all_gather(own_degree, ROW, axis=0, tiled=True)  36.7 us
    dot_general x4, matrix products, inner_rows(): lax.dot_general(left, right, (((1,), (1,)), ((), ())), precision=lax.Prec...  17.5 us
    ppermute x6, starting transfers between devices, col_reduce_scatter(): total = total + lax.ppermute(send, 'col', perm)  15.7 us
    psum x1, blocking collectives, body(): own_degree = lax.psum(jnp.sum(adjacency, axis=1), 'col')  12.8 us
    ppermute x6, starting transfers between devices, chip_reduce_scatter(): total = total + lax.ppermute(send, 'chip', perm)  7.16 us
    all_to_all x1, starting transfers between devices, body(): lax.all_to_all(chunks, order, split_axis=0, concat_axis=0, tiled=True)  5.17 us
    ppermute x6, waiting for transfers between devices, chip_reduce_scatter(): total = total + lax.ppermute(send, 'chip', perm)  4.84 us
    pallas_call x1, Pallas kernels, column_chunks(): pl.pallas_call(_copy_blocks, grid=(n_chunks // per_step,), in_specs=[pl.B...  3.71 us
  transfers between devices with their start and end apart: 15, of which 7 were waited for; matrix products, arithmetic and copies ran while one was open for 13% of the time, Pallas kernels for 0%

profile of v8, /device:TPU:0, one launch (start us, length us, event | category | flops | bytes accessed | tf_op | source)
XLA Modules:
  0.0 118.9 jit_solution(2279186029930983817)
XLA Ops:
  0.0 3.7 %shard_map.17 = f32[8,128,1024]{2,1,0:T(8,128)} custom-call(f32[128,8192]{1,0:T(8,128)} %block_ref.1), custom_call_target="tpu_custom_call" | custom-call | tf_op jit(solution)/shard_map/pallas_call | solution.py:32
  3.7 5.2 %all-to-all-start = ((f32[8,128,1024]{2,1,0:T(8,128)}), f32[8,128,1024]{2,1,0:T(8,128)}, u32[]{:S(2)}, u32[]{:S(2)}) async-start(f32[8,128,1024]{2,1,0:T(8,128)} %shard_map.17), calls=%async_computation | async-start | bytes 8388608 | tf_op jit(solution)/shard_map/all_to_all | solution.py:109
  8.9 2.5 %reduce_sum.9 = f32[128]{0:T(128)S(1)} reduce(f32[128,8192]{1,0:T(8,128)} %block_ref.1, f32[]{:T(128)} %constant.96.clone.1), dimensions={1}, to_apply=%region_0.0 | reduce | flops 1048448 | bytes 4194820 | tf_op jit(solution)/shard_map/reduce_sum | solution.py:111
  11.4 12.8 %psum.7 = f32[128]{0:T(128)S(1)} all-reduce(f32[128]{0:T(128)S(1)} %reduce_sum.9), channel_id=1, replica_groups=mesh['chip'=4,'core'=2,'col'=4] {'col'}, use_global_device_ids=true, to_apply=%region_1.0 | all-reduce | flops 128 | bytes 1024 | tf_op jit(solution)/shard_map/psum | solution.py:111
  24.2 36.7 %all-gather = f32[8,1,128]{2,1,0:T(1,128)S(1)} all-gather(f32[1,1,128]{2,1,0:T(1,128)S(1)} %bitcast.93), channel_id=1, replica_groups=mesh['chip'=4,'core'=2,'col'=4] {'chip','core'}, dimensions={0}, use_global_device_ids=true | all-gather | bytes 4608 | tf_op jit(solution)/shard_map/all_gather | solution.py:112
  60.9 0.1 dynamic_slice.62
  60.9 0.0 all-to-all-done
  60.9 2.5 %fusion.33 = (f32[4,128,1024]{2,1,0:T(8,128)S(1)}, f32[4,128,1024]{2,1,0:T(8,128)S(1)}) fusion(f32[8,128,1024]{2,1,0:T(8,128)} %all-to-all-done), kind=kLoop, calls=%fused_computation.51 | loop fusion | bytes 8388608 | tf_op jit(solution)/shard_map/slice | solution.py:122
  63.5 0.0 copy-start
  63.5 5.3 %fusion.2 = f32[512,512]{1,0:T(8,128)} fusion(f32[512,1024]{1,0:T(8,128)S(1)} %bitcast.77, f32[2,512,1024]{2,1,0:T(8,128)} %bitcast.2, s32[]{:T(128)S(6)} %select_n.76), kind=kOutput, calls=%fused_computation.2 | convolution fusion | flops 1610612736 | bytes 5242884 | tf_op jit(solution)/shard_map/dot_general | solution.py:13
  68.7 0.3 collective-permute-start
  69.1 4.4 %fusion = f32[512,512]{1,0:T(8,128)} fusion(f32[512,1024]{1,0:T(8,128)S(1)} %bitcast.75, f32[2,512,1024]{2,1,0:T(8,128)} %bitcast.2, s32[]{:T(128)S(6)} %select_n.76), kind=kOutput, calls=%fused_computation | convolution fusion | flops 1610612736 | bytes 5242884 | tf_op jit(solution)/shard_map/dot_general | solution.py:13
  73.5 0.2 collective-permute-start.7
  73.7 0.0 collective-permute-done
  73.7 4.4 %fusion.12 = f32[512,512]{1,0:T(8,128)S(1)} fusion(f32[512,512]{1,0:T(8,128)} %collective-permute-done, f32[512,1024]{1,0:T(8,128)} %bitcast.78, f32[2,512,1024]{2,1,0:T(8,128)} %bitcast.2, s32[]{:T(128)S(6)} %select_n.74), kind=kOutput, calls=%fused_computation.12 | convolution fusion | flops 1610874880 | bytes 6291460 | tf_op jit(solution)/shard_map/dot_general | solution.py:13
  78.1 0.0 collective-permute-done.7
  78.1 3.5 %fusion.15 = f32[512,512]{1,0:T(8,128)S(1)} fusion(f32[512,512]{1,0:T(8,128)S(1)} %collective-permute-done.7, f32[512,1024]{1,0:T(8,128)S(1)} %bitcast.76, f32[2,512,1024]{2,1,0:T(8,128)} %bitcast.2, s32[]{:T(128)S(6)} %select_n.74), kind=kOutput, calls=%fused_computation.13 | convolution fusion | flops 1610874880 | bytes 6291460 | tf_op jit(solution)/shard_map/dot_general | solution.py:13
  81.6 0.0 slice-start
  81.6 0.2 constant_dynamic-slice_fusion.7
  81.8 0.1 copy.43
  81.9 0.1 collective-permute-start.1
  82.0 0.1 copy.44
  82.1 0.9 collective-permute-start.2
  83.0 0.9 copy.45
  83.8 2.6 %collective-permute-start.3 = (f32[128,512]{0,1:T(8,128)}, f32[128,512]{0,1:T(8,128)S(1)}, u32[]{:S(2)}, u32[]{:S(2)}) collective-permute-start(f32[128,512]{0,1:T(8,128)} %bitcast.10), channel_id=1, source_target_pairs={{0,24},{8,16},{16,8},{24,0},{1,25},{9,17},{17,9},{25,1},{2,26},{10... | collective-permute-start | bytes 786440 | tf_op jit(solution)/shard_map/ppermute | solution.py:95
  86.5 0.0 slice-done
  86.5 0.1 copy.61
  86.6 0.1 copy.42
  86.7 0.8 copy.53
  87.6 0.3 collective-permute-start.10
  87.8 0.8 copy.51
  88.7 1.9 %collective-permute-start.8 = (f32[128,512]{0,1:T(8,128)}, f32[128,512]{0,1:T(8,128)S(1)}, u32[]{:S(2)}, u32[]{:S(2)}) collective-permute-start(f32[128,512]{0,1:T(8,128)} %bitcast.20), channel_id=1, source_target_pairs={{0,8},{8,0},{16,24},{24,16},{1,9},{9,1},{17,25},{25,17},{2,10},{10... | collective-permute-start | bytes 786440 | tf_op jit(solution)/shard_map/ppermute | solution.py:95
  90.6 0.8 copy.52
  91.4 0.1 copy.50
  91.5 0.0 collective-permute-done.1
  91.6 1.4 %collective-permute-start.9 = (f32[128,512]{0,1:T(8,128)}, f32[128,512]{0,1:T(8,128)S(1)}, u32[]{:S(2)}, u32[]{:S(2)}) collective-permute-start(f32[128,512]{0,1:T(8,128)} %bitcast.85), channel_id=1, source_target_pairs={{0,16},{8,24},{16,0},{24,8},{1,17},{9,25},{17,1},{25,9},{2,18},{10... | collective-permute-start | bytes 786440 | tf_op jit(solution)/shard_map/ppermute | solution.py:95
  92.9 0.0 collective-permute-done.2
  92.9 4.0 %collective-permute-done.3 = f32[128,512]{0,1:T(8,128)S(1)} collective-permute-done((f32[128,512]{0,1:T(8,128)}, f32[128,512]{0,1:T(8,128)S(1)}, u32[]{:S(2)}, u32[]{:S(2)}) %collective-permute-start.3) | collective-permute-done | bytes 262176 | tf_op jit(solution)/shard_map/ppermute | solution.py:95
  97.1 0.1 copy.47
  97.2 2.3 %collective-permute-start.4 = (f32[128,128]{1,0:T(8,128)S(1)}, f32[128,128]{1,0:T(8,128)S(1)}, u32[]{:S(2)}, u32[]{:S(2)}) collective-permute-start(f32[128,128]{1,0:T(8,128)S(1)} %bitcast.87), channel_id=1, source_target_pairs={{0,1},{1,2},{2,3},{3,0},{4,5},{5,6},{6,7},{7,4},{8,9},{9,10},{10,1... | collective-permute-start | bytes 196616 | tf_op jit(solution)/shard_map/ppermute | solution.py:51
  99.5 0.1 copy.48
  99.6 2.7 %collective-permute-start.5 = (f32[128,128]{1,0:T(8,128)S(1)}, f32[128,128]{1,0:T(8,128)S(1)}, u32[]{:S(2)}, u32[]{:S(2)}) collective-permute-start(f32[128,128]{1,0:T(8,128)S(1)} %bitcast.86), channel_id=1, source_target_pairs={{0,2},{1,3},{2,0},{3,1},{4,6},{5,7},{6,4},{7,5},{8,10},{9,11},{10,... | collective-permute-start | bytes 196616 | tf_op jit(solution)/shard_map/ppermute | solution.py:51
  102.2 0.1 copy.49
  102.3 0.1 copy.46
  102.4 0.1 collective-permute-done.10
  102.5 4.3 %collective-permute-start.6 = (f32[128,128]{1,0:T(8,128)S(1)}, f32[128,128]{1,0:T(8,128)S(1)}, u32[]{:S(2)}, u32[]{:S(2)}) collective-permute-start(f32[128,128]{1,0:T(8,128)S(1)} %bitcast.88), channel_id=1, source_target_pairs={{0,3},{1,0},{2,1},{3,2},{4,7},{5,4},{6,5},{7,6},{8,11},{9,8},{10,9... | collective-permute-start | bytes 196616 | tf_op jit(solution)/shard_map/ppermute | solution.py:51
  106.8 0.5 collective-permute-done.8
  107.4 0.2 collective-permute-done.9
  107.6 0.1 copy.55
  107.7 2.3 %collective-permute-start.11 = (f32[128,128]{1,0:T(8,128)S(1)}, f32[128,128]{1,0:T(8,128)S(1)}, u32[]{:S(2)}, u32[]{:S(2)}) collective-permute-start(f32[128,128]{1,0:T(8,128)S(1)} %bitcast.89), channel_id=1, source_target_pairs={{0,1},{1,2},{2,3},{3,0},{4,5},{5,6},{6,7},{7,4},{8,9},{9,10},{10,1... | collective-permute-start | bytes 196616 | tf_op jit(solution)/shard_map/ppermute | solution.py:51
  110.1 0.1 copy.56
  110.2 2.7 %collective-permute-start.12 = (f32[128,128]{1,0:T(8,128)S(1)}, f32[128,128]{1,0:T(8,128)S(1)}, u32[]{:S(2)}, u32[]{:S(2)}) collective-permute-start(f32[128,128]{1,0:T(8,128)S(1)} %bitcast.90), channel_id=1, source_target_pairs={{0,2},{1,3},{2,0},{3,1},{4,6},{5,7},{6,4},{7,5},{8,10},{9,11},{10,... | collective-permute-start | bytes 196616 | tf_op jit(solution)/shard_map/ppermute | solution.py:51
  112.8 0.1 copy.57
  112.9 0.1 copy.54
  113.0 0.0 collective-permute-done.4
  113.0 1.4 %collective-permute-start.13 = (f32[128,128]{1,0:T(8,128)S(1)}, f32[128,128]{1,0:T(8,128)S(1)}, u32[]{:S(2)}, u32[]{:S(2)}) collective-permute-start(f32[128,128]{1,0:T(8,128)S(1)} %bitcast.91), channel_id=1, source_target_pairs={{0,3},{1,0},{2,1},{3,2},{4,7},{5,4},{6,5},{7,6},{8,11},{9,8},{10,9... | collective-permute-start | bytes 196616 | tf_op jit(solution)/shard_map/ppermute | solution.py:51
  114.4 0.0 collective-permute-done.5
  114.4 0.0 collective-permute-done.6
  114.5 0.1 collective-permute-done.11
  114.5 2.8 %collective-permute-done.12 = f32[128,128]{1,0:T(8,128)S(1)} collective-permute-done((f32[128,128]{1,0:T(8,128)S(1)}, f32[128,128]{1,0:T(8,128)S(1)}, u32[]{:S(2)}, u32[]{:S(2)}) %collective-permute-start.12) | collective-permute-done | bytes 65568 | tf_op jit(solution)/shard_map/ppermute | solution.py:51
  117.3 0.5 collective-permute-done.13
  117.9 0.1 copy.58
  118.0 0.1 fusion.22
  118.1 0.8 copy.60
  (8 shorter events, 0.2 us)
Async XLA Ops:
  3.7 57.2 %all-to-all-start = ((f32[8,128,1024]{2,1,0:T(8,128)}), f32[8,128,1024]{2,1,0:T(8,128)}, u32[]{:S(2)}, u32[]{:S(2)}) async-start(f32[8,128,1024]{2,1,0:T(8,128)} %shard_map.17), calls=%async_computation | async-start | bytes 8388608 | tf_op jit(solution)/shard_map/all_to_all | solution.py:109
  63.5 5.3 %copy-start = (f32[4,128,1024]{2,1,0:T(8,128)}, f32[4,128,1024]{2,1,0:T(8,128)S(1)}, u32[]{:S(2)}) copy-start(f32[4,128,1024]{2,1,0:T(8,128)S(1)} %get-tuple-element.11) | copy-start | bytes 6291460
  68.7 4.9 %collective-permute-start = (f32[512,512]{1,0:T(8,128)}, f32[512,512]{1,0:T(8,128)}, u32[]{:S(2)}, u32[]{:S(2)}) collective-permute-start(f32[512,512]{1,0:T(8,128)} %fusion.2), channel_id=1, source_target_pairs={{0,4},{4,0},{1,5},{5,1},{2,6},{6,2},{3,7},{7,3},{8,12},{12,8},{9,1... | collective-permute-start | bytes 3145736 | tf_op jit(solution)/shard_map/ppermute | solution.py:127
  73.5 4.6 %collective-permute-start.7 = (f32[512,512]{1,0:T(8,128)}, f32[512,512]{1,0:T(8,128)S(1)}, u32[]{:S(2)}, u32[]{:S(2)}) collective-permute-start(f32[512,512]{1,0:T(8,128)} %fusion), channel_id=1, source_target_pairs={{0,4},{4,0},{1,5},{5,1},{2,6},{6,2},{3,7},{7,3},{8,12},{12,8},{9,1... | collective-permute-start | bytes 3145736 | tf_op jit(solution)/shard_map/ppermute | solution.py:127
  81.6 4.9 %slice-start = ((f32[128,8192]{1,0:T(8,128)}), f32[128,256]{1,0:T(8,128)S(1)}, s32[]{:S(2)}) async-start(f32[128,8192]{1,0:T(8,128)} %block_ref.1), calls=%async_computation.1 | async-start | bytes 262144 | tf_op jit(solution)/shard_map/slice | solution.py:141
  81.9 9.7 %collective-permute-start.1 = (f32[128,512]{0,1:T(8,128)S(1)}, f32[128,512]{0,1:T(8,128)S(1)}, u32[]{:S(2)}, u32[]{:S(2)}) collective-permute-start(f32[128,512]{0,1:T(8,128)S(1)} %bitcast.84), channel_id=1, source_target_pairs={{0,8},{8,0},{16,24},{24,16},{1,9},{9,1},{17,25},{25,17},{2,10},{10... | collective-permute-start | bytes 786440 | tf_op jit(solution)/shard_map/ppermute | solution.py:95
  82.1 10.8 %collective-permute-start.2 = (f32[128,512]{0,1:T(8,128)S(1)}, f32[128,512]{0,1:T(8,128)S(1)}, u32[]{:S(2)}, u32[]{:S(2)}) collective-permute-start(f32[128,512]{0,1:T(8,128)S(1)} %bitcast.83), channel_id=1, source_target_pairs={{0,16},{8,24},{16,0},{24,8},{1,17},{9,25},{17,1},{25,9},{2,18},{10... | collective-permute-start | bytes 786440 | tf_op jit(solution)/shard_map/ppermute | solution.py:95
  83.8 13.1 %collective-permute-start.3 = (f32[128,512]{0,1:T(8,128)}, f32[128,512]{0,1:T(8,128)S(1)}, u32[]{:S(2)}, u32[]{:S(2)}) collective-permute-start(f32[128,512]{0,1:T(8,128)} %bitcast.10), channel_id=1, source_target_pairs={{0,24},{8,16},{16,8},{24,0},{1,25},{9,17},{17,9},{25,1},{2,26},{10... | collective-permute-start | bytes 786440 | tf_op jit(solution)/shard_map/ppermute | solution.py:95
  87.6 15.0 %collective-permute-start.10 = (f32[128,512]{0,1:T(8,128)}, f32[128,512]{0,1:T(8,128)S(1)}, u32[]{:S(2)}, u32[]{:S(2)}) collective-permute-start(f32[128,512]{0,1:T(8,128)} %bitcast.22), channel_id=1, source_target_pairs={{0,24},{8,16},{16,8},{24,0},{1,25},{9,17},{17,9},{25,1},{2,26},{10... | collective-permute-start | bytes 786440 | tf_op jit(solution)/shard_map/ppermute | solution.py:95
  88.7 18.7 %collective-permute-start.8 = (f32[128,512]{0,1:T(8,128)}, f32[128,512]{0,1:T(8,128)S(1)}, u32[]{:S(2)}, u32[]{:S(2)}) collective-permute-start(f32[128,512]{0,1:T(8,128)} %bitcast.20), channel_id=1, source_target_pairs={{0,8},{8,0},{16,24},{24,16},{1,9},{9,1},{17,25},{25,17},{2,10},{10... | collective-permute-start | bytes 786440 | tf_op jit(solution)/shard_map/ppermute | solution.py:95
  91.6 16.0 %collective-permute-start.9 = (f32[128,512]{0,1:T(8,128)}, f32[128,512]{0,1:T(8,128)S(1)}, u32[]{:S(2)}, u32[]{:S(2)}) collective-permute-start(f32[128,512]{0,1:T(8,128)} %bitcast.85), channel_id=1, source_target_pairs={{0,16},{8,24},{16,0},{24,8},{1,17},{9,25},{17,1},{25,9},{2,18},{10... | collective-permute-start | bytes 786440 | tf_op jit(solution)/shard_map/ppermute | solution.py:95
  97.2 15.9 %collective-permute-start.4 = (f32[128,128]{1,0:T(8,128)S(1)}, f32[128,128]{1,0:T(8,128)S(1)}, u32[]{:S(2)}, u32[]{:S(2)}) collective-permute-start(f32[128,128]{1,0:T(8,128)S(1)} %bitcast.87), channel_id=1, source_target_pairs={{0,1},{1,2},{2,3},{3,0},{4,5},{5,6},{6,7},{7,4},{8,9},{9,10},{10,1... | collective-permute-start | bytes 196616 | tf_op jit(solution)/shard_map/ppermute | solution.py:51
  99.6 14.8 %collective-permute-start.5 = (f32[128,128]{1,0:T(8,128)S(1)}, f32[128,128]{1,0:T(8,128)S(1)}, u32[]{:S(2)}, u32[]{:S(2)}) collective-permute-start(f32[128,128]{1,0:T(8,128)S(1)} %bitcast.86), channel_id=1, source_target_pairs={{0,2},{1,3},{2,0},{3,1},{4,6},{5,7},{6,4},{7,5},{8,10},{9,11},{10,... | collective-permute-start | bytes 196616 | tf_op jit(solution)/shard_map/ppermute | solution.py:51
  102.5 11.9 %collective-permute-start.6 = (f32[128,128]{1,0:T(8,128)S(1)}, f32[128,128]{1,0:T(8,128)S(1)}, u32[]{:S(2)}, u32[]{:S(2)}) collective-permute-start(f32[128,128]{1,0:T(8,128)S(1)} %bitcast.88), channel_id=1, source_target_pairs={{0,3},{1,0},{2,1},{3,2},{4,7},{5,4},{6,5},{7,6},{8,11},{9,8},{10,9... | collective-permute-start | bytes 196616 | tf_op jit(solution)/shard_map/ppermute | solution.py:51
  107.7 6.8 %collective-permute-start.11 = (f32[128,128]{1,0:T(8,128)S(1)}, f32[128,128]{1,0:T(8,128)S(1)}, u32[]{:S(2)}, u32[]{:S(2)}) collective-permute-start(f32[128,128]{1,0:T(8,128)S(1)} %bitcast.89), channel_id=1, source_target_pairs={{0,1},{1,2},{2,3},{3,0},{4,5},{5,6},{6,7},{7,4},{8,9},{9,10},{10,1... | collective-permute-start | bytes 196616 | tf_op jit(solution)/shard_map/ppermute | solution.py:51
  110.2 7.2 %collective-permute-start.12 = (f32[128,128]{1,0:T(8,128)S(1)}, f32[128,128]{1,0:T(8,128)S(1)}, u32[]{:S(2)}, u32[]{:S(2)}) collective-permute-start(f32[128,128]{1,0:T(8,128)S(1)} %bitcast.90), channel_id=1, source_target_pairs={{0,2},{1,3},{2,0},{3,1},{4,6},{5,7},{6,4},{7,5},{8,10},{9,11},{10,... | collective-permute-start | bytes 196616 | tf_op jit(solution)/shard_map/ppermute | solution.py:51
  113.0 4.8 %collective-permute-start.13 = (f32[128,128]{1,0:T(8,128)S(1)}, f32[128,128]{1,0:T(8,128)S(1)}, u32[]{:S(2)}, u32[]{:S(2)}) collective-permute-start(f32[128,128]{1,0:T(8,128)S(1)} %bitcast.91), channel_id=1, source_target_pairs={{0,3},{1,0},{2,1},{3,2},{4,7},{5,4},{6,5},{7,6},{8,11},{9,8},{10,9... | collective-permute-start | bytes 196616 | tf_op jit(solution)/shard_map/ppermute | solution.py:51

commit v9 on v8

--- a/solution.py
+++ b/solution.py
@@ -109,9 +109,15 @@
     pieces = lax.all_to_all(chunks, order, split_axis=0, concat_axis=0, tiled=True)
     pieces = with_layout_constraint(pieces, Layout((0, 1, 2)))
     own_degree = lax.psum(jnp.sum(adjacency, axis=1), "col")
-    all_degree = lax.all_gather(own_degree, ROW, axis=0, tiled=True)
-    col_degree = lax.dynamic_slice_in_dim(all_degree, lax.axis_index("col") * window, window, 0)
-    pieces, own_degree, col_degree = lax.optimization_barrier((pieces, own_degree, col_degree))
+    if core_major:
+        chip_degree = lax.all_gather(own_degree, "core", axis=0, tiled=True)
+        pieces, own_degree, chip_degree = lax.optimization_barrier((pieces, own_degree, chip_degree))
+        n = n_col
+        col_degree = lax.ppermute(chip_degree, ("chip", "col"), [(a * n + b, b * n + a) for a in range(n) for b in range(n)])
+    else:
+        all_degree = lax.all_gather(own_degree, ROW, axis=0, tiled=True)
+        col_degree = lax.dynamic_slice_in_dim(all_degree, lax.axis_index("col") * window, window, 0)
+        pieces, own_degree, col_degree = lax.optimization_barrier((pieces, own_degree, col_degree))
     outs = []
     if core_major:
         groups = n_core

time: 119 us -> 119 us (level)
  blocking collectives: 49.5 us -> 14.6 us
  waiting for transfers between devices: 8.25 us -> 40.1 us
  starting transfers between devices: 28.6 us -> 31.6 us
    all_gather x1, blocking collectives: 36.7 us -> 1.75 us  [body(): chip_degree = lax.all_gather(own_degree, 'core', axis=0, tiled=True)]
    all_to_all x1, waiting for transfers between devices: 0.01 us -> 31.3 us  [body(): lax.all_to_all(chunks, order, split_axis=0, concat_axis=0, tiled=True)]
    ppermute x6, starting transfers between devices: 7.16 us -> 11.9 us  [chip_reduce_scatter(): total = total + lax.ppermute(send, 'chip', perm)]
    ppermute x6, starting transfers between devices: 15.7 us -> 13.3 us  [col_reduce_scatter(): total = total + lax.ppermute(send, 'col', perm)]
  transfers between devices with their start and end apart: 15 -> 16, of which waited for: 7 -> 4; matrix products, arithmetic and copies ran while one was open for 13% -> 12% of each run, Pallas kernels for 0% -> 0%
where the time goes in v9:
time: 119 us; the launch traced here: 118 us
  waiting for transfers between devices  40.1 us (34%)
  starting transfers between devices  31.6 us (27%)
  matrix products  17.5 us (15%)
  blocking collectives  14.6 us (12%)
  local copies, waits for them, and re-layouts  7.56 us (6%)
  Pallas kernels  3.72 us (3%)
  other arithmetic  2.75 us (2%)
    all_to_all x1, waiting for transfers between devices, body(): lax.all_to_all(chunks, order, split_axis=0, concat_axis=0, tiled=True)  31.3 us
    dot_general x4, matrix products, inner_rows(): lax.dot_general(left, right, (((1,), (1,)), ((), ())), precision=lax.Prec...  17.5 us
    ppermute x6, starting transfers between devices, col_reduce_scatter(): total = total + lax.ppermute(send, 'col', perm)  13.3 us
    psum x1, blocking collectives, body(): own_degree = lax.psum(jnp.sum(adjacency, axis=1), 'col')  12.8 us
    ppermute x6, starting transfers between devices, chip_reduce_scatter(): total = total + lax.ppermute(send, 'chip', perm)  11.9 us
    ppermute x6, waiting for transfers between devices, chip_reduce_scatter(): total = total + lax.ppermute(send, 'chip', perm)  5.36 us
    all_to_all x1, starting transfers between devices, body(): lax.all_to_all(chunks, order, split_axis=0, concat_axis=0, tiled=True)  5.17 us
    pallas_call x1, Pallas kernels, column_chunks(): pl.pallas_call(_copy_blocks, grid=(n_chunks // per_step,), in_specs=[pl.B...  3.72 us
  transfers between devices with their start and end apart: 16, of which 4 were waited for; matrix products, arithmetic and copies ran while one was open for 12% of the time, Pallas kernels for 0%

profile of v9, /device:TPU:0, one launch (start us, length us, event | category | flops | bytes accessed | tf_op | source)
XLA Modules:
  0.0 118.2 jit_solution(11335710237430025578)
XLA Ops:
  0.0 3.7 %shard_map.17 = f32[8,128,1024]{2,1,0:T(8,128)} custom-call(f32[128,8192]{1,0:T(8,128)} %block_ref.1), custom_call_target="tpu_custom_call" | custom-call | tf_op jit(solution)/shard_map/pallas_call | solution.py:32
  3.7 5.2 %all-to-all-start = ((f32[8,128,1024]{2,1,0:T(8,128)}), f32[8,128,1024]{2,1,0:T(8,128)}, u32[]{:S(2)}, u32[]{:S(2)}) async-start(f32[8,128,1024]{2,1,0:T(8,128)} %shard_map.17), calls=%async_computation | async-start | bytes 8388608 | tf_op jit(solution)/shard_map/all_to_all | solution.py:109
  8.9 2.5 %reduce_sum.9 = f32[128]{0:T(128)S(1)} reduce(f32[128,8192]{1,0:T(8,128)} %block_ref.1, f32[]{:T(128)} %constant.93.clone.1), dimensions={1}, to_apply=%region_0.0 | reduce | flops 1048448 | bytes 4194820 | tf_op jit(solution)/shard_map/reduce_sum | solution.py:111
  11.4 12.8 %psum.7 = f32[128]{0:T(128)S(1)} all-reduce(f32[128]{0:T(128)S(1)} %reduce_sum.9), channel_id=1, replica_groups=mesh['chip'=4,'core'=2,'col'=4] {'col'}, use_global_device_ids=true, to_apply=%region_1.0 | all-reduce | flops 128 | bytes 1024 | tf_op jit(solution)/shard_map/psum | solution.py:111
  24.2 1.8 %all-gather = f32[2,1,128]{2,1,0:T(1,128)S(1)} all-gather(f32[1,1,128]{2,1,0:T(1,128)S(1)} %bitcast.93), channel_id=1, replica_groups=mesh['chip'=4,'core'=2,'col'=4] {'core'}, dimensions={0}, use_global_device_ids=true | all-gather | bytes 1536 | tf_op jit(solution)/shard_map/all_gather | solution.py:113
  26.0 31.3 %all-to-all-done = f32[8,128,1024]{2,1,0:T(8,128)} async-done(((f32[8,128,1024]{2,1,0:T(8,128)}), f32[8,128,1024]{2,1,0:T(8,128)}, u32[]{:S(2)}, u32[]{:S(2)}) %all-to-all-start) | async-done | bytes 4194336 | tf_op jit(solution)/shard_map/all_to_all | solution.py:109
  57.3 2.5 %fusion.33 = (f32[4,128,1024]{2,1,0:T(8,128)S(1)}, f32[4,128,1024]{2,1,0:T(8,128)S(1)}) fusion(f32[8,128,1024]{2,1,0:T(8,128)} %all-to-all-done), kind=kLoop, calls=%fused_computation.51 | loop fusion | bytes 8388608 | tf_op jit(solution)/shard_map/slice | solution.py:128
  59.8 0.0 copy-start
  59.8 5.3 %fusion.2 = f32[512,512]{1,0:T(8,128)} fusion(f32[512,1024]{1,0:T(8,128)S(1)} %bitcast.77, f32[2,512,1024]{2,1,0:T(8,128)} %bitcast.2, s32[]{:T(128)S(6)} %select_n.72), kind=kOutput, calls=%fused_computation.2 | convolution fusion | flops 1610612736 | bytes 5242884 | tf_op jit(solution)/shard_map/dot_general | solution.py:13
  65.1 0.6 collective-permute-start
  65.7 4.4 %fusion = f32[512,512]{1,0:T(8,128)} fusion(f32[512,1024]{1,0:T(8,128)S(1)} %bitcast.75, f32[2,512,1024]{2,1,0:T(8,128)} %bitcast.2, s32[]{:T(128)S(6)} %select_n.72), kind=kOutput, calls=%fused_computation | convolution fusion | flops 1610612736 | bytes 5242884 | tf_op jit(solution)/shard_map/dot_general | solution.py:13
  70.1 0.0 collective-permute-start.7
  70.1 0.0 collective-permute-done
  70.1 4.4 %fusion.12 = f32[512,512]{1,0:T(8,128)S(1)} fusion(f32[512,512]{1,0:T(8,128)} %collective-permute-done, f32[512,1024]{1,0:T(8,128)} %bitcast.78, f32[2,512,1024]{2,1,0:T(8,128)} %bitcast.2, s32[]{:T(128)S(6)} %select_n.70), kind=kOutput, calls=%fused_computation.12 | convolution fusion | flops 1610874880 | bytes 6291460 | tf_op jit(solution)/shard_map/dot_general | solution.py:13
  74.5 0.0 collective-permute-done.7
  74.5 3.5 %fusion.15 = f32[512,512]{1,0:T(8,128)S(1)} fusion(f32[512,512]{1,0:T(8,128)S(1)} %collective-permute-done.7, f32[512,1024]{1,0:T(8,128)S(1)} %bitcast.76, f32[2,512,1024]{2,1,0:T(8,128)} %bitcast.2, s32[]{:T(128)S(6)} %select_n.70), kind=kOutput, calls=%fused_computation.13 | convolution fusion | flops 1610874880 | bytes 6291460 | tf_op jit(solution)/shard_map/dot_general | solution.py:13
  78.0 0.0 slice-start
  78.0 0.2 constant_dynamic-slice_fusion.7
  78.2 0.8 copy.43
  79.0 1.2 collective-permute-start.1
  80.2 0.1 copy.44
  80.3 0.7 collective-permute-start.2
  81.1 0.1 copy.45
  81.2 1.7 %collective-permute-start.3 = (f32[128,512]{0,1:T(8,128)S(1)}, f32[128,512]{0,1:T(8,128)S(1)}, u32[]{:S(2)}, u32[]{:S(2)}) collective-permute-start(f32[128,512]{0,1:T(8,128)S(1)} %bitcast.83), channel_id=1, source_target_pairs={{0,24},{8,16},{16,8},{24,0},{1,25},{9,17},{17,9},{25,1},{2,26},{10... | collective-permute-start | bytes 786440 | tf_op jit(solution)/shard_map/ppermute | solution.py:95
  82.9 0.1 copy.61
  83.0 0.7 collective-permute-start.14
  83.7 0.1 copy.42
  83.8 0.8 copy.53
  84.6 8.2 %collective-permute-start.10 = (f32[128,512]{0,1:T(8,128)}, f32[128,512]{0,1:T(8,128)S(1)}, u32[]{:S(2)}, u32[]{:S(2)}) collective-permute-start(f32[128,512]{0,1:T(8,128)} %bitcast.22), channel_id=1, source_target_pairs={{0,24},{8,16},{16,8},{24,0},{1,25},{9,17},{17,9},{25,1},{2,26},{10... | collective-permute-start | bytes 786440 | tf_op jit(solution)/shard_map/ppermute | solution.py:95
  92.8 0.8 copy.51
  93.6 0.1 copy.52
  93.8 0.1 copy.50
  93.9 0.0 collective-permute-done.1
  93.9 0.1 collective-permute-start.8
  94.0 5.3 %collective-permute-done.2 = f32[128,512]{0,1:T(8,128)S(1)} collective-permute-done((f32[128,512]{0,1:T(8,128)S(1)}, f32[128,512]{0,1:T(8,128)S(1)}, u32[]{:S(2)}, u32[]{:S(2)}) %collective-permute-start.2) | collective-permute-done | bytes 262176 | tf_op jit(solution)/shard_map/ppermute | solution.py:95
  99.3 0.0 collective-permute-start.9
  99.3 0.0 collective-permute-done.3
  99.4 0.1 copy.47
  99.5 2.4 %collective-permute-start.4 = (f32[128,128]{1,0:T(8,128)S(1)}, f32[128,128]{1,0:T(8,128)S(1)}, u32[]{:S(2)}, u32[]{:S(2)}) collective-permute-start(f32[128,128]{1,0:T(8,128)S(1)} %bitcast.89), channel_id=1, source_target_pairs={{0,1},{1,2},{2,3},{3,0},{4,5},{5,6},{6,7},{7,4},{8,9},{9,10},{10,1... | collective-permute-start | bytes 196616 | tf_op jit(solution)/shard_map/ppermute | solution.py:51
  101.9 0.1 copy.48
  102.0 0.1 copy.49
  102.1 0.1 copy.46
  102.2 0.0 collective-permute-done.10
  102.2 2.6 %collective-permute-start.5 = (f32[128,128]{1,0:T(8,128)S(1)}, f32[128,128]{1,0:T(8,128)S(1)}, u32[]{:S(2)}, u32[]{:S(2)}) collective-permute-start(f32[128,128]{1,0:T(8,128)S(1)} %bitcast.88), channel_id=1, source_target_pairs={{0,2},{1,3},{2,0},{3,1},{4,6},{5,7},{6,4},{7,5},{8,10},{9,11},{10,... | collective-permute-start | bytes 196616 | tf_op jit(solution)/shard_map/ppermute | solution.py:51
  104.9 0.0 collective-permute-done.8
  104.9 4.3 %collective-permute-start.6 = (f32[128,128]{1,0:T(8,128)S(1)}, f32[128,128]{1,0:T(8,128)S(1)}, u32[]{:S(2)}, u32[]{:S(2)}) collective-permute-start(f32[128,128]{1,0:T(8,128)S(1)} %bitcast.87), channel_id=1, source_target_pairs={{0,3},{1,0},{2,1},{3,2},{4,7},{5,4},{6,5},{7,6},{8,11},{9,8},{10,9... | collective-permute-start | bytes 196616 | tf_op jit(solution)/shard_map/ppermute | solution.py:51
  109.2 0.0 collective-permute-done.9
  109.3 0.1 copy.55
  109.4 0.1 collective-permute-start.11
  109.4 0.1 copy.56
  109.5 0.1 copy.57
  109.6 0.1 copy.54
  109.7 0.0 collective-permute-done.4
  109.7 1.5 %collective-permute-start.12 = (f32[128,128]{1,0:T(8,128)S(1)}, f32[128,128]{1,0:T(8,128)S(1)}, u32[]{:S(2)}, u32[]{:S(2)}) collective-permute-start(f32[128,128]{1,0:T(8,128)S(1)} %bitcast.92), channel_id=1, source_target_pairs={{0,2},{1,3},{2,0},{3,1},{4,6},{5,7},{6,4},{7,5},{8,10},{9,11},{10,... | collective-permute-start | bytes 196616 | tf_op jit(solution)/shard_map/ppermute | solution.py:51
  111.2 0.0 collective-permute-done.5
  111.2 2.5 %collective-permute-start.13 = (f32[128,128]{1,0:T(8,128)S(1)}, f32[128,128]{1,0:T(8,128)S(1)}, u32[]{:S(2)}, u32[]{:S(2)}) collective-permute-start(f32[128,128]{1,0:T(8,128)S(1)} %bitcast.91), channel_id=1, source_target_pairs={{0,3},{1,0},{2,1},{3,2},{4,7},{5,4},{6,5},{7,6},{8,11},{9,8},{10,9... | collective-permute-start | bytes 196616 | tf_op jit(solution)/shard_map/ppermute | solution.py:51
  113.7 0.0 collective-permute-done.6
  113.7 2.2 %collective-permute-done.11 = f32[128,128]{1,0:T(8,128)S(1)} collective-permute-done((f32[128,128]{1,0:T(8,128)S(1)}, f32[128,128]{1,0:T(8,128)S(1)}, u32[]{:S(2)}, u32[]{:S(2)}) %collective-permute-start.11) | collective-permute-done | bytes 65568 | tf_op jit(solution)/shard_map/ppermute | solution.py:51
  115.9 1.3 %collective-permute-done.12 = f32[128,128]{1,0:T(8,128)S(1)} collective-permute-done((f32[128,128]{1,0:T(8,128)S(1)}, f32[128,128]{1,0:T(8,128)S(1)}, u32[]{:S(2)}, u32[]{:S(2)}) %collective-permute-start.12) | collective-permute-done | bytes 65568 | tf_op jit(solution)/shard_map/ppermute | solution.py:51
  117.2 0.0 collective-permute-done.13
  117.2 0.1 copy.58
  117.3 0.0 collective-permute-done.14
  117.3 0.1 fusion.22
  117.4 0.8 copy.60
  (9 shorter events, 0.2 us)
Async XLA Ops:
  3.7 53.6 %all-to-all-start = ((f32[8,128,1024]{2,1,0:T(8,128)}), f32[8,128,1024]{2,1,0:T(8,128)}, u32[]{:S(2)}, u32[]{:S(2)}) async-start(f32[8,128,1024]{2,1,0:T(8,128)} %shard_map.17), calls=%async_computation | async-start | bytes 8388608 | tf_op jit(solution)/shard_map/all_to_all | solution.py:109
  59.8 5.3 %copy-start = (f32[4,128,1024]{2,1,0:T(8,128)}, f32[4,128,1024]{2,1,0:T(8,128)S(1)}, u32[]{:S(2)}) copy-start(f32[4,128,1024]{2,1,0:T(8,128)S(1)} %get-tuple-element.11) | copy-start | bytes 6291460
  65.1 5.0 %collective-permute-start = (f32[512,512]{1,0:T(8,128)}, f32[512,512]{1,0:T(8,128)}, u32[]{:S(2)}, u32[]{:S(2)}) collective-permute-start(f32[512,512]{1,0:T(8,128)} %fusion.2), channel_id=1, source_target_pairs={{0,4},{4,0},{1,5},{5,1},{2,6},{6,2},{3,7},{7,3},{8,12},{12,8},{9,1... | collective-permute-start | bytes 3145736 | tf_op jit(solution)/shard_map/ppermute | solution.py:133
  70.1 4.4 %collective-permute-start.7 = (f32[512,512]{1,0:T(8,128)}, f32[512,512]{1,0:T(8,128)S(1)}, u32[]{:S(2)}, u32[]{:S(2)}) collective-permute-start(f32[512,512]{1,0:T(8,128)} %fusion), channel_id=1, source_target_pairs={{0,4},{4,0},{1,5},{5,1},{2,6},{6,2},{3,7},{7,3},{8,12},{12,8},{9,1... | collective-permute-start | bytes 3145736 | tf_op jit(solution)/shard_map/ppermute | solution.py:133
  78.0 4.9 %slice-start = ((f32[128,8192]{1,0:T(8,128)}), f32[128,256]{1,0:T(8,128)S(1)}, s32[]{:S(2)}) async-start(f32[128,8192]{1,0:T(8,128)} %block_ref.1), calls=%async_computation.1 | async-start | bytes 262144 | tf_op jit(solution)/shard_map/slice | solution.py:147
  79.0 14.9 %collective-permute-start.1 = (f32[128,512]{0,1:T(8,128)}, f32[128,512]{0,1:T(8,128)S(1)}, u32[]{:S(2)}, u32[]{:S(2)}) collective-permute-start(f32[128,512]{0,1:T(8,128)} %bitcast.8), channel_id=1, source_target_pairs={{0,8},{8,0},{16,24},{24,16},{1,9},{9,1},{17,25},{25,17},{2,10},{10... | collective-permute-start | bytes 786440 | tf_op jit(solution)/shard_map/ppermute | solution.py:95
  80.3 19.0 %collective-permute-start.2 = (f32[128,512]{0,1:T(8,128)S(1)}, f32[128,512]{0,1:T(8,128)S(1)}, u32[]{:S(2)}, u32[]{:S(2)}) collective-permute-start(f32[128,512]{0,1:T(8,128)S(1)} %bitcast.84), channel_id=1, source_target_pairs={{0,16},{8,24},{16,0},{24,8},{1,17},{9,25},{17,1},{25,9},{2,18},{10... | collective-permute-start | bytes 786440 | tf_op jit(solution)/shard_map/ppermute | solution.py:95
  81.2 18.2 %collective-permute-start.3 = (f32[128,512]{0,1:T(8,128)S(1)}, f32[128,512]{0,1:T(8,128)S(1)}, u32[]{:S(2)}, u32[]{:S(2)}) collective-permute-start(f32[128,512]{0,1:T(8,128)S(1)} %bitcast.83), channel_id=1, source_target_pairs={{0,24},{8,16},{16,8},{24,0},{1,25},{9,17},{17,9},{25,1},{2,26},{10... | collective-permute-start | bytes 786440 | tf_op jit(solution)/shard_map/ppermute | solution.py:95
  83.0 34.3 %collective-permute-start.14 = (f32[256]{0:T(256)S(1)}, f32[256]{0:T(256)S(1)}, u32[]{:S(2)}, u32[]{:S(2)}) collective-permute-start(f32[256]{0:T(256)S(1)} %bitcast.94), channel_id=1, source_target_pairs={{0,0},{1,8},{2,16},{3,24},{8,1},{9,9},{10,17},{11,25},{16,2},{17,1... | collective-permute-start | bytes 3080 | tf_op jit(solution)/shard_map/ppermute | solution.py:116
  84.6 17.6 %collective-permute-start.10 = (f32[128,512]{0,1:T(8,128)}, f32[128,512]{0,1:T(8,128)S(1)}, u32[]{:S(2)}, u32[]{:S(2)}) collective-permute-start(f32[128,512]{0,1:T(8,128)} %bitcast.22), channel_id=1, source_target_pairs={{0,24},{8,16},{16,8},{24,0},{1,25},{9,17},{17,9},{25,1},{2,26},{10... | collective-permute-start | bytes 786440 | tf_op jit(solution)/shard_map/ppermute | solution.py:95
  93.9 10.9 %collective-permute-start.8 = (f32[128,512]{0,1:T(8,128)}, f32[128,512]{0,1:T(8,128)S(1)}, u32[]{:S(2)}, u32[]{:S(2)}) collective-permute-start(f32[128,512]{0,1:T(8,128)} %bitcast.86), channel_id=1, source_target_pairs={{0,8},{8,0},{16,24},{24,16},{1,9},{9,1},{17,25},{25,17},{2,10},{10... | collective-permute-start | bytes 786440 | tf_op jit(solution)/shard_map/ppermute | solution.py:95
  99.3 9.8 %collective-permute-start.9 = (f32[128,512]{0,1:T(8,128)S(1)}, f32[128,512]{0,1:T(8,128)S(1)}, u32[]{:S(2)}, u32[]{:S(2)}) collective-permute-start(f32[128,512]{0,1:T(8,128)S(1)} %bitcast.85), channel_id=1, source_target_pairs={{0,16},{8,24},{16,0},{24,8},{1,17},{9,25},{17,1},{25,9},{2,18},{10... | collective-permute-start | bytes 786440 | tf_op jit(solution)/shard_map/ppermute | solution.py:95
  99.5 10.2 %collective-permute-start.4 = (f32[128,128]{1,0:T(8,128)S(1)}, f32[128,128]{1,0:T(8,128)S(1)}, u32[]{:S(2)}, u32[]{:S(2)}) collective-permute-start(f32[128,128]{1,0:T(8,128)S(1)} %bitcast.89), channel_id=1, source_target_pairs={{0,1},{1,2},{2,3},{3,0},{4,5},{5,6},{6,7},{7,4},{8,9},{9,10},{10,1... | collective-permute-start | bytes 196616 | tf_op jit(solution)/shard_map/ppermute | solution.py:51
  102.2 9.0 %collective-permute-start.5 = (f32[128,128]{1,0:T(8,128)S(1)}, f32[128,128]{1,0:T(8,128)S(1)}, u32[]{:S(2)}, u32[]{:S(2)}) collective-permute-start(f32[128,128]{1,0:T(8,128)S(1)} %bitcast.88), channel_id=1, source_target_pairs={{0,2},{1,3},{2,0},{3,1},{4,6},{5,7},{6,4},{7,5},{8,10},{9,11},{10,... | collective-permute-start | bytes 196616 | tf_op jit(solution)/shard_map/ppermute | solution.py:51
  104.9 8.8 %collective-permute-start.6 = (f32[128,128]{1,0:T(8,128)S(1)}, f32[128,128]{1,0:T(8,128)S(1)}, u32[]{:S(2)}, u32[]{:S(2)}) collective-permute-start(f32[128,128]{1,0:T(8,128)S(1)} %bitcast.87), channel_id=1, source_target_pairs={{0,3},{1,0},{2,1},{3,2},{4,7},{5,4},{6,5},{7,6},{8,11},{9,8},{10,9... | collective-permute-start | bytes 196616 | tf_op jit(solution)/shard_map/ppermute | solution.py:51
  109.4 6.5 %collective-permute-start.11 = (f32[128,128]{1,0:T(8,128)S(1)}, f32[128,128]{1,0:T(8,128)S(1)}, u32[]{:S(2)}, u32[]{:S(2)}) collective-permute-start(f32[128,128]{1,0:T(8,128)S(1)} %bitcast.90), channel_id=1, source_target_pairs={{0,1},{1,2},{2,3},{3,0},{4,5},{5,6},{6,7},{7,4},{8,9},{9,10},{10,1... | collective-permute-start | bytes 196616 | tf_op jit(solution)/shard_map/ppermute | solution.py:51
  109.7 7.4 %collective-permute-start.12 = (f32[128,128]{1,0:T(8,128)S(1)}, f32[128,128]{1,0:T(8,128)S(1)}, u32[]{:S(2)}, u32[]{:S(2)}) collective-permute-start(f32[128,128]{1,0:T(8,128)S(1)} %bitcast.92), channel_id=1, source_target_pairs={{0,2},{1,3},{2,0},{3,1},{4,6},{5,7},{6,4},{7,5},{8,10},{9,11},{10,... | collective-permute-start | bytes 196616 | tf_op jit(solution)/shard_map/ppermute | solution.py:51
  111.2 6.0 %collective-permute-start.13 = (f32[128,128]{1,0:T(8,128)S(1)}, f32[128,128]{1,0:T(8,128)S(1)}, u32[]{:S(2)}, u32[]{:S(2)}) collective-permute-start(f32[128,128]{1,0:T(8,128)S(1)} %bitcast.91), channel_id=1, source_target_pairs={{0,3},{1,0},{2,1},{3,2},{4,7},{5,4},{6,5},{7,6},{8,11},{9,8},{10,9... | collective-permute-start | bytes 196616 | tf_op jit(solution)/shard_map/ppermute | solution.py:51

commit v10 on v9

--- a/solution.py
+++ b/solution.py
@@ -124,17 +124,17 @@
         flat = pieces.reshape(n_row * strip_rows, piece)
         by_core = pieces.reshape(n_core, n_col * strip_rows, piece)
         me = lax.axis_index("core")
+        on_chip = None
+        for s in range(1, n_core):
+            left = lax.dynamic_index_in_dim(by_core, (me + s) % n_core, 0, keepdims=False)
+            perm = [(i, (i + s) % n_core) for i in range(n_core)]
+            got = lax.ppermute(inner_rows(left, flat), "core", perm)
+            on_chip = got if on_chip is None else on_chip + got
+        left = lax.dynamic_index_in_dim(by_core, me, 0, keepdims=False)
+        on_chip = inner_rows(left, flat) + on_chip
+        width = on_chip.shape[1] // groups
         for g in range(groups):
-            right = by_core[g]
-            on_chip = None
-            for s in range(1, n_core):
-                left = lax.dynamic_index_in_dim(by_core, (me + s) % n_core, 0, keepdims=False)
-                perm = [(i, (i + s) % n_core) for i in range(n_core)]
-                got = lax.ppermute(inner_rows(left, right), "core", perm)
-                on_chip = got if on_chip is None else on_chip + got
-            left = lax.dynamic_index_in_dim(by_core, me, 0, keepdims=False)
-            on_chip = inner_rows(left, right) + on_chip
-            outs.append(col_reduce_scatter(chip_reduce_scatter(on_chip)))
+            outs.append(col_reduce_scatter(chip_reduce_scatter(on_chip[:, g * width : (g + 1) * width])))
     else:
         groups = 2 if window % 256 == 0 else 1
         sub = window // groups

time: 119 us -> 118 us (level)
  waiting for transfers between devices: 40.1 us -> 43.9 us
  matrix products: 17.5 us -> 14.5 us
  local copies, waits for them, and re-layouts: 7.56 us -> 5.21 us
    ppermute x2 -> x1, waiting for transfers between devices: 0.01 us -> 4 us  [body(): got = lax.ppermute(inner_rows(left, flat), 'core', perm)]
    dot_general x4 -> x2, matrix products: 17.5 us -> 14.5 us  [inner_rows(): lax.dot_general(left, right, (((1,), (1,)), ((), ())), precision=lax.Prec...]
    slice x1, local copies, waits for them, and re-layouts: 2.53 us -> 0.19 us  [body(): on_chip[:, g * width:(g + 1) * width]]
  transfers between devices with their start and end apart: 16 -> 15, of which waited for: 4 -> 6; matrix products, arithmetic and copies ran while one was open for 12% -> 5% of each run, Pallas kernels for 0% -> 0%
where the time goes in v10:
time: 118 us
  waiting for transfers between devices  43.9 us (37%)
  starting transfers between devices  32.5 us (28%)
  blocking collectives  14.6 us (12%)
  matrix products  14.5 us (12%)
  local copies, waits for them, and re-layouts  5.21 us (4%)
  Pallas kernels  3.71 us (3%)
  other arithmetic  2.75 us (2%)
    all_to_all x1, waiting for transfers between devices, body(): lax.all_to_all(chunks, order, split_axis=0, concat_axis=0, tiled=True)  31.3 us
    dot_general x2, matrix products, inner_rows(): lax.dot_general(left, right, (((1,), (1,)), ((), ())), precision=lax.Prec...  14.5 us
    ppermute x6, starting transfers between devices, col_reduce_scatter(): total = total + lax.ppermute(send, 'col', perm)  13.8 us
    psum x1, blocking collectives, body(): own_degree = lax.psum(jnp.sum(adjacency, axis=1), 'col')  12.8 us
    ppermute x6, starting transfers between devices, chip_reduce_scatter(): total = total + lax.ppermute(send, 'chip', perm)  12.3 us
    all_to_all x1, starting transfers between devices, body(): lax.all_to_all(chunks, order, split_axis=0, concat_axis=0, tiled=True)  5.17 us
    ppermute x6, waiting for transfers between devices, chip_reduce_scatter(): total = total + lax.ppermute(send, 'chip', perm)  4.38 us
    ppermute x6, waiting for transfers between devices, col_reduce_scatter(): total = total + lax.ppermute(send, 'col', perm)  4.23 us
  transfers between devices with their start and end apart: 15, of which 6 were waited for; matrix products, arithmetic and copies ran while one was open for 5% of the time, Pallas kernels for 0%

profile of v10, /device:TPU:0, one launch (start us, length us, event | category | flops | bytes accessed | tf_op | source)
XLA Modules:
  0.0 117.5 jit_solution(11789110711388018343)
XLA Ops:
  0.0 3.7 %shard_map.17 = f32[8,128,1024]{2,1,0:T(8,128)} custom-call(f32[128,8192]{1,0:T(8,128)} %block_ref.1), custom_call_target="tpu_custom_call" | custom-call | tf_op jit(solution)/shard_map/pallas_call | solution.py:32
  3.7 5.2 %all-to-all-start = ((f32[8,128,1024]{2,1,0:T(8,128)}), f32[8,128,1024]{2,1,0:T(8,128)}, u32[]{:S(2)}, u32[]{:S(2)}) async-start(f32[8,128,1024]{2,1,0:T(8,128)} %shard_map.17), calls=%async_computation | async-start | bytes 8388608 | tf_op jit(solution)/shard_map/all_to_all | solution.py:109
  8.9 2.5 %reduce_sum.9 = f32[128]{0:T(128)S(1)} reduce(f32[128,8192]{1,0:T(8,128)} %block_ref.1, f32[]{:T(128)} %constant.87.clone.1), dimensions={1}, to_apply=%region_0.0 | reduce | flops 1048448 | bytes 4194820 | tf_op jit(solution)/shard_map/reduce_sum | solution.py:111
  11.4 12.8 %psum.7 = f32[128]{0:T(128)S(1)} all-reduce(f32[128]{0:T(128)S(1)} %reduce_sum.9), channel_id=1, replica_groups=mesh['chip'=4,'core'=2,'col'=4] {'col'}, use_global_device_ids=true, to_apply=%region_1.0 | all-reduce | flops 128 | bytes 1024 | tf_op jit(solution)/shard_map/psum | solution.py:111
  24.2 1.8 %all-gather = f32[2,1,128]{2,1,0:T(1,128)S(1)} all-gather(f32[1,1,128]{2,1,0:T(1,128)S(1)} %bitcast.80), channel_id=1, replica_groups=mesh['chip'=4,'core'=2,'col'=4] {'core'}, dimensions={0}, use_global_device_ids=true | all-gather | bytes 1536 | tf_op jit(solution)/shard_map/all_gather | solution.py:113
  26.0 31.3 %all-to-all-done = f32[8,128,1024]{2,1,0:T(8,128)} async-done(((f32[8,128,1024]{2,1,0:T(8,128)}), f32[8,128,1024]{2,1,0:T(8,128)}, u32[]{:S(2)}, u32[]{:S(2)}) %all-to-all-start) | async-done | bytes 4194336 | tf_op jit(solution)/shard_map/all_to_all | solution.py:109
  57.3 7.7 %fusion = f32[512,1024]{1,0:T(8,128)} fusion(f32[1024,1024]{1,0:T(8,128)} %bitcast.4, f32[2,512,1024]{2,1,0:T(8,128)} %bitcast.2, s32[]{:T(128)S(6)} %select_n.68), kind=kOutput, calls=%fused_computation | convolution fusion | flops 3221225472 | bytes 8388612 | tf_op jit(solution)/shard_map/dot_general | solution.py:13
  65.0 0.6 collective-permute-start
  65.6 4.0 %collective-permute-done = f32[512,1024]{1,0:T(8,128)S(1)} collective-permute-done((f32[512,1024]{1,0:T(8,128)}, f32[512,1024]{1,0:T(8,128)S(1)}, u32[]{:S(2)}, u32[]{:S(2)}) %collective-permute-start) | collective-permute-done | bytes 2097184 | tf_op jit(solution)/shard_map/ppermute | solution.py:131
  69.6 6.8 %fusion.6 = f32[512,1024]{1,0:T(8,128)S(1)} fusion(f32[512,1024]{1,0:T(8,128)S(1)} %collective-permute-done, f32[1024,1024]{1,0:T(8,128)} %bitcast.4, f32[2,512,1024]{2,1,0:T(8,128)} %bitcast.2, s32[]{:T(128)S(6)} %select_n.66), kind=kOutput, calls=%fused_computation.6 | convolution fusion | flops 3221749760 | bytes 10485764 | tf_op jit(solution)/shard_map/dot_general | solution.py:13
  76.4 0.0 slice-start
  76.4 0.2 fusion.22
  76.6 0.2 constant_dynamic-slice_fusion.7
  76.8 0.8 copy.43
  77.7 1.0 collective-permute-start.1
  78.7 0.1 copy.44
  78.8 0.7 collective-permute-start.2
  79.6 0.1 copy.45
  79.7 1.8 %collective-permute-start.3 = (f32[128,512]{0,1:T(8,128)S(1)}, f32[128,512]{0,1:T(8,128)S(1)}, u32[]{:S(2)}, u32[]{:S(2)}) collective-permute-start(f32[128,512]{0,1:T(8,128)S(1)} %bitcast.70), channel_id=1, source_target_pairs={{0,24},{8,16},{16,8},{24,0},{1,25},{9,17},{17,9},{25,1},{2,26},{10... | collective-permute-start | bytes 786440 | tf_op jit(solution)/shard_map/ppermute | solution.py:95
  81.5 0.0 slice-done
  81.5 0.1 copy.61
  81.6 0.7 collective-permute-start.13
  82.3 0.1 copy.42
  82.4 0.8 copy.51
  83.3 5.1 %collective-permute-start.7 = (f32[128,512]{0,1:T(8,128)}, f32[128,512]{0,1:T(8,128)S(1)}, u32[]{:S(2)}, u32[]{:S(2)}) collective-permute-start(f32[128,512]{0,1:T(8,128)} %bitcast.19), channel_id=1, source_target_pairs={{0,8},{8,0},{16,24},{24,16},{1,9},{9,1},{17,25},{25,17},{2,10},{10... | collective-permute-start | bytes 786440 | tf_op jit(solution)/shard_map/ppermute | solution.py:95
  88.4 0.8 copy.52
  89.2 0.1 copy.53
  89.3 0.1 copy.50
  89.5 0.0 collective-permute-done.1
  89.5 3.5 %collective-permute-start.8 = (f32[128,512]{0,1:T(8,128)}, f32[128,512]{0,1:T(8,128)S(1)}, u32[]{:S(2)}, u32[]{:S(2)}) collective-permute-start(f32[128,512]{0,1:T(8,128)} %bitcast.73), channel_id=1, source_target_pairs={{0,16},{8,24},{16,0},{24,8},{1,17},{9,25},{17,1},{25,9},{2,18},{10... | collective-permute-start | bytes 786440 | tf_op jit(solution)/shard_map/ppermute | solution.py:95
  93.0 0.0 collective-permute-done.2
  93.0 0.0 collective-permute-start.9
  93.0 0.0 collective-permute-done.3
  93.0 0.1 fusion.12
  93.1 0.1 copy.47
  93.2 2.6 %collective-permute-start.4 = (f32[128,128]{1,0:T(8,128)S(1)}, f32[128,128]{1,0:T(8,128)S(1)}, u32[]{:S(2)}, u32[]{:S(2)}) collective-permute-start(f32[128,128]{1,0:T(8,128)S(1)} %bitcast.76), channel_id=1, source_target_pairs={{0,1},{1,2},{2,3},{3,0},{4,5},{5,6},{6,7},{7,4},{8,9},{9,10},{10,1... | collective-permute-start | bytes 196616 | tf_op jit(solution)/shard_map/ppermute | solution.py:51
  95.8 0.1 copy.48
  95.9 0.1 copy.49
  96.0 0.1 copy.46
  96.1 2.2 %collective-permute-done.7 = f32[128,512]{0,1:T(8,128)S(1)} collective-permute-done((f32[128,512]{0,1:T(8,128)}, f32[128,512]{0,1:T(8,128)S(1)}, u32[]{:S(2)}, u32[]{:S(2)}) %collective-permute-start.7) | collective-permute-done | bytes 262176 | tf_op jit(solution)/shard_map/ppermute | solution.py:95
  98.3 3.4 %collective-permute-start.5 = (f32[128,128]{1,0:T(8,128)S(1)}, f32[128,128]{1,0:T(8,128)S(1)}, u32[]{:S(2)}, u32[]{:S(2)}) collective-permute-start(f32[128,128]{1,0:T(8,128)S(1)} %bitcast.75), channel_id=1, source_target_pairs={{0,2},{1,3},{2,0},{3,1},{4,6},{5,7},{6,4},{7,5},{8,10},{9,11},{10,... | collective-permute-start | bytes 196616 | tf_op jit(solution)/shard_map/ppermute | solution.py:51
  101.7 2.2 %collective-permute-done.8 = f32[128,512]{0,1:T(8,128)S(1)} collective-permute-done((f32[128,512]{0,1:T(8,128)}, f32[128,512]{0,1:T(8,128)S(1)}, u32[]{:S(2)}, u32[]{:S(2)}) %collective-permute-start.8) | collective-permute-done | bytes 262176 | tf_op jit(solution)/shard_map/ppermute | solution.py:95
  103.9 3.8 %collective-permute-start.6 = (f32[128,128]{1,0:T(8,128)S(1)}, f32[128,128]{1,0:T(8,128)S(1)}, u32[]{:S(2)}, u32[]{:S(2)}) collective-permute-start(f32[128,128]{1,0:T(8,128)S(1)} %bitcast.74), channel_id=1, source_target_pairs={{0,3},{1,0},{2,1},{3,2},{4,7},{5,4},{6,5},{7,6},{8,11},{9,8},{10,9... | collective-permute-start | bytes 196616 | tf_op jit(solution)/shard_map/ppermute | solution.py:51
  107.7 0.0 collective-permute-done.9
  107.8 0.1 copy.55
  107.9 0.1 collective-permute-start.10
  108.0 0.1 copy.56
  108.1 0.1 copy.57
  108.2 0.1 copy.54
  108.3 0.0 collective-permute-done.4
  108.3 1.1 collective-permute-start.11
  109.4 0.0 collective-permute-done.5
  109.4 2.9 %collective-permute-start.12 = (f32[128,128]{1,0:T(8,128)S(1)}, f32[128,128]{1,0:T(8,128)S(1)}, u32[]{:S(2)}, u32[]{:S(2)}) collective-permute-start(f32[128,128]{1,0:T(8,128)S(1)} %bitcast.78), channel_id=1, source_target_pairs={{0,3},{1,0},{2,1},{3,2},{4,7},{5,4},{6,5},{7,6},{8,11},{9,8},{10,9... | collective-permute-start | bytes 196616 | tf_op jit(solution)/shard_map/ppermute | solution.py:51
  112.2 0.0 collective-permute-done.6
  112.3 2.5 %collective-permute-done.10 = f32[128,128]{1,0:T(8,128)S(1)} collective-permute-done((f32[128,128]{1,0:T(8,128)S(1)}, f32[128,128]{1,0:T(8,128)S(1)}, u32[]{:S(2)}, u32[]{:S(2)}) %collective-permute-start.10) | collective-permute-done | bytes 65568 | tf_op jit(solution)/shard_map/ppermute | solution.py:51
  114.8 1.7 %collective-permute-done.11 = f32[128,128]{1,0:T(8,128)S(1)} collective-permute-done((f32[128,128]{1,0:T(8,128)S(1)}, f32[128,128]{1,0:T(8,128)S(1)}, u32[]{:S(2)}, u32[]{:S(2)}) %collective-permute-start.11) | collective-permute-done | bytes 65568 | tf_op jit(solution)/shard_map/ppermute | solution.py:51
  116.5 0.0 collective-permute-done.12
  116.5 0.1 copy.58
  116.6 0.0 collective-permute-done.13
  116.6 0.1 fusion.13
  116.8 0.8 copy.60
  (6 shorter events, 0.2 us)
Async XLA Ops:
  3.7 53.6 %all-to-all-start = ((f32[8,128,1024]{2,1,0:T(8,128)}), f32[8,128,1024]{2,1,0:T(8,128)}, u32[]{:S(2)}, u32[]{:S(2)}) async-start(f32[8,128,1024]{2,1,0:T(8,128)} %shard_map.17), calls=%async_computation | async-start | bytes 8388608 | tf_op jit(solution)/shard_map/all_to_all | solution.py:109
  65.0 4.6 %collective-permute-start = (f32[512,1024]{1,0:T(8,128)}, f32[512,1024]{1,0:T(8,128)S(1)}, u32[]{:S(2)}, u32[]{:S(2)}) collective-permute-start(f32[512,1024]{1,0:T(8,128)} %fusion), channel_id=1, source_target_pairs={{0,4},{4,0},{1,5},{5,1},{2,6},{6,2},{3,7},{7,3},{8,12},{12,8},{9,1... | collective-permute-start | bytes 6291464 | tf_op jit(solution)/shard_map/ppermute | solution.py:131
  76.4 5.1 %slice-start = ((f32[128,8192]{1,0:T(8,128)}), f32[128,256]{1,0:T(8,128)S(1)}, s32[]{:S(2)}) async-start(f32[128,8192]{1,0:T(8,128)} %block_ref.1), calls=%async_computation.1 | async-start | bytes 262144 | tf_op jit(solution)/shard_map/slice | solution.py:147
  77.7 11.8 %collective-permute-start.1 = (f32[128,512]{0,1:T(8,128)}, f32[128,512]{0,1:T(8,128)S(1)}, u32[]{:S(2)}, u32[]{:S(2)}) collective-permute-start(f32[128,512]{0,1:T(8,128)} %bitcast.8), channel_id=1, source_target_pairs={{0,8},{8,0},{16,24},{24,16},{1,9},{9,1},{17,25},{25,17},{2,10},{10... | collective-permute-start | bytes 786440 | tf_op jit(solution)/shard_map/ppermute | solution.py:95
  78.8 14.2 %collective-permute-start.2 = (f32[128,512]{0,1:T(8,128)S(1)}, f32[128,512]{0,1:T(8,128)S(1)}, u32[]{:S(2)}, u32[]{:S(2)}) collective-permute-start(f32[128,512]{0,1:T(8,128)S(1)} %bitcast.71), channel_id=1, source_target_pairs={{0,16},{8,24},{16,0},{24,8},{1,17},{9,25},{17,1},{25,9},{2,18},{10... | collective-permute-start | bytes 786440 | tf_op jit(solution)/shard_map/ppermute | solution.py:95
  79.7 13.3 %collective-permute-start.3 = (f32[128,512]{0,1:T(8,128)S(1)}, f32[128,512]{0,1:T(8,128)S(1)}, u32[]{:S(2)}, u32[]{:S(2)}) collective-permute-start(f32[128,512]{0,1:T(8,128)S(1)} %bitcast.70), channel_id=1, source_target_pairs={{0,24},{8,16},{16,8},{24,0},{1,25},{9,17},{17,9},{25,1},{2,26},{10... | collective-permute-start | bytes 786440 | tf_op jit(solution)/shard_map/ppermute | solution.py:95
  81.6 35.0 %collective-permute-start.13 = (f32[256]{0:T(256)S(1)}, f32[256]{0:T(256)S(1)}, u32[]{:S(2)}, u32[]{:S(2)}) collective-permute-start(f32[256]{0:T(256)S(1)} %bitcast.81), channel_id=1, source_target_pairs={{0,0},{1,8},{2,16},{3,24},{8,1},{9,9},{10,17},{11,25},{16,2},{17,1... | collective-permute-start | bytes 3080 | tf_op jit(solution)/shard_map/ppermute | solution.py:116
  83.3 15.0 %collective-permute-start.7 = (f32[128,512]{0,1:T(8,128)}, f32[128,512]{0,1:T(8,128)S(1)}, u32[]{:S(2)}, u32[]{:S(2)}) collective-permute-start(f32[128,512]{0,1:T(8,128)} %bitcast.19), channel_id=1, source_target_pairs={{0,8},{8,0},{16,24},{24,16},{1,9},{9,1},{17,25},{25,17},{2,10},{10... | collective-permute-start | bytes 786440 | tf_op jit(solution)/shard_map/ppermute | solution.py:95
  89.5 14.4 %collective-permute-start.8 = (f32[128,512]{0,1:T(8,128)}, f32[128,512]{0,1:T(8,128)S(1)}, u32[]{:S(2)}, u32[]{:S(2)}) collective-permute-start(f32[128,512]{0,1:T(8,128)} %bitcast.73), channel_id=1, source_target_pairs={{0,16},{8,24},{16,0},{24,8},{1,17},{9,25},{17,1},{25,9},{2,18},{10... | collective-permute-start | bytes 786440 | tf_op jit(solution)/shard_map/ppermute | solution.py:95
  93.0 14.7 %collective-permute-start.9 = (f32[128,512]{0,1:T(8,128)S(1)}, f32[128,512]{0,1:T(8,128)S(1)}, u32[]{:S(2)}, u32[]{:S(2)}) collective-permute-start(f32[128,512]{0,1:T(8,128)S(1)} %bitcast.72), channel_id=1, source_target_pairs={{0,24},{8,16},{16,8},{24,0},{1,25},{9,17},{17,9},{25,1},{2,26},{10... | collective-permute-start | bytes 786440 | tf_op jit(solution)/shard_map/ppermute | solution.py:95
  93.2 15.1 %collective-permute-start.4 = (f32[128,128]{1,0:T(8,128)S(1)}, f32[128,128]{1,0:T(8,128)S(1)}, u32[]{:S(2)}, u32[]{:S(2)}) collective-permute-start(f32[128,128]{1,0:T(8,128)S(1)} %bitcast.76), channel_id=1, source_target_pairs={{0,1},{1,2},{2,3},{3,0},{4,5},{5,6},{6,7},{7,4},{8,9},{9,10},{10,1... | collective-permute-start | bytes 196616 | tf_op jit(solution)/shard_map/ppermute | solution.py:51
  98.3 11.1 %collective-permute-start.5 = (f32[128,128]{1,0:T(8,128)S(1)}, f32[128,128]{1,0:T(8,128)S(1)}, u32[]{:S(2)}, u32[]{:S(2)}) collective-permute-start(f32[128,128]{1,0:T(8,128)S(1)} %bitcast.75), channel_id=1, source_target_pairs={{0,2},{1,3},{2,0},{3,1},{4,6},{5,7},{6,4},{7,5},{8,10},{9,11},{10,... | collective-permute-start | bytes 196616 | tf_op jit(solution)/shard_map/ppermute | solution.py:51
  103.9 8.3 %collective-permute-start.6 = (f32[128,128]{1,0:T(8,128)S(1)}, f32[128,128]{1,0:T(8,128)S(1)}, u32[]{:S(2)}, u32[]{:S(2)}) collective-permute-start(f32[128,128]{1,0:T(8,128)S(1)} %bitcast.74), channel_id=1, source_target_pairs={{0,3},{1,0},{2,1},{3,2},{4,7},{5,4},{6,5},{7,6},{8,11},{9,8},{10,9... | collective-permute-start | bytes 196616 | tf_op jit(solution)/shard_map/ppermute | solution.py:51
  107.9 6.9 %collective-permute-start.10 = (f32[128,128]{1,0:T(8,128)S(1)}, f32[128,128]{1,0:T(8,128)S(1)}, u32[]{:S(2)}, u32[]{:S(2)}) collective-permute-start(f32[128,128]{1,0:T(8,128)S(1)} %bitcast.77), channel_id=1, source_target_pairs={{0,1},{1,2},{2,3},{3,0},{4,5},{5,6},{6,7},{7,4},{8,9},{9,10},{10,1... | collective-permute-start | bytes 196616 | tf_op jit(solution)/shard_map/ppermute | solution.py:51
  108.3 8.2 %collective-permute-start.11 = (f32[128,128]{1,0:T(8,128)S(1)}, f32[128,128]{1,0:T(8,128)S(1)}, u32[]{:S(2)}, u32[]{:S(2)}) collective-permute-start(f32[128,128]{1,0:T(8,128)S(1)} %bitcast.79), channel_id=1, source_target_pairs={{0,2},{1,3},{2,0},{3,1},{4,6},{5,7},{6,4},{7,5},{8,10},{9,11},{10,... | collective-permute-start | bytes 196616 | tf_op jit(solution)/shard_map/ppermute | solution.py:51
  109.4 7.1 %collective-permute-start.12 = (f32[128,128]{1,0:T(8,128)S(1)}, f32[128,128]{1,0:T(8,128)S(1)}, u32[]{:S(2)}, u32[]{:S(2)}) collective-permute-start(f32[128,128]{1,0:T(8,128)S(1)} %bitcast.78), channel_id=1, source_target_pairs={{0,3},{1,0},{2,1},{3,2},{4,7},{5,4},{6,5},{7,6},{8,11},{9,8},{10,9... | collective-permute-start | bytes 196616 | tf_op jit(solution)/shard_map/ppermute | solution.py:51

commit v11 on v10

--- a/solution.py
+++ b/solution.py
@@ -45,7 +45,7 @@
     width = cols // n_col
     blocks = part.reshape(rows, n_col, width)
     total = lax.dynamic_index_in_dim(blocks, me, 1, keepdims=False)
-    for s in range(1, n_col):
+    for s in sorted(range(1, n_col), key=lambda s: -min(s, n_col - s)):
         send = lax.dynamic_index_in_dim(blocks, (me + s) % n_col, 1, keepdims=False)
         perm = [(i, (i + s) % n_col) for i in range(n_col)]
         total = total + lax.ppermute(send, "col", perm)

time: 118 us -> 117 us (level)
  no operation moved by 1% of the time
where the time goes in v11:
time: 117 us
  waiting for transfers between devices  43.1 us (37%)
  starting transfers between devices  32.5 us (28%)
  blocking collectives  14.6 us (12%)
  matrix products  14.5 us (12%)
  local copies, waits for them, and re-layouts  5.21 us (4%)
  Pallas kernels  3.71 us (3%)
  other arithmetic  2.75 us (2%)
    all_to_all x1, waiting for transfers between devices, body(): lax.all_to_all(chunks, order, split_axis=0, concat_axis=0, tiled=True)  31.3 us
    dot_general x2, matrix products, inner_rows(): lax.dot_general(left, right, (((1,), (1,)), ((), ())), precision=lax.Prec...  14.5 us
    ppermute x6, starting transfers between devices, col_reduce_scatter(): total = total + lax.ppermute(send, 'col', perm)  13.8 us
    psum x1, blocking collectives, body(): own_degree = lax.psum(jnp.sum(adjacency, axis=1), 'col')  12.8 us
    ppermute x6, starting transfers between devices, chip_reduce_scatter(): total = total + lax.ppermute(send, 'chip', perm)  12.3 us
    all_to_all x1, starting transfers between devices, body(): lax.all_to_all(chunks, order, split_axis=0, concat_axis=0, tiled=True)  5.17 us
    ppermute x6, waiting for transfers between devices, chip_reduce_scatter(): total = total + lax.ppermute(send, 'chip', perm)  4.37 us
    ppermute x1, waiting for transfers between devices, body(): got = lax.ppermute(inner_rows(left, flat), 'core', perm)  4 us
  transfers between devices with their start and end apart: 15, of which 6 were waited for; matrix products, arithmetic and copies ran while one was open for 5% of the time, Pallas kernels for 0%

profile of v11, /device:TPU:0, one launch (start us, length us, event | category | flops | bytes accessed | tf_op | source)
XLA Modules:
  0.0 116.7 jit_solution(16481184895899825657)
XLA Ops:
  0.0 3.7 %shard_map.17 = f32[8,128,1024]{2,1,0:T(8,128)} custom-call(f32[128,8192]{1,0:T(8,128)} %block_ref.1), custom_call_target="tpu_custom_call" | custom-call | tf_op jit(solution)/shard_map/pallas_call | solution.py:32
  3.7 5.2 %all-to-all-start = ((f32[8,128,1024]{2,1,0:T(8,128)}), f32[8,128,1024]{2,1,0:T(8,128)}, u32[]{:S(2)}, u32[]{:S(2)}) async-start(f32[8,128,1024]{2,1,0:T(8,128)} %shard_map.17), calls=%async_computation | async-start | bytes 8388608 | tf_op jit(solution)/shard_map/all_to_all | solution.py:109
  8.9 2.5 %reduce_sum.9 = f32[128]{0:T(128)S(1)} reduce(f32[128,8192]{1,0:T(8,128)} %block_ref.1, f32[]{:T(128)} %constant.87.clone.1), dimensions={1}, to_apply=%region_0.0 | reduce | flops 1048448 | bytes 4194820 | tf_op jit(solution)/shard_map/reduce_sum | solution.py:111
  11.4 12.8 %psum.7 = f32[128]{0:T(128)S(1)} all-reduce(f32[128]{0:T(128)S(1)} %reduce_sum.9), channel_id=1, replica_groups=mesh['chip'=4,'core'=2,'col'=4] {'col'}, use_global_device_ids=true, to_apply=%region_1.0 | all-reduce | flops 128 | bytes 1024 | tf_op jit(solution)/shard_map/psum | solution.py:111
  24.2 1.8 %all-gather = f32[2,1,128]{2,1,0:T(1,128)S(1)} all-gather(f32[1,1,128]{2,1,0:T(1,128)S(1)} %bitcast.80), channel_id=1, replica_groups=mesh['chip'=4,'core'=2,'col'=4] {'core'}, dimensions={0}, use_global_device_ids=true | all-gather | bytes 1536 | tf_op jit(solution)/shard_map/all_gather | solution.py:113
  26.0 31.3 %all-to-all-done = f32[8,128,1024]{2,1,0:T(8,128)} async-done(((f32[8,128,1024]{2,1,0:T(8,128)}), f32[8,128,1024]{2,1,0:T(8,128)}, u32[]{:S(2)}, u32[]{:S(2)}) %all-to-all-start) | async-done | bytes 4194336 | tf_op jit(solution)/shard_map/all_to_all | solution.py:109
  57.3 7.7 %fusion = f32[512,1024]{1,0:T(8,128)} fusion(f32[1024,1024]{1,0:T(8,128)} %bitcast.4, f32[2,512,1024]{2,1,0:T(8,128)} %bitcast.2, s32[]{:T(128)S(6)} %select_n.68), kind=kOutput, calls=%fused_computation | convolution fusion | flops 3221225472 | bytes 8388612 | tf_op jit(solution)/shard_map/dot_general | solution.py:13
  65.0 0.6 collective-permute-start
  65.6 4.0 %collective-permute-done = f32[512,1024]{1,0:T(8,128)S(1)} collective-permute-done((f32[512,1024]{1,0:T(8,128)}, f32[512,1024]{1,0:T(8,128)S(1)}, u32[]{:S(2)}, u32[]{:S(2)}) %collective-permute-start) | collective-permute-done | bytes 2097184 | tf_op jit(solution)/shard_map/ppermute | solution.py:131
  69.6 6.8 %fusion.6 = f32[512,1024]{1,0:T(8,128)S(1)} fusion(f32[512,1024]{1,0:T(8,128)S(1)} %collective-permute-done, f32[1024,1024]{1,0:T(8,128)} %bitcast.4, f32[2,512,1024]{2,1,0:T(8,128)} %bitcast.2, s32[]{:T(128)S(6)} %select_n.66), kind=kOutput, calls=%fused_computation.6 | convolution fusion | flops 3221749760 | bytes 10485764 | tf_op jit(solution)/shard_map/dot_general | solution.py:13
  76.4 0.0 slice-start
  76.4 0.2 fusion.22
  76.6 0.2 constant_dynamic-slice_fusion.7
  76.8 0.8 copy.43
  77.7 1.0 collective-permute-start.1
  78.7 0.1 copy.44
  78.8 0.7 collective-permute-start.2
  79.6 0.1 copy.45
  79.7 1.8 %collective-permute-start.3 = (f32[128,512]{0,1:T(8,128)S(1)}, f32[128,512]{0,1:T(8,128)S(1)}, u32[]{:S(2)}, u32[]{:S(2)}) collective-permute-start(f32[128,512]{0,1:T(8,128)S(1)} %bitcast.70), channel_id=1, source_target_pairs={{0,24},{8,16},{16,8},{24,0},{1,25},{9,17},{17,9},{25,1},{2,26},{10... | collective-permute-start | bytes 786440 | tf_op jit(solution)/shard_map/ppermute | solution.py:95
  81.5 0.0 slice-done
  81.5 0.1 copy.61
  81.6 0.7 collective-permute-start.13
  82.3 0.1 copy.42
  82.4 0.8 copy.51
  83.3 5.1 %collective-permute-start.7 = (f32[128,512]{0,1:T(8,128)}, f32[128,512]{0,1:T(8,128)S(1)}, u32[]{:S(2)}, u32[]{:S(2)}) collective-permute-start(f32[128,512]{0,1:T(8,128)} %bitcast.19), channel_id=1, source_target_pairs={{0,8},{8,0},{16,24},{24,16},{1,9},{9,1},{17,25},{25,17},{2,10},{10... | collective-permute-start | bytes 786440 | tf_op jit(solution)/shard_map/ppermute | solution.py:95
  88.4 0.8 copy.52
  89.2 0.1 copy.53
  89.3 0.1 copy.50
  89.5 0.0 collective-permute-done.1
  89.5 3.5 %collective-permute-start.8 = (f32[128,512]{0,1:T(8,128)}, f32[128,512]{0,1:T(8,128)S(1)}, u32[]{:S(2)}, u32[]{:S(2)}) collective-permute-start(f32[128,512]{0,1:T(8,128)} %bitcast.73), channel_id=1, source_target_pairs={{0,16},{8,24},{16,0},{24,8},{1,17},{9,25},{17,1},{25,9},{2,18},{10... | collective-permute-start | bytes 786440 | tf_op jit(solution)/shard_map/ppermute | solution.py:95
  93.0 0.0 collective-permute-done.2
  93.0 0.0 collective-permute-start.9
  93.0 0.0 collective-permute-done.3
  93.0 0.1 fusion.12
  93.1 0.1 copy.47
  93.2 3.6 %collective-permute-start.4 = (f32[128,128]{1,0:T(8,128)S(1)}, f32[128,128]{1,0:T(8,128)S(1)}, u32[]{:S(2)}, u32[]{:S(2)}) collective-permute-start(f32[128,128]{1,0:T(8,128)S(1)} %bitcast.76), channel_id=1, source_target_pairs={{0,2},{1,3},{2,0},{3,1},{4,6},{5,7},{6,4},{7,5},{8,10},{9,11},{10,... | collective-permute-start | bytes 196616 | tf_op jit(solution)/shard_map/ppermute | solution.py:51
  96.8 0.1 copy.48
  96.9 0.1 copy.49
  97.0 0.1 copy.46
  97.1 1.2 %collective-permute-done.7 = f32[128,512]{0,1:T(8,128)S(1)} collective-permute-done((f32[128,512]{0,1:T(8,128)}, f32[128,512]{0,1:T(8,128)S(1)}, u32[]{:S(2)}, u32[]{:S(2)}) %collective-permute-start.7) | collective-permute-done | bytes 262176 | tf_op jit(solution)/shard_map/ppermute | solution.py:95
  98.3 2.4 %collective-permute-start.5 = (f32[128,128]{1,0:T(8,128)S(1)}, f32[128,128]{1,0:T(8,128)S(1)}, u32[]{:S(2)}, u32[]{:S(2)}) collective-permute-start(f32[128,128]{1,0:T(8,128)S(1)} %bitcast.75), channel_id=1, source_target_pairs={{0,1},{1,2},{2,3},{3,0},{4,5},{5,6},{6,7},{7,4},{8,9},{9,10},{10,1... | collective-permute-start | bytes 196616 | tf_op jit(solution)/shard_map/ppermute | solution.py:51
  100.7 3.2 %collective-permute-done.8 = f32[128,512]{0,1:T(8,128)S(1)} collective-permute-done((f32[128,512]{0,1:T(8,128)}, f32[128,512]{0,1:T(8,128)S(1)}, u32[]{:S(2)}, u32[]{:S(2)}) %collective-permute-start.8) | collective-permute-done | bytes 262176 | tf_op jit(solution)/shard_map/ppermute | solution.py:95
  103.9 3.8 %collective-permute-start.6 = (f32[128,128]{1,0:T(8,128)S(1)}, f32[128,128]{1,0:T(8,128)S(1)}, u32[]{:S(2)}, u32[]{:S(2)}) collective-permute-start(f32[128,128]{1,0:T(8,128)S(1)} %bitcast.74), channel_id=1, source_target_pairs={{0,3},{1,0},{2,1},{3,2},{4,7},{5,4},{6,5},{7,6},{8,11},{9,8},{10,9... | collective-permute-start | bytes 196616 | tf_op jit(solution)/shard_map/ppermute | solution.py:51
  107.7 0.0 collective-permute-done.9
  107.8 0.1 copy.55
  107.9 0.1 collective-permute-start.10
  108.0 0.1 copy.56
  108.1 0.1 copy.57
  108.2 0.1 copy.54
  108.3 0.0 collective-permute-done.4
  108.3 1.1 collective-permute-start.11
  109.4 0.0 collective-permute-done.5
  109.4 2.8 %collective-permute-start.12 = (f32[128,128]{1,0:T(8,128)S(1)}, f32[128,128]{1,0:T(8,128)S(1)}, u32[]{:S(2)}, u32[]{:S(2)}) collective-permute-start(f32[128,128]{1,0:T(8,128)S(1)} %bitcast.78), channel_id=1, source_target_pairs={{0,3},{1,0},{2,1},{3,2},{4,7},{5,4},{6,5},{7,6},{8,11},{9,8},{10,9... | collective-permute-start | bytes 196616 | tf_op jit(solution)/shard_map/ppermute | solution.py:51
  112.2 0.0 collective-permute-done.6
  112.2 2.8 %collective-permute-done.10 = f32[128,128]{1,0:T(8,128)S(1)} collective-permute-done((f32[128,128]{1,0:T(8,128)S(1)}, f32[128,128]{1,0:T(8,128)S(1)}, u32[]{:S(2)}, u32[]{:S(2)}) %collective-permute-start.10) | collective-permute-done | bytes 65568 | tf_op jit(solution)/shard_map/ppermute | solution.py:51
  115.1 0.0 collective-permute-done.11
  115.1 0.6 collective-permute-done.12
  115.7 0.1 copy.58
  115.8 0.0 collective-permute-done.13
  115.8 0.1 fusion.13
  115.9 0.8 copy.60
  (6 shorter events, 0.2 us)
Async XLA Ops:
  3.7 53.6 %all-to-all-start = ((f32[8,128,1024]{2,1,0:T(8,128)}), f32[8,128,1024]{2,1,0:T(8,128)}, u32[]{:S(2)}, u32[]{:S(2)}) async-start(f32[8,128,1024]{2,1,0:T(8,128)} %shard_map.17), calls=%async_computation | async-start | bytes 8388608 | tf_op jit(solution)/shard_map/all_to_all | solution.py:109
  65.0 4.6 %collective-permute-start = (f32[512,1024]{1,0:T(8,128)}, f32[512,1024]{1,0:T(8,128)S(1)}, u32[]{:S(2)}, u32[]{:S(2)}) collective-permute-start(f32[512,1024]{1,0:T(8,128)} %fusion), channel_id=1, source_target_pairs={{0,4},{4,0},{1,5},{5,1},{2,6},{6,2},{3,7},{7,3},{8,12},{12,8},{9,1... | collective-permute-start | bytes 6291464 | tf_op jit(solution)/shard_map/ppermute | solution.py:131
  76.4 5.1 %slice-start = ((f32[128,8192]{1,0:T(8,128)}), f32[128,256]{1,0:T(8,128)S(1)}, s32[]{:S(2)}) async-start(f32[128,8192]{1,0:T(8,128)} %block_ref.1), calls=%async_computation.1 | async-start | bytes 262144 | tf_op jit(solution)/shard_map/slice | solution.py:147
  77.7 11.8 %collective-permute-start.1 = (f32[128,512]{0,1:T(8,128)}, f32[128,512]{0,1:T(8,128)S(1)}, u32[]{:S(2)}, u32[]{:S(2)}) collective-permute-start(f32[128,512]{0,1:T(8,128)} %bitcast.8), channel_id=1, source_target_pairs={{0,8},{8,0},{16,24},{24,16},{1,9},{9,1},{17,25},{25,17},{2,10},{10... | collective-permute-start | bytes 786440 | tf_op jit(solution)/shard_map/ppermute | solution.py:95
  78.8 14.2 %collective-permute-start.2 = (f32[128,512]{0,1:T(8,128)S(1)}, f32[128,512]{0,1:T(8,128)S(1)}, u32[]{:S(2)}, u32[]{:S(2)}) collective-permute-start(f32[128,512]{0,1:T(8,128)S(1)} %bitcast.71), channel_id=1, source_target_pairs={{0,16},{8,24},{16,0},{24,8},{1,17},{9,25},{17,1},{25,9},{2,18},{10... | collective-permute-start | bytes 786440 | tf_op jit(solution)/shard_map/ppermute | solution.py:95
  79.7 13.3 %collective-permute-start.3 = (f32[128,512]{0,1:T(8,128)S(1)}, f32[128,512]{0,1:T(8,128)S(1)}, u32[]{:S(2)}, u32[]{:S(2)}) collective-permute-start(f32[128,512]{0,1:T(8,128)S(1)} %bitcast.70), channel_id=1, source_target_pairs={{0,24},{8,16},{16,8},{24,0},{1,25},{9,17},{17,9},{25,1},{2,26},{10... | collective-permute-start | bytes 786440 | tf_op jit(solution)/shard_map/ppermute | solution.py:95
  81.6 34.2 %collective-permute-start.13 = (f32[256]{0:T(256)S(1)}, f32[256]{0:T(256)S(1)}, u32[]{:S(2)}, u32[]{:S(2)}) collective-permute-start(f32[256]{0:T(256)S(1)} %bitcast.81), channel_id=1, source_target_pairs={{0,0},{1,8},{2,16},{3,24},{8,1},{9,9},{10,17},{11,25},{16,2},{17,1... | collective-permute-start | bytes 3080 | tf_op jit(solution)/shard_map/ppermute | solution.py:116
  83.3 15.0 %collective-permute-start.7 = (f32[128,512]{0,1:T(8,128)}, f32[128,512]{0,1:T(8,128)S(1)}, u32[]{:S(2)}, u32[]{:S(2)}) collective-permute-start(f32[128,512]{0,1:T(8,128)} %bitcast.19), channel_id=1, source_target_pairs={{0,8},{8,0},{16,24},{24,16},{1,9},{9,1},{17,25},{25,17},{2,10},{10... | collective-permute-start | bytes 786440 | tf_op jit(solution)/shard_map/ppermute | solution.py:95
  89.5 14.4 %collective-permute-start.8 = (f32[128,512]{0,1:T(8,128)}, f32[128,512]{0,1:T(8,128)S(1)}, u32[]{:S(2)}, u32[]{:S(2)}) collective-permute-start(f32[128,512]{0,1:T(8,128)} %bitcast.73), channel_id=1, source_target_pairs={{0,16},{8,24},{16,0},{24,8},{1,17},{9,25},{17,1},{25,9},{2,18},{10... | collective-permute-start | bytes 786440 | tf_op jit(solution)/shard_map/ppermute | solution.py:95
  93.0 14.7 %collective-permute-start.9 = (f32[128,512]{0,1:T(8,128)S(1)}, f32[128,512]{0,1:T(8,128)S(1)}, u32[]{:S(2)}, u32[]{:S(2)}) collective-permute-start(f32[128,512]{0,1:T(8,128)S(1)} %bitcast.72), channel_id=1, source_target_pairs={{0,24},{8,16},{16,8},{24,0},{1,25},{9,17},{17,9},{25,1},{2,26},{10... | collective-permute-start | bytes 786440 | tf_op jit(solution)/shard_map/ppermute | solution.py:95
  93.2 15.1 %collective-permute-start.4 = (f32[128,128]{1,0:T(8,128)S(1)}, f32[128,128]{1,0:T(8,128)S(1)}, u32[]{:S(2)}, u32[]{:S(2)}) collective-permute-start(f32[128,128]{1,0:T(8,128)S(1)} %bitcast.76), channel_id=1, source_target_pairs={{0,2},{1,3},{2,0},{3,1},{4,6},{5,7},{6,4},{7,5},{8,10},{9,11},{10,... | collective-permute-start | bytes 196616 | tf_op jit(solution)/shard_map/ppermute | solution.py:51
  98.3 11.1 %collective-permute-start.5 = (f32[128,128]{1,0:T(8,128)S(1)}, f32[128,128]{1,0:T(8,128)S(1)}, u32[]{:S(2)}, u32[]{:S(2)}) collective-permute-start(f32[128,128]{1,0:T(8,128)S(1)} %bitcast.75), channel_id=1, source_target_pairs={{0,1},{1,2},{2,3},{3,0},{4,5},{5,6},{6,7},{7,4},{8,9},{9,10},{10,1... | collective-permute-start | bytes 196616 | tf_op jit(solution)/shard_map/ppermute | solution.py:51
  103.9 8.3 %collective-permute-start.6 = (f32[128,128]{1,0:T(8,128)S(1)}, f32[128,128]{1,0:T(8,128)S(1)}, u32[]{:S(2)}, u32[]{:S(2)}) collective-permute-start(f32[128,128]{1,0:T(8,128)S(1)} %bitcast.74), channel_id=1, source_target_pairs={{0,3},{1,0},{2,1},{3,2},{4,7},{5,4},{6,5},{7,6},{8,11},{9,8},{10,9... | collective-permute-start | bytes 196616 | tf_op jit(solution)/shard_map/ppermute | solution.py:51
  107.9 7.1 %collective-permute-start.10 = (f32[128,128]{1,0:T(8,128)S(1)}, f32[128,128]{1,0:T(8,128)S(1)}, u32[]{:S(2)}, u32[]{:S(2)}) collective-permute-start(f32[128,128]{1,0:T(8,128)S(1)} %bitcast.77), channel_id=1, source_target_pairs={{0,2},{1,3},{2,0},{3,1},{4,6},{5,7},{6,4},{7,5},{8,10},{9,11},{10,... | collective-permute-start | bytes 196616 | tf_op jit(solution)/shard_map/ppermute | solution.py:51
  108.3 6.8 %collective-permute-start.11 = (f32[128,128]{1,0:T(8,128)S(1)}, f32[128,128]{1,0:T(8,128)S(1)}, u32[]{:S(2)}, u32[]{:S(2)}) collective-permute-start(f32[128,128]{1,0:T(8,128)S(1)} %bitcast.79), channel_id=1, source_target_pairs={{0,1},{1,2},{2,3},{3,0},{4,5},{5,6},{6,7},{7,4},{8,9},{9,10},{10,1... | collective-permute-start | bytes 196616 | tf_op jit(solution)/shard_map/ppermute | solution.py:51
  109.4 6.3 %collective-permute-start.12 = (f32[128,128]{1,0:T(8,128)S(1)}, f32[128,128]{1,0:T(8,128)S(1)}, u32[]{:S(2)}, u32[]{:S(2)}) collective-permute-start(f32[128,128]{1,0:T(8,128)S(1)} %bitcast.78), channel_id=1, source_target_pairs={{0,3},{1,0},{2,1},{3,2},{4,7},{5,4},{6,5},{7,6},{8,11},{9,8},{10,9... | collective-permute-start | bytes 196616 | tf_op jit(solution)/shard_map/ppermute | solution.py:51

commit v12 on v11

--- a/solution.py
+++ b/solution.py
@@ -86,7 +86,7 @@
     blocks = on_chip.reshape(n_chip, rows // n_chip, width)
     mine = lax.axis_index("chip")
     total = lax.dynamic_index_in_dim(blocks, mine, 0, keepdims=False)
-    for s in range(1, n_chip):
+    for s in sorted(range(1, n_chip), key=lambda s: -s):
         if n_chip & (n_chip - 1) == 0:
             peer, perm = mine ^ s, [(i, i ^ s) for i in range(n_chip)]
         else:

time: 117 us -> 117 us (level)
  waiting for transfers between devices: 43.1 us -> 41.2 us
  starting transfers between devices: 32.5 us -> 34.3 us
    ppermute x6, waiting for transfers between devices: 4.37 us -> 2.63 us  [chip_reduce_scatter(): total = total + lax.ppermute(send, 'chip', perm)]
    ppermute x6, starting transfers between devices: 12.3 us -> 13.5 us  [chip_reduce_scatter(): total = total + lax.ppermute(send, 'chip', perm)]
where the time goes in v12:
time: 117 us
  waiting for transfers between devices  41.2 us (35%)
  starting transfers between devices  34.3 us (29%)
  blocking collectives  14.6 us (12%)
  matrix products  14.5 us (12%)
  local copies, waits for them, and re-layouts  5.21 us (4%)
  Pallas kernels  3.71 us (3%)
  other arithmetic  2.75 us (2%)
    all_to_all x1, waiting for transfers between devices, body(): lax.all_to_all(chunks, order, split_axis=0, concat_axis=0, tiled=True)  31.3 us
    dot_general x2, matrix products, inner_rows(): lax.dot_general(left, right, (((1,), (1,)), ((), ())), precision=lax.Prec...  14.5 us
    ppermute x6, starting transfers between devices, col_reduce_scatter(): total = total + lax.ppermute(send, 'col', perm)  14.4 us
    ppermute x6, starting transfers between devices, chip_reduce_scatter(): total = total + lax.ppermute(send, 'chip', perm)  13.5 us
    psum x1, blocking collectives, body(): own_degree = lax.psum(jnp.sum(adjacency, axis=1), 'col')  12.8 us
    all_to_all x1, starting transfers between devices, body(): lax.all_to_all(chunks, order, split_axis=0, concat_axis=0, tiled=True)  5.17 us
    ppermute x1, waiting for transfers between devices, body(): got = lax.ppermute(inner_rows(left, flat), 'core', perm)  4 us
    pallas_call x1, Pallas kernels, column_chunks(): pl.pallas_call(_copy_blocks, grid=(n_chunks // per_step,), in_specs=[pl.B...  3.71 us
  transfers between devices with their start and end apart: 15, of which 6 were waited for; matrix products, arithmetic and copies ran while one was open for 5% of the time, Pallas kernels for 0%

profile of v12, /device:TPU:0, one launch (start us, length us, event | category | flops | bytes accessed | tf_op | source)
XLA Modules:
  0.0 116.6 jit_solution(10557542932758763732)
XLA Ops:
  0.0 3.7 %shard_map.17 = f32[8,128,1024]{2,1,0:T(8,128)} custom-call(f32[128,8192]{1,0:T(8,128)} %block_ref.1), custom_call_target="tpu_custom_call" | custom-call | tf_op jit(solution)/shard_map/pallas_call | solution.py:32
  3.7 5.2 %all-to-all-start = ((f32[8,128,1024]{2,1,0:T(8,128)}), f32[8,128,1024]{2,1,0:T(8,128)}, u32[]{:S(2)}, u32[]{:S(2)}) async-start(f32[8,128,1024]{2,1,0:T(8,128)} %shard_map.17), calls=%async_computation | async-start | bytes 8388608 | tf_op jit(solution)/shard_map/all_to_all | solution.py:109
  8.9 2.5 %reduce_sum.9 = f32[128]{0:T(128)S(1)} reduce(f32[128,8192]{1,0:T(8,128)} %block_ref.1, f32[]{:T(128)} %constant.87.clone.1), dimensions={1}, to_apply=%region_0.0 | reduce | flops 1048448 | bytes 4194820 | tf_op jit(solution)/shard_map/reduce_sum | solution.py:111
  11.4 12.8 %psum.7 = f32[128]{0:T(128)S(1)} all-reduce(f32[128]{0:T(128)S(1)} %reduce_sum.9), channel_id=1, replica_groups=mesh['chip'=4,'core'=2,'col'=4] {'col'}, use_global_device_ids=true, to_apply=%region_1.0 | all-reduce | flops 128 | bytes 1024 | tf_op jit(solution)/shard_map/psum | solution.py:111
  24.2 1.8 %all-gather = f32[2,1,128]{2,1,0:T(1,128)S(1)} all-gather(f32[1,1,128]{2,1,0:T(1,128)S(1)} %bitcast.80), channel_id=1, replica_groups=mesh['chip'=4,'core'=2,'col'=4] {'core'}, dimensions={0}, use_global_device_ids=true | all-gather | bytes 1536 | tf_op jit(solution)/shard_map/all_gather | solution.py:113
  26.0 31.3 %all-to-all-done = f32[8,128,1024]{2,1,0:T(8,128)} async-done(((f32[8,128,1024]{2,1,0:T(8,128)}), f32[8,128,1024]{2,1,0:T(8,128)}, u32[]{:S(2)}, u32[]{:S(2)}) %all-to-all-start) | async-done | bytes 4194336 | tf_op jit(solution)/shard_map/all_to_all | solution.py:109
  57.3 7.7 %fusion = f32[512,1024]{1,0:T(8,128)} fusion(f32[1024,1024]{1,0:T(8,128)} %bitcast.4, f32[2,512,1024]{2,1,0:T(8,128)} %bitcast.2, s32[]{:T(128)S(6)} %select_n.68), kind=kOutput, calls=%fused_computation | convolution fusion | flops 3221225472 | bytes 8388612 | tf_op jit(solution)/shard_map/dot_general | solution.py:13
  65.0 0.6 collective-permute-start
  65.6 4.0 %collective-permute-done = f32[512,1024]{1,0:T(8,128)S(1)} collective-permute-done((f32[512,1024]{1,0:T(8,128)}, f32[512,1024]{1,0:T(8,128)S(1)}, u32[]{:S(2)}, u32[]{:S(2)}) %collective-permute-start) | collective-permute-done | bytes 2097184 | tf_op jit(solution)/shard_map/ppermute | solution.py:131
  69.6 6.8 %fusion.6 = f32[512,1024]{1,0:T(8,128)S(1)} fusion(f32[512,1024]{1,0:T(8,128)S(1)} %collective-permute-done, f32[1024,1024]{1,0:T(8,128)} %bitcast.4, f32[2,512,1024]{2,1,0:T(8,128)} %bitcast.2, s32[]{:T(128)S(6)} %select_n.66), kind=kOutput, calls=%fused_computation.6 | convolution fusion | flops 3221749760 | bytes 10485764 | tf_op jit(solution)/shard_map/dot_general | solution.py:13
  76.4 0.0 slice-start
  76.4 0.2 fusion.22
  76.6 0.2 constant_dynamic-slice_fusion.7
  76.8 0.8 copy.43
  77.7 1.2 collective-permute-start.1
  78.8 0.1 copy.44
  78.9 1.4 %collective-permute-start.2 = (f32[128,512]{0,1:T(8,128)S(1)}, f32[128,512]{0,1:T(8,128)S(1)}, u32[]{:S(2)}, u32[]{:S(2)}) collective-permute-start(f32[128,512]{0,1:T(8,128)S(1)} %bitcast.71), channel_id=1, source_target_pairs={{0,16},{8,24},{16,0},{24,8},{1,17},{9,25},{17,1},{25,9},{2,18},{10... | collective-permute-start | bytes 786440 | tf_op jit(solution)/shard_map/ppermute | solution.py:95
  80.3 0.1 copy.45
  80.5 1.1 collective-permute-start.3
  81.5 0.0 slice-done
  81.5 0.1 copy.61
  81.6 0.7 collective-permute-start.13
  82.3 0.1 copy.42
  82.4 0.8 copy.51
  83.3 8.0 %collective-permute-start.7 = (f32[128,512]{0,1:T(8,128)}, f32[128,512]{0,1:T(8,128)S(1)}, u32[]{:S(2)}, u32[]{:S(2)}) collective-permute-start(f32[128,512]{0,1:T(8,128)} %bitcast.19), channel_id=1, source_target_pairs={{0,24},{8,16},{16,8},{24,0},{1,25},{9,17},{17,9},{25,1},{2,26},{10... | collective-permute-start | bytes 786440 | tf_op jit(solution)/shard_map/ppermute | solution.py:95
  91.3 0.8 copy.52
  92.1 0.1 copy.53
  92.2 0.1 copy.50
  92.4 0.0 collective-permute-done.1
  92.4 0.1 collective-permute-start.8
  92.5 0.4 collective-permute-done.2
  92.9 1.8 %collective-permute-start.9 = (f32[128,512]{0,1:T(8,128)S(1)}, f32[128,512]{0,1:T(8,128)S(1)}, u32[]{:S(2)}, u32[]{:S(2)}) collective-permute-start(f32[128,512]{0,1:T(8,128)S(1)} %bitcast.72), channel_id=1, source_target_pairs={{0,8},{8,0},{16,24},{24,16},{1,9},{9,1},{17,25},{25,17},{2,10},{10... | collective-permute-start | bytes 786440 | tf_op jit(solution)/shard_map/ppermute | solution.py:95
  94.7 0.0 collective-permute-done.3
  94.8 0.1 copy.47
  94.9 6.0 %collective-permute-start.4 = (f32[128,128]{1,0:T(8,128)S(1)}, f32[128,128]{1,0:T(8,128)S(1)}, u32[]{:S(2)}, u32[]{:S(2)}) collective-permute-start(f32[128,128]{1,0:T(8,128)S(1)} %bitcast.76), channel_id=1, source_target_pairs={{0,2},{1,3},{2,0},{3,1},{4,6},{5,7},{6,4},{7,5},{8,10},{9,11},{10,... | collective-permute-start | bytes 196616 | tf_op jit(solution)/shard_map/ppermute | solution.py:51
  100.9 0.1 copy.48
  101.0 0.1 copy.49
  101.1 0.1 copy.46
  101.2 0.0 collective-permute-done.7
  101.2 0.4 collective-permute-start.5
  101.6 2.2 %collective-permute-done.8 = f32[128,512]{0,1:T(8,128)S(1)} collective-permute-done((f32[128,512]{0,1:T(8,128)}, f32[128,512]{0,1:T(8,128)S(1)}, u32[]{:S(2)}, u32[]{:S(2)}) %collective-permute-start.8) | collective-permute-done | bytes 262176 | tf_op jit(solution)/shard_map/ppermute | solution.py:95
  103.8 4.0 %collective-permute-start.6 = (f32[128,128]{1,0:T(8,128)S(1)}, f32[128,128]{1,0:T(8,128)S(1)}, u32[]{:S(2)}, u32[]{:S(2)}) collective-permute-start(f32[128,128]{1,0:T(8,128)S(1)} %bitcast.74), channel_id=1, source_target_pairs={{0,3},{1,0},{2,1},{3,2},{4,7},{5,4},{6,5},{7,6},{8,11},{9,8},{10,9... | collective-permute-start | bytes 196616 | tf_op jit(solution)/shard_map/ppermute | solution.py:51
  107.8 0.0 collective-permute-done.9
  107.9 0.1 copy.55
  108.0 0.1 collective-permute-start.10
  108.1 0.1 copy.56
  108.2 0.1 copy.57
  108.3 0.1 copy.54
  108.4 0.0 collective-permute-done.4
  108.4 1.1 collective-permute-start.11
  109.5 0.0 collective-permute-done.5
  109.5 2.8 %collective-permute-start.12 = (f32[128,128]{1,0:T(8,128)S(1)}, f32[128,128]{1,0:T(8,128)S(1)}, u32[]{:S(2)}, u32[]{:S(2)}) collective-permute-start(f32[128,128]{1,0:T(8,128)S(1)} %bitcast.78), channel_id=1, source_target_pairs={{0,3},{1,0},{2,1},{3,2},{4,7},{5,4},{6,5},{7,6},{8,11},{9,8},{10,9... | collective-permute-start | bytes 196616 | tf_op jit(solution)/shard_map/ppermute | solution.py:51
  112.3 0.0 collective-permute-done.6
  112.3 2.7 %collective-permute-done.10 = f32[128,128]{1,0:T(8,128)S(1)} collective-permute-done((f32[128,128]{1,0:T(8,128)S(1)}, f32[128,128]{1,0:T(8,128)S(1)}, u32[]{:S(2)}, u32[]{:S(2)}) %collective-permute-start.10) | collective-permute-done | bytes 65568 | tf_op jit(solution)/shard_map/ppermute | solution.py:51
  115.0 0.0 collective-permute-done.11
  115.0 0.5 collective-permute-done.12
  115.6 0.1 copy.58
  115.7 0.0 collective-permute-done.13
  115.7 0.1 fusion.13
  115.8 0.8 copy.60
  (7 shorter events, 0.2 us)
Async XLA Ops:
  3.7 53.6 %all-to-all-start = ((f32[8,128,1024]{2,1,0:T(8,128)}), f32[8,128,1024]{2,1,0:T(8,128)}, u32[]{:S(2)}, u32[]{:S(2)}) async-start(f32[8,128,1024]{2,1,0:T(8,128)} %shard_map.17), calls=%async_computation | async-start | bytes 8388608 | tf_op jit(solution)/shard_map/all_to_all | solution.py:109
  65.0 4.6 %collective-permute-start = (f32[512,1024]{1,0:T(8,128)}, f32[512,1024]{1,0:T(8,128)S(1)}, u32[]{:S(2)}, u32[]{:S(2)}) collective-permute-start(f32[512,1024]{1,0:T(8,128)} %fusion), channel_id=1, source_target_pairs={{0,4},{4,0},{1,5},{5,1},{2,6},{6,2},{3,7},{7,3},{8,12},{12,8},{9,1... | collective-permute-start | bytes 6291464 | tf_op jit(solution)/shard_map/ppermute | solution.py:131
  76.4 5.1 %slice-start = ((f32[128,8192]{1,0:T(8,128)}), f32[128,256]{1,0:T(8,128)S(1)}, s32[]{:S(2)}) async-start(f32[128,8192]{1,0:T(8,128)} %block_ref.1), calls=%async_computation.1 | async-start | bytes 262144 | tf_op jit(solution)/shard_map/slice | solution.py:147
  77.7 14.7 %collective-permute-start.1 = (f32[128,512]{0,1:T(8,128)}, f32[128,512]{0,1:T(8,128)S(1)}, u32[]{:S(2)}, u32[]{:S(2)}) collective-permute-start(f32[128,512]{0,1:T(8,128)} %bitcast.8), channel_id=1, source_target_pairs={{0,24},{8,16},{16,8},{24,0},{1,25},{9,17},{17,9},{25,1},{2,26},{10... | collective-permute-start | bytes 786440 | tf_op jit(solution)/shard_map/ppermute | solution.py:95
  78.9 14.0 %collective-permute-start.2 = (f32[128,512]{0,1:T(8,128)S(1)}, f32[128,512]{0,1:T(8,128)S(1)}, u32[]{:S(2)}, u32[]{:S(2)}) collective-permute-start(f32[128,512]{0,1:T(8,128)S(1)} %bitcast.71), channel_id=1, source_target_pairs={{0,16},{8,24},{16,0},{24,8},{1,17},{9,25},{17,1},{25,9},{2,18},{10... | collective-permute-start | bytes 786440 | tf_op jit(solution)/shard_map/ppermute | solution.py:95
  80.5 14.3 %collective-permute-start.3 = (f32[128,512]{0,1:T(8,128)S(1)}, f32[128,512]{0,1:T(8,128)S(1)}, u32[]{:S(2)}, u32[]{:S(2)}) collective-permute-start(f32[128,512]{0,1:T(8,128)S(1)} %bitcast.70), channel_id=1, source_target_pairs={{0,8},{8,0},{16,24},{24,16},{1,9},{9,1},{17,25},{25,17},{2,10},{10... | collective-permute-start | bytes 786440 | tf_op jit(solution)/shard_map/ppermute | solution.py:95
  81.6 34.0 %collective-permute-start.13 = (f32[256]{0:T(256)S(1)}, f32[256]{0:T(256)S(1)}, u32[]{:S(2)}, u32[]{:S(2)}) collective-permute-start(f32[256]{0:T(256)S(1)} %bitcast.81), channel_id=1, source_target_pairs={{0,0},{1,8},{2,16},{3,24},{8,1},{9,9},{10,17},{11,25},{16,2},{17,1... | collective-permute-start | bytes 3080 | tf_op jit(solution)/shard_map/ppermute | solution.py:116
  83.3 17.9 %collective-permute-start.7 = (f32[128,512]{0,1:T(8,128)}, f32[128,512]{0,1:T(8,128)S(1)}, u32[]{:S(2)}, u32[]{:S(2)}) collective-permute-start(f32[128,512]{0,1:T(8,128)} %bitcast.19), channel_id=1, source_target_pairs={{0,24},{8,16},{16,8},{24,0},{1,25},{9,17},{17,9},{25,1},{2,26},{10... | collective-permute-start | bytes 786440 | tf_op jit(solution)/shard_map/ppermute | solution.py:95
  92.4 11.4 %collective-permute-start.8 = (f32[128,512]{0,1:T(8,128)}, f32[128,512]{0,1:T(8,128)S(1)}, u32[]{:S(2)}, u32[]{:S(2)}) collective-permute-start(f32[128,512]{0,1:T(8,128)} %bitcast.73), channel_id=1, source_target_pairs={{0,16},{8,24},{16,0},{24,8},{1,17},{9,25},{17,1},{25,9},{2,18},{10... | collective-permute-start | bytes 786440 | tf_op jit(solution)/shard_map/ppermute | solution.py:95
  92.9 14.9 %collective-permute-start.9 = (f32[128,512]{0,1:T(8,128)S(1)}, f32[128,512]{0,1:T(8,128)S(1)}, u32[]{:S(2)}, u32[]{:S(2)}) collective-permute-start(f32[128,512]{0,1:T(8,128)S(1)} %bitcast.72), channel_id=1, source_target_pairs={{0,8},{8,0},{16,24},{24,16},{1,9},{9,1},{17,25},{25,17},{2,10},{10... | collective-permute-start | bytes 786440 | tf_op jit(solution)/shard_map/ppermute | solution.py:95
  94.9 13.5 %collective-permute-start.4 = (f32[128,128]{1,0:T(8,128)S(1)}, f32[128,128]{1,0:T(8,128)S(1)}, u32[]{:S(2)}, u32[]{:S(2)}) collective-permute-start(f32[128,128]{1,0:T(8,128)S(1)} %bitcast.76), channel_id=1, source_target_pairs={{0,2},{1,3},{2,0},{3,1},{4,6},{5,7},{6,4},{7,5},{8,10},{9,11},{10,... | collective-permute-start | bytes 196616 | tf_op jit(solution)/shard_map/ppermute | solution.py:51
  101.2 8.3 %collective-permute-start.5 = (f32[128,128]{1,0:T(8,128)S(1)}, f32[128,128]{1,0:T(8,128)S(1)}, u32[]{:S(2)}, u32[]{:S(2)}) collective-permute-start(f32[128,128]{1,0:T(8,128)S(1)} %bitcast.75), channel_id=1, source_target_pairs={{0,1},{1,2},{2,3},{3,0},{4,5},{5,6},{6,7},{7,4},{8,9},{9,10},{10,1... | collective-permute-start | bytes 196616 | tf_op jit(solution)/shard_map/ppermute | solution.py:51
  103.8 8.5 %collective-permute-start.6 = (f32[128,128]{1,0:T(8,128)S(1)}, f32[128,128]{1,0:T(8,128)S(1)}, u32[]{:S(2)}, u32[]{:S(2)}) collective-permute-start(f32[128,128]{1,0:T(8,128)S(1)} %bitcast.74), channel_id=1, source_target_pairs={{0,3},{1,0},{2,1},{3,2},{4,7},{5,4},{6,5},{7,6},{8,11},{9,8},{10,9... | collective-permute-start | bytes 196616 | tf_op jit(solution)/shard_map/ppermute | solution.py:51
  108.0 7.0 %collective-permute-start.10 = (f32[128,128]{1,0:T(8,128)S(1)}, f32[128,128]{1,0:T(8,128)S(1)}, u32[]{:S(2)}, u32[]{:S(2)}) collective-permute-start(f32[128,128]{1,0:T(8,128)S(1)} %bitcast.77), channel_id=1, source_target_pairs={{0,2},{1,3},{2,0},{3,1},{4,6},{5,7},{6,4},{7,5},{8,10},{9,11},{10,... | collective-permute-start | bytes 196616 | tf_op jit(solution)/shard_map/ppermute | solution.py:51
  108.4 6.6 %collective-permute-start.11 = (f32[128,128]{1,0:T(8,128)S(1)}, f32[128,128]{1,0:T(8,128)S(1)}, u32[]{:S(2)}, u32[]{:S(2)}) collective-permute-start(f32[128,128]{1,0:T(8,128)S(1)} %bitcast.79), channel_id=1, source_target_pairs={{0,1},{1,2},{2,3},{3,0},{4,5},{5,6},{6,7},{7,4},{8,9},{9,10},{10,1... | collective-permute-start | bytes 196616 | tf_op jit(solution)/shard_map/ppermute | solution.py:51
  109.5 6.1 %collective-permute-start.12 = (f32[128,128]{1,0:T(8,128)S(1)}, f32[128,128]{1,0:T(8,128)S(1)}, u32[]{:S(2)}, u32[]{:S(2)}) collective-permute-start(f32[128,128]{1,0:T(8,128)S(1)} %bitcast.78), channel_id=1, source_target_pairs={{0,3},{1,0},{2,1},{3,2},{4,7},{5,4},{6,5},{7,6},{8,11},{9,8},{10,9... | collective-permute-start | bytes 196616 | tf_op jit(solution)/shard_map/ppermute | solution.py:51
